TPU v7x, 256 devices: a whole 4x4x8 slice. The times are simulated.
256 devices in a mesh: tm: 32 (over y, x, core), state: 8 (over z).
Axes of the slice: x: 4, y: 4, z: 8, core: 2. Of those that a mesh axis runs over, the one named last changes fastest.
Arguments:
- solution: float32 [32, 96, 8192], P('tm', None, 'state'), may hold values from -6 to 6
- kernel: bfloat16 [256, 32, 128, 128], P('state', 'tm'), may hold values from -0.0625 to 0.0625
- pattern: int32 [256, 2], P('state'), may hold values from 0 to 63, as said below
- offsets: int32 [2], replicated, may hold values from 8 to 23, as said below
Outputs:
- field: float32 [32, 96, 8192], P('tm', None, 'state')
Inputs may be any that keep to these rules, and one draw needn't show every extreme that they name: `pattern`: entries 32 * j to 32 * (j + 1) - 1 have row blocks among j * 8 to (j + 1) * 8 - 1; column blocks may be any, some much more common than others; a pair may repeat, and repeated blocks add. offsets[0] lies in [8, 16), and offsets[1] is 23.
All inputs are finite; a program needn't handle non-finite values.
Results may differ from a plain program's by a relative error of at most 0.0031.
Values may be sent and summed in bfloat16 or wider, within the bound.
No kernel may reach another device: no remote copies, remote signals or barrier semaphores. Data moves between devices by JAX's collectives and lax.ppermute only.
A program may use at most 64 MiB of HBM per device.

v0:
```python
import math

import jax
import jax.numpy as jnp
import numpy as np
from jax import lax
from jax.experimental import pallas as pl
from jax.experimental.pallas import tpu as pltpu
from jax.sharding import PartitionSpec as P

LEVELS = 2
HIGH = lax.Precision.HIGHEST


def slot_tables(length):
    half = length // 2
    t = np.arange(length)
    q = np.arange(half)
    angle = 2.0 * np.pi * np.outer(q, t) / length
    fwd_re = np.cos(angle)
    fwd_im = -np.sin(angle)
    fwd_re[0] = 1.0
    fwd_im[0] = np.cos(np.pi * t)
    inv_re = 2.0 * np.cos(angle.T) / length
    inv_im = -2.0 * np.sin(angle.T) / length
    inv_re[:, 0] = 1.0 / length
    inv_im[:, 0] = np.cos(np.pi * t) / length
    return tuple(jnp.asarray(a, jnp.float32) for a in (fwd_re, fwd_im, inv_re, inv_im))


def _products_body(pick_ref, src_ref, row_ref, mine_ref, other_ref, kk_ref, out_ref):
    out_ref[...] = jnp.zeros_like(out_ref)

    def step(k, carry):
        p = pick_ref[k]
        x = jnp.where(src_ref[k] == 1, other_ref[p], mine_ref[p])
        prod = lax.dot_general(
            x, kk_ref[k], (((1,), (1,)), ((), ())), preferred_element_type=jnp.float32
        )
        r = row_ref[k]
        out_ref[r] = out_ref[r] + prod
        return carry

    lax.fori_loop(0, kk_ref.shape[0], step, 0, unroll=8)


def block_products(pick, src, row, mine, other, kk, rows_local):
    nblk, m, j = mine.shape
    nnz, n, _ = kk.shape
    full = lambda *shape: pl.BlockSpec(shape, lambda i, *_: (0,) * len(shape))
    return pl.pallas_call(
        _products_body,
        grid_spec=pltpu.PrefetchScalarGridSpec(
            num_scalar_prefetch=3,
            grid=(1,),
            in_specs=[full(nblk, m, j), full(nblk, m, j), full(nnz, n, j)],
            out_specs=full(rows_local, m, n),
        ),
        out_shape=jax.ShapeDtypeStruct((rows_local, m, n), jnp.float32),
    )(pick, src, row, mine, other, kk)


def shards(solution, kernel, pattern, offsets):
    ntm = lax.axis_size("tm")
    nst = lax.axis_size("state")
    length = solution.shape[0] * ntm
    half = length // 2
    per_slot = ntm // half
    cols = solution.shape[1]
    states_local = solution.shape[2]
    nnz, _, block, _ = kernel.shape
    rows_local = states_local // block
    csl = cols // ntm
    sh = states_local // per_slot
    fwd_re, fwd_im, inv_re, inv_im = slot_tables(length)

    me = lax.axis_index("tm")
    my_state = lax.axis_index("state")
    my_slot = me // per_slot
    my_half = me % per_slot
    swap = [(i, i ^ 1) for i in range(ntm)]

    ksrc = kernel[:, 0].reshape(nnz, per_slot, ntm, block // (per_slot * ntm), block)
    ksrc = jnp.transpose(ksrc, (2, 0, 1, 3, 4))
    klags = lax.all_to_all(ksrc, "tm", 0, 0, tiled=True).astype(jnp.float32)
    kre = jnp.einsum("qt,tkhij->qhkij", fwd_re, klags, precision=HIGH).astype(jnp.bfloat16)
    kim = jnp.einsum("qt,tkhij->qhkij", fwd_im, klags, precision=HIGH).astype(jnp.bfloat16)
    kspec = jnp.stack([kre, kim], 2).reshape(ntm, 2, nnz, block // (per_slot * ntm), block)
    kspec = lax.all_to_all(kspec, "tm", 0, 0, tiled=True)
    local_rows = pattern[:, 0] - my_state * rows_local
    kk = jnp.transpose(kspec, (2, 1, 0, 3, 4)).reshape(nnz, block, block)
    row_of = jnp.clip(local_rows, 0, rows_local - 1)
    real_slot = (my_slot != 0).astype(jnp.float32)

    col_block = pattern[:, 1]
    blocks_half = rows_local // per_slot
    rel = (col_block // rows_local - my_state) % nst
    rel = jnp.where(rel < nst // 2, rel, rel - nst)
    position = jnp.where(rel > 0, 2 * rel, -2 * rel - 1)
    position = jnp.where(rel == 0, 0, position)
    cb_half = (col_block // blocks_half) % per_slot
    cb_src = (cb_half != my_half).astype(jnp.int32)
    pick = position * blocks_half + col_block % blocks_half
    fwd = [(i, (i + 1) % nst) for i in range(nst)]
    bwd = [(i, (i - 1) % nst) for i in range(nst)]

    def ring_gather(x):
        parts = [x]
        a = x
        b = x
        for step in range(1, nst // 2 + 1):
            a = lax.ppermute(a, "state", fwd)
            parts.append(a)
            if step < nst // 2:
                b = lax.ppermute(b, "state", bwd)
                parts.append(b)
        return jnp.concatenate(parts, 0)

    def respond(left):
        xre = jnp.einsum("qt,tcn->qcn", fwd_re, left, precision=HIGH).astype(jnp.bfloat16)
        xim = jnp.einsum("qt,tcn->qcn", fwd_im, left, precision=HIGH).astype(jnp.bfloat16)
        xs = jnp.stack([xre, xim], 0).reshape(2, half, csl, per_slot, sh)
        xs = jnp.transpose(xs, (1, 3, 0, 2, 4)).reshape(ntm, 2, csl, sh)
        xs = lax.all_to_all(xs, "tm", 0, 0, tiled=True)
        xs = xs.reshape(ntm, 2, csl, blocks_half, block)
        xs = jnp.transpose(xs, (3, 1, 0, 2, 4)).reshape(blocks_half, 2 * cols, block)
        mine = ring_gather(xs)
        other = lax.ppermute(mine, "tm", swap)
        prod = block_products(pick, cb_src, row_of, mine, other, kk, rows_local)
        ah = block // per_slot
        a, c_ = prod[:, :cols, :ah], prod[:, :cols, ah:]
        d, b = prod[:, cols:, :ah], prod[:, cols:, ah:]
        ys_re = a - real_slot * b
        ys_im = real_slot * (c_ + d) + (1.0 - real_slot) * b
        ys_re = jnp.transpose(ys_re, (1, 0, 2)).reshape(cols, rows_local * ah)
        ys_im = jnp.transpose(ys_im, (1, 0, 2)).reshape(cols, rows_local * ah)
        ys = jnp.stack([ys_re, ys_im], 0).reshape(2, ntm, csl, rows_local, block // per_slot)
        ys = jnp.transpose(ys, (1, 0, 2, 3, 4))
        ys = lax.all_to_all(ys, "tm", 0, 0, tiled=True)
        ys = ys.reshape(half, per_slot, 2, csl, rows_local, block // per_slot)
        ys = jnp.transpose(ys, (2, 0, 3, 4, 1, 5)).reshape(2, half, csl, states_local)
        return jnp.einsum("tq,qcn->tcn", inv_re, ys[0], precision=HIGH) + jnp.einsum(
            "tq,qcn->tcn", inv_im, ys[1], precision=HIGH
        )

    field = solution[0].reshape(ntm, csl, states_local)
    field = lax.all_to_all(field, "tm", 0, 0, tiled=True)
    times = jnp.arange(length, dtype=jnp.int32)[:, None, None]
    for level_index in range(LEVELS):
        boundary = offsets[level_index]
        left = jnp.where(times < boundary, field, 0.0)
        response = respond(left)
        field = field + jnp.where(times >= boundary, response, 0.0)
    field = lax.all_to_all(field, "tm", 0, 0, tiled=True)
    return field.reshape(1, cols, states_local)


def solution(mesh):
    return jax.shard_map(
        shards,
        mesh=mesh,
        in_specs=(P("tm", None, "state"), P("state", "tm", None, None), P("state", None), P()),
        out_specs=P("tm", None, "state"),
        check_vma=False,
    )
```

profile of v0, /device:TPU:1, one launch (start us, length us, event | category | flops | bytes accessed | tf_op | source)
XLA Modules:
  0.0 219.7 jit_solution(2108147809873613396)
XLA Ops:
  2.0 8.6 %all-to-all-start = ((f32[32,3,1024]{2,1,0:T(4,128)}), f32[32,3,1024]{2,1,0:T(4,128)S(1)}, u32[]{:S(2)}, u32[]{:S(2)}) async-start(f32[32,3,1024]{2,1,0:T(4,128)} %reshape_squeeze.6), calls=%async_computation | async-start | bytes 1048576 | tf_op jit(solution)/shard_map/all_to_all | solution.py:147
  12.4 9.6 %all-to-all-done = f32[32,3,1024]{2,1,0:T(4,128)S(1)} async-done(((f32[32,3,1024]{2,1,0:T(4,128)}), f32[32,3,1024]{2,1,0:T(4,128)S(1)}, u32[]{:S(2)}, u32[]{:S(2)}) %all-to-all-start) | async-done | bytes 393248 | tf_op jit(solution)/shard_map/all_to_all | solution.py:147
  23.8 11.9 %all_to_all.40 = bf16[32,2,3,512]{3,1,2,0:T(2,128)(2,1)S(1)} all-to-all(bf16[32,2,3,512]{3,1,2,0:T(2,128)(2,1)S(1)} %bitcast.143), channel_id=1, replica_groups=mesh['tm'=32,'state'=8] {'tm'}, dimensions={0} | all-to-all | bytes 393216 | tf_op jit(solution)/shard_map/all_to_all | solution.py:124
  38.3 3.9 %collective-permute-start.1 = (bf16[4,192,128]{2,1,0:T(8,128)(2,1)}, bf16[4,192,128]{2,1,0:T(8,128)(2,1)S(1)}, u32[]{:S(2)}, u32[]{:S(2)}) collective-permute-start(bf16[4,192,128]{2,1,0:T(8,128)(2,1)} %get-tuple-element.15), channel_id=1, source_target_pairs={{0,7},{1,0},{2,1},{3,2},{4,3},{5,4},{6,5},{7,6},{8,15},{9,8},{10,9... | collective-permute-start | bytes 589832 | tf_op jit(solution)/shard_map/ppermute | solution.py:115
  44.9 4.1 %all-to-all-start.2 = ((bf16[32,32,2,2,128]{4,3,2,1,0:T(2,128)(2,1)}), bf16[32,32,2,2,128]{4,3,2,1,0:T(2,128)(2,1)S(1)}, u32[]{:S(2)}, u32[]{:S(2)}) async-start(bf16[32,32,2,2,128]{4,3,2,1,0:T(2,128)(2,1)} %copy.70), calls=%async_computation.2 | async-start | bytes 2097152 | tf_op jit(solution)/shard_map/all_to_all | solution.py:85
  51.9 4.6 %collective-permute-done.2 = bf16[4,192,128]{2,1,0:T(8,128)(2,1)S(1)} collective-permute-done((bf16[4,192,128]{2,1,0:T(8,128)(2,1)S(1)}, bf16[4,192,128]{2,1,0:T(8,128)(2,1)S(1)}, u32[]{:S(2)}, u32[]{:S(2)}) %collective-permute-start.2) | collective-permute-done | bytes 196640 | tf_op jit(solution)/shard_map/ppermute | solution.py:112
  59.2 3.8 %collective-permute-done.4 = bf16[4,192,128]{2,1,0:T(8,128)(2,1)S(1)} collective-permute-done((bf16[4,192,128]{2,1,0:T(8,128)(2,1)S(1)}, bf16[4,192,128]{2,1,0:T(8,128)(2,1)S(1)}, u32[]{:S(2)}, u32[]{:S(2)}) %collective-permute-start.4) | collective-permute-done | bytes 196640 | tf_op jit(solution)/shard_map/ppermute | solution.py:112
  63.1 5.6 %collective-permute-done.6 = bf16[4,192,128]{2,1,0:T(8,128)(2,1)S(1)} collective-permute-done((bf16[4,192,128]{2,1,0:T(8,128)(2,1)S(1)}, bf16[4,192,128]{2,1,0:T(8,128)(2,1)S(1)}, u32[]{:S(2)}, u32[]{:S(2)}) %collective-permute-start.6) | collective-permute-done | bytes 196640 | tf_op jit(solution)/shard_map/ppermute | solution.py:112
  68.8 3.4 %collective-permute-start.7 = (bf16[32,192,128]{2,1,0:T(8,128)(2,1)S(1)}, bf16[32,192,128]{2,1,0:T(8,128)(2,1)}, u32[]{:S(2)}, u32[]{:S(2)}) collective-permute-start(bf16[32,192,128]{2,1,0:T(8,128)(2,1)S(1)} %constant_dynamic-update-slice_fusion.mine_ref), channel_id=1, source_target_pairs={{0,8},{8,0},{16,24},{24,16},{32,40},{40,32},{48,56},{56,48},{64,72... | collective-permute-start | bytes 4718600 | tf_op jit(solution)/shard_map/ppermute | solution.py:128
  76.0 7.2 %all-to-all-start.3 = ((bf16[32,2,32,2,128]{4,2,3,1,0:T(8,128)(2,1)}), bf16[32,2,32,2,128]{4,2,3,1,0:T(8,128)(2,1)S(1)}, u32[]{:S(2)}, u32[]{:S(2)}) async-start(bf16[32,2,32,2,128]{4,2,3,1,0:T(8,128)(2,1)} %pad_maximum_fusion), calls=%async_computation.3 | async-start | bytes 2097152 | tf_op jit(solution)/shard_map/all_to_all | solution.py:89
  84.9 15.3 %all-to-all-done.3 = bf16[32,2,32,2,128]{4,2,3,1,0:T(8,128)(2,1)S(1)} async-done(((bf16[32,2,32,2,128]{4,2,3,1,0:T(8,128)(2,1)}), bf16[32,2,32,2,128]{4,2,3,1,0:T(8,128)(2,1)S(1)}, u32[]{:S(2)}, u32[]{:S(2)}) %all-to-all-start.3) | async-done | bytes 1048608 | tf_op jit(solution)/shard_map/all_to_all | solution.py:89
  102.4 5.1 %shard_map.82 = f32[8,192,128]{2,1,0:T(8,128)} custom-call(s32[32]{0:T(128)} %fusion.36.pick_ref, s32[32]{0:T(128)} %compare_convert_fusion.src_ref, s32[32]{0:T(128)} %clamp_bitcast_fusion.row_ref, bf16[32,192,128]{2,1,0:T(8,128)(2,1)} %copy-done, bf16[32,192,128]{2,1,0:T(8,128)(2,1)} %collective-permute-done.7.other_ref, bf16[32,128,128]{2,1,0:T(8,128)(2,1)} %bitcast.129), custom_call_target="tpu_custom_call" | custom-call | tf_op jit(solution)/shard_map/pallas_call | solution.py:51
  111.0 3.9 %all-to-all-start.4 = ((f32[32,1,3072]{2,1,0:T(1,128)}), f32[32,1,3072]{2,1,0:T(1,128)S(1)}, u32[]{:S(2)}, u32[]{:S(2)}) async-start(f32[32,1,3072]{2,1,0:T(1,128)} %reshape.108), calls=%async_computation.4 | async-start | bytes 786432 | tf_op jit(solution)/shard_map/all_to_all | solution.py:139
  116.1 9.1 %all-to-all-done.4 = f32[32,1,3072]{2,1,0:T(1,128)S(1)} async-done(((f32[32,1,3072]{2,1,0:T(1,128)}), f32[32,1,3072]{2,1,0:T(1,128)S(1)}, u32[]{:S(2)}, u32[]{:S(2)}) %all-to-all-start.4) | async-done | bytes 393248 | tf_op jit(solution)/shard_map/all_to_all | solution.py:139
  131.5 11.7 %all_to_all.41 = bf16[32,2,3,512]{3,1,2,0:T(2,128)(2,1)S(1)} all-to-all(bf16[32,2,3,512]{3,1,2,0:T(2,128)(2,1)S(1)} %bitcast.145), channel_id=1, replica_groups=mesh['tm'=32,'state'=8] {'tm'}, dimensions={0} | all-to-all | bytes 393216 | tf_op jit(solution)/shard_map/all_to_all | solution.py:124
  146.5 4.8 %collective-permute-done.8 = bf16[4,192,128]{2,1,0:T(8,128)(2,1)S(1)} collective-permute-done((bf16[4,192,128]{2,1,0:T(8,128)(2,1)S(1)}, bf16[4,192,128]{2,1,0:T(8,128)(2,1)S(1)}, u32[]{:S(2)}, u32[]{:S(2)}) %collective-permute-start.8) | collective-permute-done | bytes 196640 | tf_op jit(solution)/shard_map/ppermute | solution.py:112
  154.1 3.9 %collective-permute-done.10 = bf16[4,192,128]{2,1,0:T(8,128)(2,1)S(1)} collective-permute-done((bf16[4,192,128]{2,1,0:T(8,128)(2,1)S(1)}, bf16[4,192,128]{2,1,0:T(8,128)(2,1)S(1)}, u32[]{:S(2)}, u32[]{:S(2)}) %collective-permute-start.10) | collective-permute-done | bytes 196640 | tf_op jit(solution)/shard_map/ppermute | solution.py:112
  160.7 3.0 %collective-permute-done.12 = bf16[4,192,128]{2,1,0:T(8,128)(2,1)S(1)} collective-permute-done((bf16[4,192,128]{2,1,0:T(8,128)(2,1)S(1)}, bf16[4,192,128]{2,1,0:T(8,128)(2,1)S(1)}, u32[]{:S(2)}, u32[]{:S(2)}) %collective-permute-start.12) | collective-permute-done | bytes 196640 | tf_op jit(solution)/shard_map/ppermute | solution.py:112
  163.8 5.7 %collective-permute-done.14 = bf16[4,192,128]{2,1,0:T(8,128)(2,1)S(1)} collective-permute-done((bf16[4,192,128]{2,1,0:T(8,128)(2,1)S(1)}, bf16[4,192,128]{2,1,0:T(8,128)(2,1)S(1)}, u32[]{:S(2)}, u32[]{:S(2)}) %collective-permute-start.14) | collective-permute-done | bytes 196640 | tf_op jit(solution)/shard_map/ppermute | solution.py:112
  169.5 4.3 %collective-permute-start.15 = (bf16[32,192,128]{2,1,0:T(8,128)(2,1)S(1)}, bf16[32,192,128]{2,1,0:T(8,128)(2,1)S(1)}, u32[]{:S(2)}, u32[]{:S(2)}) collective-permute-start(bf16[32,192,128]{2,1,0:T(8,128)(2,1)S(1)} %constant_dynamic-update-slice_fusion.8.mine_ref), channel_id=1, source_target_pairs={{0,8},{8,0},{16,24},{24,16},{32,40},{40,32},{48,56},{56,48},{64,72... | collective-permute-start | bytes 4718600 | tf_op jit(solution)/shard_map/ppermute | solution.py:128
  173.7 3.0 %collective-permute-done.15.other_ref = bf16[32,192,128]{2,1,0:T(8,128)(2,1)S(1)} collective-permute-done((bf16[32,192,128]{2,1,0:T(8,128)(2,1)S(1)}, bf16[32,192,128]{2,1,0:T(8,128)(2,1)S(1)}, u32[]{:S(2)}, u32[]{:S(2)}) %collective-permute-start.15) | collective-permute-done | bytes 1572896 | tf_op jit(solution)/shard_map/ppermute | solution.py:128
  177.9 5.1 %shard_map.83 = f32[8,192,128]{2,1,0:T(8,128)} custom-call(s32[32]{0:T(128)} %fusion.36.pick_ref, s32[32]{0:T(128)} %compare_convert_fusion.src_ref, s32[32]{0:T(128)} %clamp_bitcast_fusion.row_ref, bf16[32,192,128]{2,1,0:T(8,128)(2,1)} %copy-done.1, bf16[32,192,128]{2,1,0:T(8,128)(2,1)} %copy-done.2, bf16[32,128,128]{2,1,0:T(8,128)(2,1)} %bitcast.130), custom_call_target="tpu_custom_call" | custom-call | tf_op jit(solution)/shard_map/pallas_call | solution.py:51
  185.8 13.6 %all_to_all.42 = f32[32,1,3072]{2,1,0:T(1,128)S(1)} all-to-all(f32[32,1,3072]{2,1,0:T(1,128)S(1)} %reshape.110), channel_id=1, replica_groups=mesh['tm'=32,'state'=8] {'tm'}, dimensions={0} | all-to-all | bytes 786432 | tf_op jit(solution)/shard_map/all_to_all | solution.py:139
  203.8 14.9 %all_to_all.43 = f32[32,3,1024]{2,1,0:T(4,128)S(1)} all-to-all(f32[32,3,1024]{2,1,0:T(4,128)S(1)} %copy.91), channel_id=1, replica_groups=mesh['tm'=32,'state'=8] {'tm'}, dimensions={0} | all-to-all | bytes 786432 | tf_op jit(solution)/shard_map/all_to_all | solution.py:154
  (132 shorter events, 52.8 us)
Async XLA Ops:
  0.0 22.0 %copy-start.6 = (f32[16,32,1]{1,0,2:T(8,128)S(1)}, f32[16,32,1]{1,0,2:T(8,128)}, u32[]{:S(2)}) copy-start(f32[16,32,1]{1,0,2:T(8,128)} %constant.111) | copy-start | bytes 6148
  0.0 22.6 %copy-start.8 = (f32[16,32,1]{1,0,2:T(8,128)S(1)}, f32[16,32,1]{1,0,2:T(8,128)}, u32[]{:S(2)}) copy-start(f32[16,32,1]{1,0,2:T(8,128)} %constant.112) | copy-start | bytes 6148
  2.0 20.0 %all-to-all-start = ((f32[32,3,1024]{2,1,0:T(4,128)}), f32[32,3,1024]{2,1,0:T(4,128)S(1)}, u32[]{:S(2)}, u32[]{:S(2)}) async-start(f32[32,3,1024]{2,1,0:T(4,128)} %reshape_squeeze.6), calls=%async_computation | async-start | bytes 1048576 | tf_op jit(solution)/shard_map/all_to_all | solution.py:147
  22.7 19.5 %copy-start.3 = (bf16[32,1,128,128]{3,2,1,0:T(8,128)(2,1)S(1)}, bf16[32,1,128,128]{3,2,1,0:T(8,128)(2,1)}, u32[]{:S(2)}) copy-start(bf16[32,1,128,128]{3,2,1,0:T(8,128)(2,1)} %param.9) | copy-start | bytes 3145732
  36.6 12.4 %collective-permute-start = (bf16[4,192,128]{2,1,0:T(8,128)(2,1)}, bf16[4,192,128]{2,1,0:T(8,128)(2,1)S(1)}, u32[]{:S(2)}, u32[]{:S(2)}) collective-permute-start(bf16[4,192,128]{2,1,0:T(8,128)(2,1)} %get-tuple-element.15), channel_id=1, source_target_pairs={{0,1},{1,2},{2,3},{3,4},{4,5},{5,6},{6,7},{7,0},{8,9},{9,10},{10,1... | collective-permute-start | bytes 589832 | tf_op jit(solution)/shard_map/ppermute | solution.py:112
  38.3 10.9 %collective-permute-start.1 = (bf16[4,192,128]{2,1,0:T(8,128)(2,1)}, bf16[4,192,128]{2,1,0:T(8,128)(2,1)S(1)}, u32[]{:S(2)}, u32[]{:S(2)}) collective-permute-start(bf16[4,192,128]{2,1,0:T(8,128)(2,1)} %get-tuple-element.15), channel_id=1, source_target_pairs={{0,7},{1,0},{2,1},{3,2},{4,3},{5,4},{6,5},{7,6},{8,15},{9,8},{10,9... | collective-permute-start | bytes 589832 | tf_op jit(solution)/shard_map/ppermute | solution.py:115
  44.9 27.3 %all-to-all-start.2 = ((bf16[32,32,2,2,128]{4,3,2,1,0:T(2,128)(2,1)}), bf16[32,32,2,2,128]{4,3,2,1,0:T(2,128)(2,1)S(1)}, u32[]{:S(2)}, u32[]{:S(2)}) async-start(bf16[32,32,2,2,128]{4,3,2,1,0:T(2,128)(2,1)} %copy.70), calls=%async_computation.2 | async-start | bytes 2097152 | tf_op jit(solution)/shard_map/all_to_all | solution.py:85
  49.0 23.2 %copy-start.11 = (f32[16,32,1,1,1]{1,0,4,3,2:T(8,128)S(1)}, f32[16,32,1,1,1]{1,0,4,3,2:T(8,128)}, u32[]{:S(2)}) copy-start(f32[16,32,1,1,1]{1,0,4,3,2:T(8,128)} %constant.113) | copy-start | bytes 6148
  49.0 7.5 %collective-permute-start.2 = (bf16[4,192,128]{2,1,0:T(8,128)(2,1)S(1)}, bf16[4,192,128]{2,1,0:T(8,128)(2,1)S(1)}, u32[]{:S(2)}, u32[]{:S(2)}) collective-permute-start(bf16[4,192,128]{2,1,0:T(8,128)(2,1)S(1)} %collective-permute-done), channel_id=1, source_target_pairs={{0,1},{1,2},{2,3},{3,4},{4,5},{5,6},{6,7},{7,0},{8,9},{9,10},{10,1... | collective-permute-start | bytes 589832 | tf_op jit(solution)/shard_map/ppermute | solution.py:112
  49.1 7.4 %collective-permute-start.3 = (bf16[4,192,128]{2,1,0:T(8,128)(2,1)S(1)}, bf16[4,192,128]{2,1,0:T(8,128)(2,1)S(1)}, u32[]{:S(2)}, u32[]{:S(2)}) collective-permute-start(bf16[4,192,128]{2,1,0:T(8,128)(2,1)S(1)} %collective-permute-done.1), channel_id=1, source_target_pairs={{0,7},{1,0},{2,1},{3,2},{4,3},{5,4},{6,5},{7,6},{8,15},{9,8},{10,9... | collective-permute-start | bytes 589832 | tf_op jit(solution)/shard_map/ppermute | solution.py:115
  56.5 6.5 %collective-permute-start.4 = (bf16[4,192,128]{2,1,0:T(8,128)(2,1)S(1)}, bf16[4,192,128]{2,1,0:T(8,128)(2,1)S(1)}, u32[]{:S(2)}, u32[]{:S(2)}) collective-permute-start(bf16[4,192,128]{2,1,0:T(8,128)(2,1)S(1)} %collective-permute-done.2), channel_id=1, source_target_pairs={{0,1},{1,2},{2,3},{3,4},{4,5},{5,6},{6,7},{7,0},{8,9},{9,10},{10,1... | collective-permute-start | bytes 589832 | tf_op jit(solution)/shard_map/ppermute | solution.py:112
  56.5 6.6 %collective-permute-start.5 = (bf16[4,192,128]{2,1,0:T(8,128)(2,1)S(1)}, bf16[4,192,128]{2,1,0:T(8,128)(2,1)S(1)}, u32[]{:S(2)}, u32[]{:S(2)}) collective-permute-start(bf16[4,192,128]{2,1,0:T(8,128)(2,1)S(1)} %collective-permute-done.3), channel_id=1, source_target_pairs={{0,7},{1,0},{2,1},{3,2},{4,3},{5,4},{6,5},{7,6},{8,15},{9,8},{10,9... | collective-permute-start | bytes 589832 | tf_op jit(solution)/shard_map/ppermute | solution.py:115
  63.0 5.7 %collective-permute-start.6 = (bf16[4,192,128]{2,1,0:T(8,128)(2,1)S(1)}, bf16[4,192,128]{2,1,0:T(8,128)(2,1)S(1)}, u32[]{:S(2)}, u32[]{:S(2)}) collective-permute-start(bf16[4,192,128]{2,1,0:T(8,128)(2,1)S(1)} %collective-permute-done.4), channel_id=1, source_target_pairs={{0,1},{1,2},{2,3},{3,4},{4,5},{5,6},{6,7},{7,0},{8,9},{9,10},{10,1... | collective-permute-start | bytes 589832 | tf_op jit(solution)/shard_map/ppermute | solution.py:112
  68.8 33.6 %collective-permute-start.7 = (bf16[32,192,128]{2,1,0:T(8,128)(2,1)S(1)}, bf16[32,192,128]{2,1,0:T(8,128)(2,1)}, u32[]{:S(2)}, u32[]{:S(2)}) collective-permute-start(bf16[32,192,128]{2,1,0:T(8,128)(2,1)S(1)} %constant_dynamic-update-slice_fusion.mine_ref), channel_id=1, source_target_pairs={{0,8},{8,0},{16,24},{24,16},{32,40},{40,32},{48,56},{56,48},{64,72... | collective-permute-start | bytes 4718600 | tf_op jit(solution)/shard_map/ppermute | solution.py:128
  76.0 24.2 %all-to-all-start.3 = ((bf16[32,2,32,2,128]{4,2,3,1,0:T(8,128)(2,1)}), bf16[32,2,32,2,128]{4,2,3,1,0:T(8,128)(2,1)S(1)}, u32[]{:S(2)}, u32[]{:S(2)}) async-start(bf16[32,2,32,2,128]{4,2,3,1,0:T(8,128)(2,1)} %pad_maximum_fusion), calls=%async_computation.3 | async-start | bytes 2097152 | tf_op jit(solution)/shard_map/all_to_all | solution.py:89
  111.0 14.2 %all-to-all-start.4 = ((f32[32,1,3072]{2,1,0:T(1,128)}), f32[32,1,3072]{2,1,0:T(1,128)S(1)}, u32[]{:S(2)}, u32[]{:S(2)}) async-start(f32[32,1,3072]{2,1,0:T(1,128)} %reshape.108), calls=%async_computation.4 | async-start | bytes 786432 | tf_op jit(solution)/shard_map/all_to_all | solution.py:139
  143.5 7.8 %collective-permute-start.8 = (bf16[4,192,128]{2,1,0:T(8,128)(2,1)S(1)}, bf16[4,192,128]{2,1,0:T(8,128)(2,1)S(1)}, u32[]{:S(2)}, u32[]{:S(2)}) collective-permute-start(bf16[4,192,128]{2,1,0:T(8,128)(2,1)S(1)} %get-tuple-element.13), channel_id=1, source_target_pairs={{0,1},{1,2},{2,3},{3,4},{4,5},{5,6},{6,7},{7,0},{8,9},{9,10},{10,1... | collective-permute-start | bytes 589832 | tf_op jit(solution)/shard_map/ppermute | solution.py:112
  143.8 7.5 %collective-permute-start.9 = (bf16[4,192,128]{2,1,0:T(8,128)(2,1)S(1)}, bf16[4,192,128]{2,1,0:T(8,128)(2,1)S(1)}, u32[]{:S(2)}, u32[]{:S(2)}) collective-permute-start(bf16[4,192,128]{2,1,0:T(8,128)(2,1)S(1)} %get-tuple-element.13), channel_id=1, source_target_pairs={{0,7},{1,0},{2,1},{3,2},{4,3},{5,4},{6,5},{7,6},{8,15},{9,8},{10,9... | collective-permute-start | bytes 589832 | tf_op jit(solution)/shard_map/ppermute | solution.py:115
  151.3 6.7 %collective-permute-start.10 = (bf16[4,192,128]{2,1,0:T(8,128)(2,1)S(1)}, bf16[4,192,128]{2,1,0:T(8,128)(2,1)S(1)}, u32[]{:S(2)}, u32[]{:S(2)}) collective-permute-start(bf16[4,192,128]{2,1,0:T(8,128)(2,1)S(1)} %collective-permute-done.8), channel_id=1, source_target_pairs={{0,1},{1,2},{2,3},{3,4},{4,5},{5,6},{6,7},{7,0},{8,9},{9,10},{10,1... | collective-permute-start | bytes 589832 | tf_op jit(solution)/shard_map/ppermute | solution.py:112
  151.3 6.7 %collective-permute-start.11 = (bf16[4,192,128]{2,1,0:T(8,128)(2,1)S(1)}, bf16[4,192,128]{2,1,0:T(8,128)(2,1)S(1)}, u32[]{:S(2)}, u32[]{:S(2)}) collective-permute-start(bf16[4,192,128]{2,1,0:T(8,128)(2,1)S(1)} %collective-permute-done.9), channel_id=1, source_target_pairs={{0,7},{1,0},{2,1},{3,2},{4,3},{5,4},{6,5},{7,6},{8,15},{9,8},{10,9... | collective-permute-start | bytes 589832 | tf_op jit(solution)/shard_map/ppermute | solution.py:115
  158.0 5.7 %collective-permute-start.12 = (bf16[4,192,128]{2,1,0:T(8,128)(2,1)S(1)}, bf16[4,192,128]{2,1,0:T(8,128)(2,1)S(1)}, u32[]{:S(2)}, u32[]{:S(2)}) collective-permute-start(bf16[4,192,128]{2,1,0:T(8,128)(2,1)S(1)} %collective-permute-done.10), channel_id=1, source_target_pairs={{0,1},{1,2},{2,3},{3,4},{4,5},{5,6},{6,7},{7,0},{8,9},{9,10},{10,1... | collective-permute-start | bytes 589832 | tf_op jit(solution)/shard_map/ppermute | solution.py:112
  158.0 5.8 %collective-permute-start.13 = (bf16[4,192,128]{2,1,0:T(8,128)(2,1)S(1)}, bf16[4,192,128]{2,1,0:T(8,128)(2,1)S(1)}, u32[]{:S(2)}, u32[]{:S(2)}) collective-permute-start(bf16[4,192,128]{2,1,0:T(8,128)(2,1)S(1)} %collective-permute-done.11), channel_id=1, source_target_pairs={{0,7},{1,0},{2,1},{3,2},{4,3},{5,4},{6,5},{7,6},{8,15},{9,8},{10,9... | collective-permute-start | bytes 589832 | tf_op jit(solution)/shard_map/ppermute | solution.py:115
  163.7 5.7 %collective-permute-start.14 = (bf16[4,192,128]{2,1,0:T(8,128)(2,1)S(1)}, bf16[4,192,128]{2,1,0:T(8,128)(2,1)S(1)}, u32[]{:S(2)}, u32[]{:S(2)}) collective-permute-start(bf16[4,192,128]{2,1,0:T(8,128)(2,1)S(1)} %collective-permute-done.12), channel_id=1, source_target_pairs={{0,1},{1,2},{2,3},{3,4},{4,5},{5,6},{6,7},{7,0},{8,9},{9,10},{10,1... | collective-permute-start | bytes 589832 | tf_op jit(solution)/shard_map/ppermute | solution.py:112
  169.5 7.3 %collective-permute-start.15 = (bf16[32,192,128]{2,1,0:T(8,128)(2,1)S(1)}, bf16[32,192,128]{2,1,0:T(8,128)(2,1)S(1)}, u32[]{:S(2)}, u32[]{:S(2)}) collective-permute-start(bf16[32,192,128]{2,1,0:T(8,128)(2,1)S(1)} %constant_dynamic-update-slice_fusion.8.mine_ref), channel_id=1, source_target_pairs={{0,8},{8,0},{16,24},{24,16},{32,40},{40,32},{48,56},{56,48},{64,72... | collective-permute-start | bytes 4718600 | tf_op jit(solution)/shard_map/ppermute | solution.py:128
  (12 other events, 51.7 us)
where the time goes:
time: 220 us
  waiting for transfers between devices  68.5 us (31%)
  blocking collectives  52.2 us (24%)
  starting transfers between devices  50.8 us (23%)
  local copies, waits for them, and re-layouts  18.9 us (9%)
  other arithmetic  12.3 us (6%)
  Pallas kernels  10.1 us (5%)
  matrix products  6.22 us (3%)
    ppermute x8, waiting for transfers between devices, ring_gather(): a = lax.ppermute(a, 'state', fwd)  31.4 us
    all_to_all x2, blocking collectives, respond(): xs = lax.all_to_all(xs, 'tm', 0, 0, tiled=True)  23.6 us
    ppermute x6, starting transfers between devices, ring_gather(): b = lax.ppermute(b, 'state', bwd)  17.3 us
    all_to_all x1, waiting for transfers between devices, shards(): kspec = lax.all_to_all(kspec, 'tm', 0, 0, tiled=True)  15.3 us
    all_to_all x1, blocking collectives, shards(): field = lax.all_to_all(field, 'tm', 0, 0, tiled=True)  14.9 us
    all_to_all x1, blocking collectives, respond(): ys = lax.all_to_all(ys, 'tm', 0, 0, tiled=True)  13.6 us
    pallas_call x2, Pallas kernels, block_products(): pl.pallas_call(_products_body, grid_spec=pltpu.PrefetchScalarGridSpec(num...  10.1 us
    all_to_all x1, waiting for transfers between devices, shards(): field = lax.all_to_all(field, 'tm', 0, 0, tiled=True)  9.59 us
  transfers between devices with their start and end apart: 20, of which 11 were waited for; matrix products, arithmetic and copies ran while one was open for 6% of the time, Pallas kernels for 0%

commit v1 on v0

--- a/solution.py
+++ b/solution.py
@@ -25,7 +25,9 @@
     inv_im = -2.0 * np.sin(angle.T) / length
     inv_re[:, 0] = 1.0 / length
     inv_im[:, 0] = np.cos(np.pi * t) / length
-    return tuple(jnp.asarray(a, jnp.float32) for a in (fwd_re, fwd_im, inv_re, inv_im))
+    fwd = np.concatenate([fwd_re, fwd_im], 0)
+    inv = np.concatenate([inv_re, inv_im], 1)
+    return jnp.asarray(fwd, jnp.float32), jnp.asarray(inv, jnp.float32)
 
 
 def _products_body(pick_ref, src_ref, row_ref, mine_ref, other_ref, kk_ref, out_ref):
@@ -72,7 +74,7 @@
     rows_local = states_local // block
     csl = cols // ntm
     sh = states_local // per_slot
-    fwd_re, fwd_im, inv_re, inv_im = slot_tables(length)
+    fwd_table, inv_table = slot_tables(length)
 
     me = lax.axis_index("tm")
     my_state = lax.axis_index("state")
@@ -83,9 +85,10 @@
     ksrc = kernel[:, 0].reshape(nnz, per_slot, ntm, block // (per_slot * ntm), block)
     ksrc = jnp.transpose(ksrc, (2, 0, 1, 3, 4))
     klags = lax.all_to_all(ksrc, "tm", 0, 0, tiled=True).astype(jnp.float32)
-    kre = jnp.einsum("qt,tkhij->qhkij", fwd_re, klags, precision=HIGH).astype(jnp.bfloat16)
-    kim = jnp.einsum("qt,tkhij->qhkij", fwd_im, klags, precision=HIGH).astype(jnp.bfloat16)
-    kspec = jnp.stack([kre, kim], 2).reshape(ntm, 2, nnz, block // (per_slot * ntm), block)
+    kspec = jnp.einsum(
+        "xqt,tkhij->qhxkij", fwd_table.reshape(2, half, length), klags, precision=HIGH
+    ).astype(jnp.bfloat16)
+    kspec = kspec.reshape(ntm, 2, nnz, block // (per_slot * ntm), block)
     kspec = lax.all_to_all(kspec, "tm", 0, 0, tiled=True)
     local_rows = pattern[:, 0] - my_state * rows_local
     kk = jnp.transpose(kspec, (2, 1, 0, 3, 4)).reshape(nnz, block, block)
@@ -117,9 +120,8 @@
         return jnp.concatenate(parts, 0)
 
     def respond(left):
-        xre = jnp.einsum("qt,tcn->qcn", fwd_re, left, precision=HIGH).astype(jnp.bfloat16)
-        xim = jnp.einsum("qt,tcn->qcn", fwd_im, left, precision=HIGH).astype(jnp.bfloat16)
-        xs = jnp.stack([xre, xim], 0).reshape(2, half, csl, per_slot, sh)
+        xs = jnp.einsum("qt,tcn->qcn", fwd_table, left, precision=HIGH).astype(jnp.bfloat16)
+        xs = xs.reshape(2, half, csl, per_slot, sh)
         xs = jnp.transpose(xs, (1, 3, 0, 2, 4)).reshape(ntm, 2, csl, sh)
         xs = lax.all_to_all(xs, "tm", 0, 0, tiled=True)
         xs = xs.reshape(ntm, 2, csl, blocks_half, block)
@@ -139,9 +141,7 @@
         ys = lax.all_to_all(ys, "tm", 0, 0, tiled=True)
         ys = ys.reshape(half, per_slot, 2, csl, rows_local, block // per_slot)
         ys = jnp.transpose(ys, (2, 0, 3, 4, 1, 5)).reshape(2, half, csl, states_local)
-        return jnp.einsum("tq,qcn->tcn", inv_re, ys[0], precision=HIGH) + jnp.einsum(
-            "tq,qcn->tcn", inv_im, ys[1], precision=HIGH
-        )
+        return jnp.einsum("tq,qcn->tcn", inv_table, ys.reshape(length, csl, states_local), precision=HIGH)
 
     field = solution[0].reshape(ntm, csl, states_local)
     field = lax.all_to_all(field, "tm", 0, 0, tiled=True)

time: 220 us -> 217 us (0.986)
  matrix products: 6.22 us -> 3.63 us
    dot_general x10 -> x5, matrix products: 6.22 us -> 3.63 us  [the longest x2 1.27 us: respond(): jnp.einsum('qt,tcn->qcn', fwd_table, left, precision=HIGH)]
where the time goes in v1:
time: 217 us; the launch traced here: 216 us
  waiting for transfers between devices  68.5 us (32%)
  blocking collectives  52.2 us (24%)
  starting transfers between devices  50.6 us (23%)
  local copies, waits for them, and re-layouts  19.7 us (9%)
  other arithmetic  10.7 us (5%)
  Pallas kernels  10.1 us (5%)
  matrix products  3.63 us (2%)
    ppermute x8, waiting for transfers between devices, ring_gather(): a = lax.ppermute(a, 'state', fwd)  31.4 us
    all_to_all x2, blocking collectives, respond(): xs = lax.all_to_all(xs, 'tm', 0, 0, tiled=True)  23.6 us
    ppermute x6, starting transfers between devices, ring_gather(): b = lax.ppermute(b, 'state', bwd)  17.3 us
    all_to_all x1, waiting for transfers between devices, shards(): kspec = lax.all_to_all(kspec, 'tm', 0, 0, tiled=True)  15.3 us
    all_to_all x1, blocking collectives, shards(): field = lax.all_to_all(field, 'tm', 0, 0, tiled=True)  14.9 us
    all_to_all x1, blocking collectives, respond(): ys = lax.all_to_all(ys, 'tm', 0, 0, tiled=True)  13.6 us
    pallas_call x2, Pallas kernels, block_products(): pl.pallas_call(_products_body, grid_spec=pltpu.PrefetchScalarGridSpec(num...  10.1 us
    all_to_all x1, waiting for transfers between devices, shards(): field = lax.all_to_all(field, 'tm', 0, 0, tiled=True)  9.61 us
  transfers between devices with their start and end apart: 20, of which 11 were waited for; matrix products, arithmetic and copies ran while one was open for 6% of the time, Pallas kernels for 0%

profile of v1, /device:TPU:1, one launch (start us, length us, event | category | flops | bytes accessed | tf_op | source)
XLA Modules:
  0.0 215.9 jit_solution(8415319377314829335)
XLA Ops:
  2.0 8.6 %all-to-all-start = ((f32[32,3,1024]{2,1,0:T(4,128)}), f32[32,3,1024]{2,1,0:T(4,128)S(1)}, u32[]{:S(2)}, u32[]{:S(2)}) async-start(f32[32,3,1024]{2,1,0:T(4,128)} %reshape_squeeze.6), calls=%async_computation | async-start | bytes 1048576 | tf_op jit(solution)/shard_map/all_to_all | solution.py:147
  12.4 9.6 %all-to-all-done = f32[32,3,1024]{2,1,0:T(4,128)S(1)} async-done(((f32[32,3,1024]{2,1,0:T(4,128)}), f32[32,3,1024]{2,1,0:T(4,128)S(1)}, u32[]{:S(2)}, u32[]{:S(2)}) %all-to-all-start) | async-done | bytes 393248 | tf_op jit(solution)/shard_map/all_to_all | solution.py:147
  23.1 11.9 %all_to_all.40 = bf16[32,2,3,512]{3,1,2,0:T(2,128)(2,1)S(1)} all-to-all(bf16[32,2,3,512]{3,1,2,0:T(2,128)(2,1)S(1)} %bitcast.116), channel_id=1, replica_groups=mesh['tm'=32,'state'=8] {'tm'}, dimensions={0} | all-to-all | bytes 393216 | tf_op jit(solution)/shard_map/all_to_all | solution.py:126
  37.5 3.9 %collective-permute-start.1 = (bf16[4,192,128]{2,1,0:T(8,128)(2,1)}, bf16[4,192,128]{2,1,0:T(8,128)(2,1)S(1)}, u32[]{:S(2)}, u32[]{:S(2)}) collective-permute-start(bf16[4,192,128]{2,1,0:T(8,128)(2,1)} %get-tuple-element.11), channel_id=1, source_target_pairs={{0,7},{1,0},{2,1},{3,2},{4,3},{5,4},{6,5},{7,6},{8,15},{9,8},{10,9... | collective-permute-start | bytes 589832 | tf_op jit(solution)/shard_map/ppermute | solution.py:118
  44.2 4.1 %all-to-all-start.2 = ((bf16[32,32,2,2,128]{4,3,2,1,0:T(2,128)(2,1)}), bf16[32,32,2,2,128]{4,3,2,1,0:T(2,128)(2,1)S(1)}, u32[]{:S(2)}, u32[]{:S(2)}) async-start(bf16[32,32,2,2,128]{4,3,2,1,0:T(2,128)(2,1)} %copy.67), calls=%async_computation.2 | async-start | bytes 2097152 | tf_op jit(solution)/shard_map/all_to_all | solution.py:87
  51.1 4.6 %collective-permute-done.2 = bf16[4,192,128]{2,1,0:T(8,128)(2,1)S(1)} collective-permute-done((bf16[4,192,128]{2,1,0:T(8,128)(2,1)S(1)}, bf16[4,192,128]{2,1,0:T(8,128)(2,1)S(1)}, u32[]{:S(2)}, u32[]{:S(2)}) %collective-permute-start.2) | collective-permute-done | bytes 196640 | tf_op jit(solution)/shard_map/ppermute | solution.py:115
  58.5 3.8 %collective-permute-done.4 = bf16[4,192,128]{2,1,0:T(8,128)(2,1)S(1)} collective-permute-done((bf16[4,192,128]{2,1,0:T(8,128)(2,1)S(1)}, bf16[4,192,128]{2,1,0:T(8,128)(2,1)S(1)}, u32[]{:S(2)}, u32[]{:S(2)}) %collective-permute-start.4) | collective-permute-done | bytes 196640 | tf_op jit(solution)/shard_map/ppermute | solution.py:115
  62.4 5.7 %collective-permute-done.6 = bf16[4,192,128]{2,1,0:T(8,128)(2,1)S(1)} collective-permute-done((bf16[4,192,128]{2,1,0:T(8,128)(2,1)S(1)}, bf16[4,192,128]{2,1,0:T(8,128)(2,1)S(1)}, u32[]{:S(2)}, u32[]{:S(2)}) %collective-permute-start.6) | collective-permute-done | bytes 196640 | tf_op jit(solution)/shard_map/ppermute | solution.py:115
  68.1 3.4 %collective-permute-start.7 = (bf16[32,192,128]{2,1,0:T(8,128)(2,1)S(1)}, bf16[32,192,128]{2,1,0:T(8,128)(2,1)}, u32[]{:S(2)}, u32[]{:S(2)}) collective-permute-start(bf16[32,192,128]{2,1,0:T(8,128)(2,1)S(1)} %constant_dynamic-update-slice_fusion.mine_ref), channel_id=1, source_target_pairs={{0,8},{8,0},{16,24},{24,16},{32,40},{40,32},{48,56},{56,48},{64,72... | collective-permute-start | bytes 4718600 | tf_op jit(solution)/shard_map/ppermute | solution.py:130
  74.4 7.2 %all-to-all-start.3 = ((bf16[32,2,32,2,128]{4,2,3,1,0:T(8,128)(2,1)}), bf16[32,2,32,2,128]{4,2,3,1,0:T(8,128)(2,1)S(1)}, u32[]{:S(2)}, u32[]{:S(2)}) async-start(bf16[32,2,32,2,128]{4,2,3,1,0:T(8,128)(2,1)} %bitcast.16), calls=%async_computation.3 | async-start | bytes 2097152 | tf_op jit(solution)/shard_map/all_to_all | solution.py:92
  83.4 15.3 %all-to-all-done.3 = bf16[32,2,32,2,128]{4,2,3,1,0:T(8,128)(2,1)S(1)} async-done(((bf16[32,2,32,2,128]{4,2,3,1,0:T(8,128)(2,1)}), bf16[32,2,32,2,128]{4,2,3,1,0:T(8,128)(2,1)S(1)}, u32[]{:S(2)}, u32[]{:S(2)}) %all-to-all-start.3) | async-done | bytes 1048608 | tf_op jit(solution)/shard_map/all_to_all | solution.py:92
  100.8 5.1 %shard_map.64 = f32[8,192,128]{2,1,0:T(8,128)} custom-call(s32[32]{0:T(128)} %fusion.24.pick_ref, s32[32]{0:T(128)} %compare_convert_fusion.src_ref, s32[32]{0:T(128)} %clamp_bitcast_fusion.row_ref, bf16[32,192,128]{2,1,0:T(8,128)(2,1)} %copy-done, bf16[32,192,128]{2,1,0:T(8,128)(2,1)} %collective-permute-done.7.other_ref, bf16[32,128,128]{2,1,0:T(8,128)(2,1)} %bitcast.103), custom_call_target="tpu_custom_call" | custom-call | tf_op jit(solution)/shard_map/pallas_call | solution.py:53
  109.5 3.9 %all-to-all-start.4 = ((f32[32,1,3072]{2,1,0:T(1,128)}), f32[32,1,3072]{2,1,0:T(1,128)S(1)}, u32[]{:S(2)}, u32[]{:S(2)}) async-start(f32[32,1,3072]{2,1,0:T(1,128)} %reshape.97), calls=%async_computation.4 | async-start | bytes 786432 | tf_op jit(solution)/shard_map/all_to_all | solution.py:141
  114.5 9.1 %all-to-all-done.4 = f32[32,1,3072]{2,1,0:T(1,128)S(1)} async-done(((f32[32,1,3072]{2,1,0:T(1,128)}), f32[32,1,3072]{2,1,0:T(1,128)S(1)}, u32[]{:S(2)}, u32[]{:S(2)}) %all-to-all-start.4) | async-done | bytes 393248 | tf_op jit(solution)/shard_map/all_to_all | solution.py:141
  128.6 11.7 %all_to_all.41 = bf16[32,2,3,512]{3,1,2,0:T(2,128)(2,1)S(1)} all-to-all(bf16[32,2,3,512]{3,1,2,0:T(2,128)(2,1)S(1)} %bitcast.119), channel_id=1, replica_groups=mesh['tm'=32,'state'=8] {'tm'}, dimensions={0} | all-to-all | bytes 393216 | tf_op jit(solution)/shard_map/all_to_all | solution.py:126
  143.4 4.8 %collective-permute-done.8 = bf16[4,192,128]{2,1,0:T(8,128)(2,1)S(1)} collective-permute-done((bf16[4,192,128]{2,1,0:T(8,128)(2,1)S(1)}, bf16[4,192,128]{2,1,0:T(8,128)(2,1)S(1)}, u32[]{:S(2)}, u32[]{:S(2)}) %collective-permute-start.8) | collective-permute-done | bytes 196640 | tf_op jit(solution)/shard_map/ppermute | solution.py:115
  151.0 3.9 %collective-permute-done.10 = bf16[4,192,128]{2,1,0:T(8,128)(2,1)S(1)} collective-permute-done((bf16[4,192,128]{2,1,0:T(8,128)(2,1)S(1)}, bf16[4,192,128]{2,1,0:T(8,128)(2,1)S(1)}, u32[]{:S(2)}, u32[]{:S(2)}) %collective-permute-start.10) | collective-permute-done | bytes 196640 | tf_op jit(solution)/shard_map/ppermute | solution.py:115
  157.6 3.0 %collective-permute-done.12 = bf16[4,192,128]{2,1,0:T(8,128)(2,1)S(1)} collective-permute-done((bf16[4,192,128]{2,1,0:T(8,128)(2,1)S(1)}, bf16[4,192,128]{2,1,0:T(8,128)(2,1)S(1)}, u32[]{:S(2)}, u32[]{:S(2)}) %collective-permute-start.12) | collective-permute-done | bytes 196640 | tf_op jit(solution)/shard_map/ppermute | solution.py:115
  160.7 5.7 %collective-permute-done.14 = bf16[4,192,128]{2,1,0:T(8,128)(2,1)S(1)} collective-permute-done((bf16[4,192,128]{2,1,0:T(8,128)(2,1)S(1)}, bf16[4,192,128]{2,1,0:T(8,128)(2,1)S(1)}, u32[]{:S(2)}, u32[]{:S(2)}) %collective-permute-start.14) | collective-permute-done | bytes 196640 | tf_op jit(solution)/shard_map/ppermute | solution.py:115
  166.4 4.3 %collective-permute-start.15 = (bf16[32,192,128]{2,1,0:T(8,128)(2,1)S(1)}, bf16[32,192,128]{2,1,0:T(8,128)(2,1)S(1)}, u32[]{:S(2)}, u32[]{:S(2)}) collective-permute-start(bf16[32,192,128]{2,1,0:T(8,128)(2,1)S(1)} %constant_dynamic-update-slice_fusion.8.mine_ref), channel_id=1, source_target_pairs={{0,8},{8,0},{16,24},{24,16},{32,40},{40,32},{48,56},{56,48},{64,72... | collective-permute-start | bytes 4718600 | tf_op jit(solution)/shard_map/ppermute | solution.py:130
  170.7 3.0 %collective-permute-done.15.other_ref = bf16[32,192,128]{2,1,0:T(8,128)(2,1)S(1)} collective-permute-done((bf16[32,192,128]{2,1,0:T(8,128)(2,1)S(1)}, bf16[32,192,128]{2,1,0:T(8,128)(2,1)S(1)}, u32[]{:S(2)}, u32[]{:S(2)}) %collective-permute-start.15) | collective-permute-done | bytes 1572896 | tf_op jit(solution)/shard_map/ppermute | solution.py:130
  174.9 5.1 %shard_map.65 = f32[8,192,128]{2,1,0:T(8,128)} custom-call(s32[32]{0:T(128)} %fusion.24.pick_ref, s32[32]{0:T(128)} %compare_convert_fusion.src_ref, s32[32]{0:T(128)} %clamp_bitcast_fusion.row_ref, bf16[32,192,128]{2,1,0:T(8,128)(2,1)} %copy-done.1, bf16[32,192,128]{2,1,0:T(8,128)(2,1)} %copy-done.2, bf16[32,128,128]{2,1,0:T(8,128)(2,1)} %bitcast.104), custom_call_target="tpu_custom_call" | custom-call | tf_op jit(solution)/shard_map/pallas_call | solution.py:53
  182.8 13.6 %all_to_all.42 = f32[32,1,3072]{2,1,0:T(1,128)S(1)} all-to-all(f32[32,1,3072]{2,1,0:T(1,128)S(1)} %reshape.99), channel_id=1, replica_groups=mesh['tm'=32,'state'=8] {'tm'}, dimensions={0} | all-to-all | bytes 786432 | tf_op jit(solution)/shard_map/all_to_all | solution.py:141
  200.1 14.9 %all_to_all.43 = f32[32,3,1024]{2,1,0:T(4,128)S(1)} all-to-all(f32[32,3,1024]{2,1,0:T(4,128)S(1)} %copy.86), channel_id=1, replica_groups=mesh['tm'=32,'state'=8] {'tm'}, dimensions={0} | all-to-all | bytes 786432 | tf_op jit(solution)/shard_map/all_to_all | solution.py:154
  (109 shorter events, 49.2 us)
Async XLA Ops:
  0.0 22.0 %copy-start.5 = (f32[32,32,1]{1,0,2:T(8,128)S(1)}, f32[32,32,1]{1,0,2:T(8,128)}, u32[]{:S(2)}) copy-start(f32[32,32,1]{1,0,2:T(8,128)} %constant.106) | copy-start | bytes 12292
  0.0 10.6 %copy-start.8 = (s32[2]{0:T(128)S(1)}, s32[2]{0:T(128)}, u32[]{:S(2)}) copy-start(s32[2]{0:T(128)} %param.9) | copy-start | bytes 28
  2.0 20.0 %all-to-all-start = ((f32[32,3,1024]{2,1,0:T(4,128)}), f32[32,3,1024]{2,1,0:T(4,128)S(1)}, u32[]{:S(2)}, u32[]{:S(2)}) async-start(f32[32,3,1024]{2,1,0:T(4,128)} %reshape_squeeze.6), calls=%async_computation | async-start | bytes 1048576 | tf_op jit(solution)/shard_map/all_to_all | solution.py:147
  22.0 19.5 %copy-start.3 = (bf16[32,1,128,128]{3,2,1,0:T(8,128)(2,1)S(1)}, bf16[32,1,128,128]{3,2,1,0:T(8,128)(2,1)}, u32[]{:S(2)}) copy-start(bf16[32,1,128,128]{3,2,1,0:T(8,128)(2,1)} %param.7) | copy-start | bytes 3145732
  35.9 12.4 %collective-permute-start = (bf16[4,192,128]{2,1,0:T(8,128)(2,1)}, bf16[4,192,128]{2,1,0:T(8,128)(2,1)S(1)}, u32[]{:S(2)}, u32[]{:S(2)}) collective-permute-start(bf16[4,192,128]{2,1,0:T(8,128)(2,1)} %get-tuple-element.11), channel_id=1, source_target_pairs={{0,1},{1,2},{2,3},{3,4},{4,5},{5,6},{6,7},{7,0},{8,9},{9,10},{10,1... | collective-permute-start | bytes 589832 | tf_op jit(solution)/shard_map/ppermute | solution.py:115
  37.5 10.9 %collective-permute-start.1 = (bf16[4,192,128]{2,1,0:T(8,128)(2,1)}, bf16[4,192,128]{2,1,0:T(8,128)(2,1)S(1)}, u32[]{:S(2)}, u32[]{:S(2)}) collective-permute-start(bf16[4,192,128]{2,1,0:T(8,128)(2,1)} %get-tuple-element.11), channel_id=1, source_target_pairs={{0,7},{1,0},{2,1},{3,2},{4,3},{5,4},{6,5},{7,6},{8,15},{9,8},{10,9... | collective-permute-start | bytes 589832 | tf_op jit(solution)/shard_map/ppermute | solution.py:118
  44.2 27.3 %all-to-all-start.2 = ((bf16[32,32,2,2,128]{4,3,2,1,0:T(2,128)(2,1)}), bf16[32,32,2,2,128]{4,3,2,1,0:T(2,128)(2,1)S(1)}, u32[]{:S(2)}, u32[]{:S(2)}) async-start(bf16[32,32,2,2,128]{4,3,2,1,0:T(2,128)(2,1)} %copy.67), calls=%async_computation.2 | async-start | bytes 2097152 | tf_op jit(solution)/shard_map/all_to_all | solution.py:87
  48.3 23.2 %copy-start.7 = (f32[2,16,32,1,1,1]{2,1,5,4,3,0:T(8,128)S(1)}, f32[2,16,32,1,1,1]{2,1,5,4,3,0:T(8,128)}, u32[]{:S(2)}) copy-start(f32[2,16,32,1,1,1]{2,1,5,4,3,0:T(8,128)} %constant.107) | copy-start | bytes 12292
  48.3 7.5 %collective-permute-start.2 = (bf16[4,192,128]{2,1,0:T(8,128)(2,1)S(1)}, bf16[4,192,128]{2,1,0:T(8,128)(2,1)S(1)}, u32[]{:S(2)}, u32[]{:S(2)}) collective-permute-start(bf16[4,192,128]{2,1,0:T(8,128)(2,1)S(1)} %collective-permute-done), channel_id=1, source_target_pairs={{0,1},{1,2},{2,3},{3,4},{4,5},{5,6},{6,7},{7,0},{8,9},{9,10},{10,1... | collective-permute-start | bytes 589832 | tf_op jit(solution)/shard_map/ppermute | solution.py:115
  48.4 7.4 %collective-permute-start.3 = (bf16[4,192,128]{2,1,0:T(8,128)(2,1)S(1)}, bf16[4,192,128]{2,1,0:T(8,128)(2,1)S(1)}, u32[]{:S(2)}, u32[]{:S(2)}) collective-permute-start(bf16[4,192,128]{2,1,0:T(8,128)(2,1)S(1)} %collective-permute-done.1), channel_id=1, source_target_pairs={{0,7},{1,0},{2,1},{3,2},{4,3},{5,4},{6,5},{7,6},{8,15},{9,8},{10,9... | collective-permute-start | bytes 589832 | tf_op jit(solution)/shard_map/ppermute | solution.py:118
  55.8 6.5 %collective-permute-start.4 = (bf16[4,192,128]{2,1,0:T(8,128)(2,1)S(1)}, bf16[4,192,128]{2,1,0:T(8,128)(2,1)S(1)}, u32[]{:S(2)}, u32[]{:S(2)}) collective-permute-start(bf16[4,192,128]{2,1,0:T(8,128)(2,1)S(1)} %collective-permute-done.2), channel_id=1, source_target_pairs={{0,1},{1,2},{2,3},{3,4},{4,5},{5,6},{6,7},{7,0},{8,9},{9,10},{10,1... | collective-permute-start | bytes 589832 | tf_op jit(solution)/shard_map/ppermute | solution.py:115
  55.8 6.6 %collective-permute-start.5 = (bf16[4,192,128]{2,1,0:T(8,128)(2,1)S(1)}, bf16[4,192,128]{2,1,0:T(8,128)(2,1)S(1)}, u32[]{:S(2)}, u32[]{:S(2)}) collective-permute-start(bf16[4,192,128]{2,1,0:T(8,128)(2,1)S(1)} %collective-permute-done.3), channel_id=1, source_target_pairs={{0,7},{1,0},{2,1},{3,2},{4,3},{5,4},{6,5},{7,6},{8,15},{9,8},{10,9... | collective-permute-start | bytes 589832 | tf_op jit(solution)/shard_map/ppermute | solution.py:118
  62.3 5.7 %collective-permute-start.6 = (bf16[4,192,128]{2,1,0:T(8,128)(2,1)S(1)}, bf16[4,192,128]{2,1,0:T(8,128)(2,1)S(1)}, u32[]{:S(2)}, u32[]{:S(2)}) collective-permute-start(bf16[4,192,128]{2,1,0:T(8,128)(2,1)S(1)} %collective-permute-done.4), channel_id=1, source_target_pairs={{0,1},{1,2},{2,3},{3,4},{4,5},{5,6},{6,7},{7,0},{8,9},{9,10},{10,1... | collective-permute-start | bytes 589832 | tf_op jit(solution)/shard_map/ppermute | solution.py:115
  68.1 32.8 %collective-permute-start.7 = (bf16[32,192,128]{2,1,0:T(8,128)(2,1)S(1)}, bf16[32,192,128]{2,1,0:T(8,128)(2,1)}, u32[]{:S(2)}, u32[]{:S(2)}) collective-permute-start(bf16[32,192,128]{2,1,0:T(8,128)(2,1)S(1)} %constant_dynamic-update-slice_fusion.mine_ref), channel_id=1, source_target_pairs={{0,8},{8,0},{16,24},{24,16},{32,40},{40,32},{48,56},{56,48},{64,72... | collective-permute-start | bytes 4718600 | tf_op jit(solution)/shard_map/ppermute | solution.py:130
  74.4 24.3 %all-to-all-start.3 = ((bf16[32,2,32,2,128]{4,2,3,1,0:T(8,128)(2,1)}), bf16[32,2,32,2,128]{4,2,3,1,0:T(8,128)(2,1)S(1)}, u32[]{:S(2)}, u32[]{:S(2)}) async-start(bf16[32,2,32,2,128]{4,2,3,1,0:T(8,128)(2,1)} %bitcast.16), calls=%async_computation.3 | async-start | bytes 2097152 | tf_op jit(solution)/shard_map/all_to_all | solution.py:92
  109.5 14.2 %all-to-all-start.4 = ((f32[32,1,3072]{2,1,0:T(1,128)}), f32[32,1,3072]{2,1,0:T(1,128)S(1)}, u32[]{:S(2)}, u32[]{:S(2)}) async-start(f32[32,1,3072]{2,1,0:T(1,128)} %reshape.97), calls=%async_computation.4 | async-start | bytes 786432 | tf_op jit(solution)/shard_map/all_to_all | solution.py:141
  140.7 7.6 %collective-permute-start.8 = (bf16[4,192,128]{2,1,0:T(8,128)(2,1)S(1)}, bf16[4,192,128]{2,1,0:T(8,128)(2,1)S(1)}, u32[]{:S(2)}, u32[]{:S(2)}) collective-permute-start(bf16[4,192,128]{2,1,0:T(8,128)(2,1)S(1)} %get-tuple-element.9), channel_id=1, source_target_pairs={{0,1},{1,2},{2,3},{3,4},{4,5},{5,6},{6,7},{7,0},{8,9},{9,10},{10,1... | collective-permute-start | bytes 589832 | tf_op jit(solution)/shard_map/ppermute | solution.py:115
  140.7 7.5 %collective-permute-start.9 = (bf16[4,192,128]{2,1,0:T(8,128)(2,1)S(1)}, bf16[4,192,128]{2,1,0:T(8,128)(2,1)S(1)}, u32[]{:S(2)}, u32[]{:S(2)}) collective-permute-start(bf16[4,192,128]{2,1,0:T(8,128)(2,1)S(1)} %get-tuple-element.9), channel_id=1, source_target_pairs={{0,7},{1,0},{2,1},{3,2},{4,3},{5,4},{6,5},{7,6},{8,15},{9,8},{10,9... | collective-permute-start | bytes 589832 | tf_op jit(solution)/shard_map/ppermute | solution.py:118
  148.2 6.7 %collective-permute-start.10 = (bf16[4,192,128]{2,1,0:T(8,128)(2,1)S(1)}, bf16[4,192,128]{2,1,0:T(8,128)(2,1)S(1)}, u32[]{:S(2)}, u32[]{:S(2)}) collective-permute-start(bf16[4,192,128]{2,1,0:T(8,128)(2,1)S(1)} %collective-permute-done.8), channel_id=1, source_target_pairs={{0,1},{1,2},{2,3},{3,4},{4,5},{5,6},{6,7},{7,0},{8,9},{9,10},{10,1... | collective-permute-start | bytes 589832 | tf_op jit(solution)/shard_map/ppermute | solution.py:115
  148.2 6.7 %collective-permute-start.11 = (bf16[4,192,128]{2,1,0:T(8,128)(2,1)S(1)}, bf16[4,192,128]{2,1,0:T(8,128)(2,1)S(1)}, u32[]{:S(2)}, u32[]{:S(2)}) collective-permute-start(bf16[4,192,128]{2,1,0:T(8,128)(2,1)S(1)} %collective-permute-done.9), channel_id=1, source_target_pairs={{0,7},{1,0},{2,1},{3,2},{4,3},{5,4},{6,5},{7,6},{8,15},{9,8},{10,9... | collective-permute-start | bytes 589832 | tf_op jit(solution)/shard_map/ppermute | solution.py:118
  154.9 5.7 %collective-permute-start.12 = (bf16[4,192,128]{2,1,0:T(8,128)(2,1)S(1)}, bf16[4,192,128]{2,1,0:T(8,128)(2,1)S(1)}, u32[]{:S(2)}, u32[]{:S(2)}) collective-permute-start(bf16[4,192,128]{2,1,0:T(8,128)(2,1)S(1)} %collective-permute-done.10), channel_id=1, source_target_pairs={{0,1},{1,2},{2,3},{3,4},{4,5},{5,6},{6,7},{7,0},{8,9},{9,10},{10,1... | collective-permute-start | bytes 589832 | tf_op jit(solution)/shard_map/ppermute | solution.py:115
  154.9 5.8 %collective-permute-start.13 = (bf16[4,192,128]{2,1,0:T(8,128)(2,1)S(1)}, bf16[4,192,128]{2,1,0:T(8,128)(2,1)S(1)}, u32[]{:S(2)}, u32[]{:S(2)}) collective-permute-start(bf16[4,192,128]{2,1,0:T(8,128)(2,1)S(1)} %collective-permute-done.11), channel_id=1, source_target_pairs={{0,7},{1,0},{2,1},{3,2},{4,3},{5,4},{6,5},{7,6},{8,15},{9,8},{10,9... | collective-permute-start | bytes 589832 | tf_op jit(solution)/shard_map/ppermute | solution.py:118
  160.6 5.7 %collective-permute-start.14 = (bf16[4,192,128]{2,1,0:T(8,128)(2,1)S(1)}, bf16[4,192,128]{2,1,0:T(8,128)(2,1)S(1)}, u32[]{:S(2)}, u32[]{:S(2)}) collective-permute-start(bf16[4,192,128]{2,1,0:T(8,128)(2,1)S(1)} %collective-permute-done.12), channel_id=1, source_target_pairs={{0,1},{1,2},{2,3},{3,4},{4,5},{5,6},{6,7},{7,0},{8,9},{9,10},{10,1... | collective-permute-start | bytes 589832 | tf_op jit(solution)/shard_map/ppermute | solution.py:115
  166.4 7.3 %collective-permute-start.15 = (bf16[32,192,128]{2,1,0:T(8,128)(2,1)S(1)}, bf16[32,192,128]{2,1,0:T(8,128)(2,1)S(1)}, u32[]{:S(2)}, u32[]{:S(2)}) collective-permute-start(bf16[32,192,128]{2,1,0:T(8,128)(2,1)S(1)} %constant_dynamic-update-slice_fusion.8.mine_ref), channel_id=1, source_target_pairs={{0,8},{8,0},{16,24},{24,16},{32,40},{40,32},{48,56},{56,48},{64,72... | collective-permute-start | bytes 4718600 | tf_op jit(solution)/shard_map/ppermute | solution.py:130
  (8 other events, 26.8 us)

commit v2 on v1

--- a/solution.py
+++ b/solution.py
@@ -1,5 +1,3 @@
-import math
-
 import jax
 import jax.numpy as jnp
 import numpy as np
@@ -7,6 +5,7 @@
 from jax.experimental import pallas as pl
 from jax.experimental.pallas import tpu as pltpu
 from jax.sharding import PartitionSpec as P
+
 
 LEVELS = 2
 HIGH = lax.Precision.HIGHEST
@@ -85,13 +84,16 @@
     ksrc = kernel[:, 0].reshape(nnz, per_slot, ntm, block // (per_slot * ntm), block)
     ksrc = jnp.transpose(ksrc, (2, 0, 1, 3, 4))
     klags = lax.all_to_all(ksrc, "tm", 0, 0, tiled=True).astype(jnp.float32)
-    kspec = jnp.einsum(
-        "xqt,tkhij->qhxkij", fwd_table.reshape(2, half, length), klags, precision=HIGH
-    ).astype(jnp.bfloat16)
-    kspec = kspec.reshape(ntm, 2, nnz, block // (per_slot * ntm), block)
-    kspec = lax.all_to_all(kspec, "tm", 0, 0, tiled=True)
+
+    def kernel_spectrum():
+        kspec = jnp.einsum(
+            "xqt,tkhij->qhxkij", fwd_table.reshape(2, half, length), klags, precision=HIGH
+        ).astype(jnp.bfloat16)
+        kspec = kspec.reshape(ntm, 2, nnz, block // (per_slot * ntm), block)
+        kspec = lax.all_to_all(kspec, "tm", 0, 0, tiled=True)
+        return jnp.transpose(kspec, (2, 1, 0, 3, 4)).reshape(nnz, block, block)
+
     local_rows = pattern[:, 0] - my_state * rows_local
-    kk = jnp.transpose(kspec, (2, 1, 0, 3, 4)).reshape(nnz, block, block)
     row_of = jnp.clip(local_rows, 0, rows_local - 1)
     real_slot = (my_slot != 0).astype(jnp.float32)
 
@@ -103,7 +105,8 @@
     position = jnp.where(rel == 0, 0, position)
     cb_half = (col_block // blocks_half) % per_slot
     cb_src = (cb_half != my_half).astype(jnp.int32)
-    pick = position * blocks_half + col_block % blocks_half
+    pick_ring = position * blocks_half + col_block % blocks_half
+    pick_ordered = (col_block // rows_local) * blocks_half + col_block % blocks_half
     fwd = [(i, (i + 1) % nst) for i in range(nst)]
     bwd = [(i, (i - 1) % nst) for i in range(nst)]
 
@@ -119,14 +122,21 @@
                 parts.append(b)
         return jnp.concatenate(parts, 0)
 
-    def respond(left):
+    def respond(left, on_ring):
         xs = jnp.einsum("qt,tcn->qcn", fwd_table, left, precision=HIGH).astype(jnp.bfloat16)
         xs = xs.reshape(2, half, csl, per_slot, sh)
         xs = jnp.transpose(xs, (1, 3, 0, 2, 4)).reshape(ntm, 2, csl, sh)
         xs = lax.all_to_all(xs, "tm", 0, 0, tiled=True)
         xs = xs.reshape(ntm, 2, csl, blocks_half, block)
         xs = jnp.transpose(xs, (3, 1, 0, 2, 4)).reshape(blocks_half, 2 * cols, block)
-        mine = ring_gather(xs)
+        if on_ring:
+            mine = ring_gather(xs)
+            pick = pick_ring
+            kk = kk_prev
+        else:
+            mine = lax.all_gather(xs, "state", axis=0, tiled=True)
+            pick = pick_ordered
+            kk = kernel_spectrum()
         other = lax.ppermute(mine, "tm", swap)
         prod = block_products(pick, cb_src, row_of, mine, other, kk, rows_local)
         ah = block // per_slot
@@ -141,15 +151,16 @@
         ys = lax.all_to_all(ys, "tm", 0, 0, tiled=True)
         ys = ys.reshape(half, per_slot, 2, csl, rows_local, block // per_slot)
         ys = jnp.transpose(ys, (2, 0, 3, 4, 1, 5)).reshape(2, half, csl, states_local)
-        return jnp.einsum("tq,qcn->tcn", inv_table, ys.reshape(length, csl, states_local), precision=HIGH)
+        return kk, jnp.einsum("tq,qcn->tcn", inv_table, ys.reshape(length, csl, states_local), precision=HIGH)
 
     field = solution[0].reshape(ntm, csl, states_local)
     field = lax.all_to_all(field, "tm", 0, 0, tiled=True)
     times = jnp.arange(length, dtype=jnp.int32)[:, None, None]
+    kk_prev = None
     for level_index in range(LEVELS):
         boundary = offsets[level_index]
         left = jnp.where(times < boundary, field, 0.0)
-        response = respond(left)
+        kk_prev, response = respond(left, level_index > 0)
         field = field + jnp.where(times >= boundary, response, 0.0)
     field = lax.all_to_all(field, "tm", 0, 0, tiled=True)
     return field.reshape(1, cols, states_local)

time: 217 us -> 235 us (1.083)
  waiting for transfers between devices: 68.5 us -> 83.2 us
  between operations: 0.52 us -> 13.8 us
  starting transfers between devices: 50.6 us -> 40.8 us
    all_gather x0 -> x1, waiting for transfers between devices: none -> 28.2 us  [respond(): mine = lax.all_gather(xs, 'state', axis=0, tiled=True)]
    ppermute x8 -> x4, waiting for transfers between devices: 31.4 us -> 17.4 us  [ring_gather(): a = lax.ppermute(a, 'state', fwd)]
    ppermute x6 -> x3, starting transfers between devices: 17.3 us -> 7.39 us  [ring_gather(): b = lax.ppermute(b, 'state', bwd)]
    unnamed x41 -> x29, local copies, waits for them, and re-layouts: 4.34 us -> 5.28 us
  transfers between devices with their start and end apart: 20 -> 14, of which waited for: 11 -> 9; matrix products, arithmetic and copies ran while one was open for 6% -> 5% of each run, Pallas kernels for 0% -> 0%
where the time goes in v2:
time: 235 us; the launch traced here: 234 us
  waiting for transfers between devices  83.2 us (35%)
  blocking collectives  52.2 us (22%)
  starting transfers between devices  40.8 us (17%)
  local copies, waits for them, and re-layouts  20.5 us (9%)
  between operations  13.8 us (6%)
  Pallas kernels  10.1 us (4%)
  other arithmetic  10 us (4%)
  matrix products  3.63 us (2%)
    all_gather x1, waiting for transfers between devices, respond(): mine = lax.all_gather(xs, 'state', axis=0, tiled=True)  28.2 us
    all_to_all x2, blocking collectives, respond(): xs = lax.all_to_all(xs, 'tm', 0, 0, tiled=True)  23.6 us
    ppermute x4, waiting for transfers between devices, ring_gather(): a = lax.ppermute(a, 'state', fwd)  17.4 us
    all_to_all x1, blocking collectives, shards(): field = lax.all_to_all(field, 'tm', 0, 0, tiled=True)  14.9 us
    all_to_all x1, waiting for transfers between devices, kernel_spectrum(): kspec = lax.all_to_all(kspec, 'tm', 0, 0, tiled=True)  14.9 us
    all_to_all x1, blocking collectives, respond(): ys = lax.all_to_all(ys, 'tm', 0, 0, tiled=True)  13.6 us
    all_to_all x1, waiting for transfers between devices, shards(): field = lax.all_to_all(field, 'tm', 0, 0, tiled=True)  10.1 us
    pallas_call x2, Pallas kernels, block_products(): pl.pallas_call(_products_body, grid_spec=pltpu.PrefetchScalarGridSpec(num...  10.1 us
  transfers between devices with their start and end apart: 14, of which 9 were waited for; matrix products, arithmetic and copies ran while one was open for 5% of the time, Pallas kernels for 0%

profile of v2, /device:TPU:1, one launch (start us, length us, event | category | flops | bytes accessed | tf_op | source)
XLA Modules:
  0.0 234.3 jit_solution(2262654827133071560)
XLA Ops:
  8.5 8.6 %all-to-all-start = ((f32[32,3,1024]{2,1,0:T(4,128)}), f32[32,3,1024]{2,1,0:T(4,128)S(1)}, u32[]{:S(2)}, u32[]{:S(2)}) async-start(f32[32,3,1024]{2,1,0:T(4,128)} %reshape_squeeze.6), calls=%async_computation | async-start | bytes 1048576 | tf_op jit(solution)/shard_map/all_to_all | solution.py:157
  18.5 10.1 %all-to-all-done = f32[32,3,1024]{2,1,0:T(4,128)S(1)} async-done(((f32[32,3,1024]{2,1,0:T(4,128)}), f32[32,3,1024]{2,1,0:T(4,128)S(1)}, u32[]{:S(2)}, u32[]{:S(2)}) %all-to-all-start) | async-done | bytes 393248 | tf_op jit(solution)/shard_map/all_to_all | solution.py:157
  29.6 11.9 %all_to_all.40 = bf16[32,2,3,512]{3,1,2,0:T(2,128)(2,1)S(1)} all-to-all(bf16[32,2,3,512]{3,1,2,0:T(2,128)(2,1)S(1)} %bitcast.122), channel_id=1, replica_groups=mesh['tm'=32,'state'=8] {'tm'}, dimensions={0} | all-to-all | bytes 393216 | tf_op jit(solution)/shard_map/all_to_all | solution.py:129
  45.2 3.8 %all-to-all-start.2 = ((bf16[32,32,2,2,128]{4,3,2,1,0:T(2,128)(2,1)}), bf16[32,32,2,2,128]{4,3,2,1,0:T(2,128)(2,1)S(1)}, u32[]{:S(2)}, u32[]{:S(2)}) async-start(bf16[32,32,2,2,128]{4,3,2,1,0:T(2,128)(2,1)} %copy.61), calls=%async_computation.2 | async-start | bytes 2097152 | tf_op jit(solution)/shard_map/all_to_all | solution.py:86
  49.0 28.2 %all-gather.2.cloned.1.call-done.mine_ref = bf16[32,192,128]{2,1,0:T(8,128)(2,1)} async-done(((bf16[4,192,128]{2,1,0:T(8,128)(2,1)}), bf16[32,192,128]{2,1,0:T(8,128)(2,1)}) %all-gather.2.cloned.1.call-update) | async-done | bytes 1572880 | tf_op jit(solution)/shard_map/all_gather | solution.py:137
  77.2 4.7 %collective-permute-start = (bf16[32,192,128]{2,1,0:T(8,128)(2,1)}, bf16[32,192,128]{2,1,0:T(8,128)(2,1)S(1)}, u32[]{:S(2)}, u32[]{:S(2)}) collective-permute-start(bf16[32,192,128]{2,1,0:T(8,128)(2,1)} %all-gather.2.cloned.1.call-done.mine_ref), channel_id=1, source_target_pairs={{0,8},{8,0},{16,24},{24,16},{32,40},{40,32},{48,56},{56,48},{64,72... | collective-permute-start | bytes 4718600 | tf_op jit(solution)/shard_map/ppermute | solution.py:140
  84.9 7.1 %all-to-all-start.3 = ((bf16[32,2,32,2,128]{4,2,3,1,0:T(8,128)(2,1)}), bf16[32,2,32,2,128]{4,2,3,1,0:T(8,128)(2,1)S(1)}, u32[]{:S(2)}, u32[]{:S(2)}) async-start(bf16[32,2,32,2,128]{4,2,3,1,0:T(8,128)(2,1)} %bitcast.16), calls=%async_computation.3 | async-start | bytes 2097152 | tf_op jit(solution)/shard_map/all_to_all | solution.py:93
  94.2 14.9 %all-to-all-done.3 = bf16[32,2,32,2,128]{4,2,3,1,0:T(8,128)(2,1)S(1)} async-done(((bf16[32,2,32,2,128]{4,2,3,1,0:T(8,128)(2,1)}), bf16[32,2,32,2,128]{4,2,3,1,0:T(8,128)(2,1)S(1)}, u32[]{:S(2)}, u32[]{:S(2)}) %all-to-all-start.3) | async-done | bytes 1048608 | tf_op jit(solution)/shard_map/all_to_all | solution.py:93
  109.0 2.1 copy.64
  112.3 5.1 %shard_map.64 = f32[8,192,128]{2,1,0:T(8,128)} custom-call(s32[32]{0:T(128)} %multiply_add_fusion.pick_ref, s32[32]{0:T(128)} %compare_convert_fusion.src_ref, s32[32]{0:T(128)} %clamp_bitcast_fusion.row_ref, bf16[32,192,128]{2,1,0:T(8,128)(2,1)} %all-gather.2.cloned.1.call-done.mine_ref, bf16[32,192,128]{2,1,0:T(8,128)(2,1)} %copy-done.1, ...), custom_call_target="tpu_custom_call" | custom-call | tf_op jit(solution)/shard_map/pallas_call | solution.py:52
  120.9 3.9 %all-to-all-start.4 = ((f32[32,1,3072]{2,1,0:T(1,128)}), f32[32,1,3072]{2,1,0:T(1,128)S(1)}, u32[]{:S(2)}, u32[]{:S(2)}) async-start(f32[32,1,3072]{2,1,0:T(1,128)} %reshape.97), calls=%async_computation.4 | async-start | bytes 786432 | tf_op jit(solution)/shard_map/all_to_all | solution.py:151
  125.5 9.6 %all-to-all-done.4 = f32[32,1,3072]{2,1,0:T(1,128)S(1)} async-done(((f32[32,1,3072]{2,1,0:T(1,128)}), f32[32,1,3072]{2,1,0:T(1,128)S(1)}, u32[]{:S(2)}, u32[]{:S(2)}) %all-to-all-start.4) | async-done | bytes 393248 | tf_op jit(solution)/shard_map/all_to_all | solution.py:151
  140.0 11.7 %all_to_all.41 = bf16[32,2,3,512]{3,1,2,0:T(2,128)(2,1)S(1)} all-to-all(bf16[32,2,3,512]{3,1,2,0:T(2,128)(2,1)S(1)} %bitcast.126), channel_id=1, replica_groups=mesh['tm'=32,'state'=8] {'tm'}, dimensions={0} | all-to-all | bytes 393216 | tf_op jit(solution)/shard_map/all_to_all | solution.py:129
  154.8 4.8 %collective-permute-done.1 = bf16[4,192,128]{2,1,0:T(8,128)(2,1)S(1)} collective-permute-done((bf16[4,192,128]{2,1,0:T(8,128)(2,1)S(1)}, bf16[4,192,128]{2,1,0:T(8,128)(2,1)S(1)}, u32[]{:S(2)}, u32[]{:S(2)}) %collective-permute-start.1) | collective-permute-done | bytes 196640 | tf_op jit(solution)/shard_map/ppermute | solution.py:118
  159.6 2.7 %collective-permute-start.4 = (bf16[4,192,128]{2,1,0:T(8,128)(2,1)S(1)}, bf16[4,192,128]{2,1,0:T(8,128)(2,1)S(1)}, u32[]{:S(2)}, u32[]{:S(2)}) collective-permute-start(bf16[4,192,128]{2,1,0:T(8,128)(2,1)S(1)} %collective-permute-done.2), channel_id=1, source_target_pairs={{0,7},{1,0},{2,1},{3,2},{4,3},{5,4},{6,5},{7,6},{8,15},{9,8},{10,9... | collective-permute-start | bytes 589832 | tf_op jit(solution)/shard_map/ppermute | solution.py:121
  162.4 3.9 %collective-permute-done.3 = bf16[4,192,128]{2,1,0:T(8,128)(2,1)S(1)} collective-permute-done((bf16[4,192,128]{2,1,0:T(8,128)(2,1)S(1)}, bf16[4,192,128]{2,1,0:T(8,128)(2,1)S(1)}, u32[]{:S(2)}, u32[]{:S(2)}) %collective-permute-start.3) | collective-permute-done | bytes 196640 | tf_op jit(solution)/shard_map/ppermute | solution.py:118
  166.3 2.7 %collective-permute-start.6 = (bf16[4,192,128]{2,1,0:T(8,128)(2,1)S(1)}, bf16[4,192,128]{2,1,0:T(8,128)(2,1)S(1)}, u32[]{:S(2)}, u32[]{:S(2)}) collective-permute-start(bf16[4,192,128]{2,1,0:T(8,128)(2,1)S(1)} %collective-permute-done.4), channel_id=1, source_target_pairs={{0,7},{1,0},{2,1},{3,2},{4,3},{5,4},{6,5},{7,6},{8,15},{9,8},{10,9... | collective-permute-start | bytes 589832 | tf_op jit(solution)/shard_map/ppermute | solution.py:121
  169.0 3.0 %collective-permute-done.5 = bf16[4,192,128]{2,1,0:T(8,128)(2,1)S(1)} collective-permute-done((bf16[4,192,128]{2,1,0:T(8,128)(2,1)S(1)}, bf16[4,192,128]{2,1,0:T(8,128)(2,1)S(1)}, u32[]{:S(2)}, u32[]{:S(2)}) %collective-permute-start.5) | collective-permute-done | bytes 196640 | tf_op jit(solution)/shard_map/ppermute | solution.py:118
  172.1 5.7 %collective-permute-done.7 = bf16[4,192,128]{2,1,0:T(8,128)(2,1)S(1)} collective-permute-done((bf16[4,192,128]{2,1,0:T(8,128)(2,1)S(1)}, bf16[4,192,128]{2,1,0:T(8,128)(2,1)S(1)}, u32[]{:S(2)}, u32[]{:S(2)}) %collective-permute-start.7) | collective-permute-done | bytes 196640 | tf_op jit(solution)/shard_map/ppermute | solution.py:118
  177.8 4.5 %collective-permute-start.8 = (bf16[32,192,128]{2,1,0:T(8,128)(2,1)S(1)}, bf16[32,192,128]{2,1,0:T(8,128)(2,1)S(1)}, u32[]{:S(2)}, u32[]{:S(2)}) collective-permute-start(bf16[32,192,128]{2,1,0:T(8,128)(2,1)S(1)} %constant_dynamic-update-slice_fusion.mine_ref), channel_id=1, source_target_pairs={{0,8},{8,0},{16,24},{24,16},{32,40},{40,32},{48,56},{56,48},{64,72... | collective-permute-start | bytes 4718600 | tf_op jit(solution)/shard_map/ppermute | solution.py:140
  182.3 3.0 %collective-permute-done.8.other_ref = bf16[32,192,128]{2,1,0:T(8,128)(2,1)S(1)} collective-permute-done((bf16[32,192,128]{2,1,0:T(8,128)(2,1)S(1)}, bf16[32,192,128]{2,1,0:T(8,128)(2,1)S(1)}, u32[]{:S(2)}, u32[]{:S(2)}) %collective-permute-start.8) | collective-permute-done | bytes 1572896 | tf_op jit(solution)/shard_map/ppermute | solution.py:140
  186.5 5.1 %shard_map.65 = f32[8,192,128]{2,1,0:T(8,128)} custom-call(s32[32]{0:T(128)} %get-tuple-element.5.pick_ref, s32[32]{0:T(128)} %compare_convert_fusion.src_ref, s32[32]{0:T(128)} %clamp_bitcast_fusion.row_ref, bf16[32,192,128]{2,1,0:T(8,128)(2,1)} %copy-done, bf16[32,192,128]{2,1,0:T(8,128)(2,1)} %copy-done.2, bf16[32,128,128]{2,1,0:T(8,128)(2,1)} %bitcast.110), custom_call_target="tpu_custom_call" | custom-call | tf_op jit(solution)/shard_map/pallas_call | solution.py:52
  194.3 13.6 %all_to_all.42 = f32[32,1,3072]{2,1,0:T(1,128)S(1)} all-to-all(f32[32,1,3072]{2,1,0:T(1,128)S(1)} %reshape.99), channel_id=1, replica_groups=mesh['tm'=32,'state'=8] {'tm'}, dimensions={0} | all-to-all | bytes 786432 | tf_op jit(solution)/shard_map/all_to_all | solution.py:151
  211.6 14.9 %all_to_all.43 = f32[32,3,1024]{2,1,0:T(4,128)S(1)} all-to-all(f32[32,3,1024]{2,1,0:T(4,128)S(1)} %copy.80), channel_id=1, replica_groups=mesh['tm'=32,'state'=8] {'tm'}, dimensions={0} | all-to-all | bytes 786432 | tf_op jit(solution)/shard_map/all_to_all | solution.py:165
  (86 shorter events, 34.9 us)
Async XLA Ops:
  6.5 22.0 %copy-start.5 = (f32[32,32,1]{1,0,2:T(8,128)S(1)}, f32[32,32,1]{1,0,2:T(8,128)}, u32[]{:S(2)}) copy-start(f32[32,32,1]{1,0,2:T(8,128)} %constant.111) | copy-start | bytes 12292
  6.5 10.6 %copy-start.7 = (s32[2]{0:T(128)S(1)}, s32[2]{0:T(128)}, u32[]{:S(2)}) copy-start(s32[2]{0:T(128)} %param.9) | copy-start | bytes 28
  8.5 20.0 %all-to-all-start = ((f32[32,3,1024]{2,1,0:T(4,128)}), f32[32,3,1024]{2,1,0:T(4,128)S(1)}, u32[]{:S(2)}, u32[]{:S(2)}) async-start(f32[32,3,1024]{2,1,0:T(4,128)} %reshape_squeeze.6), calls=%async_computation | async-start | bytes 1048576 | tf_op jit(solution)/shard_map/all_to_all | solution.py:157
  17.1 60.1 %all-gather.2.cloned.1.call-start = ((), (), s32[]{:S(2)}) async-start(), calls=%async_computation.8 | async-start | bytes 1769472 | tf_op jit(solution)/shard_map/all_gather | solution.py:137
  28.6 13.9 %copy-start.3 = (bf16[32,1,128,128]{3,2,1,0:T(8,128)(2,1)S(1)}, bf16[32,1,128,128]{3,2,1,0:T(8,128)(2,1)}, u32[]{:S(2)}) copy-start(bf16[32,1,128,128]{3,2,1,0:T(8,128)(2,1)} %param.7) | copy-start | bytes 3145732
  43.1 38.8 %copy-start.6 = (f32[2,16,32,1,1,1]{2,1,5,4,3,0:T(8,128)S(1)}, f32[2,16,32,1,1,1]{2,1,5,4,3,0:T(8,128)}, u32[]{:S(2)}) copy-start(f32[2,16,32,1,1,1]{2,1,5,4,3,0:T(8,128)} %constant.112) | copy-start | bytes 12292
  45.2 36.8 %all-to-all-start.2 = ((bf16[32,32,2,2,128]{4,3,2,1,0:T(2,128)(2,1)}), bf16[32,32,2,2,128]{4,3,2,1,0:T(2,128)(2,1)S(1)}, u32[]{:S(2)}, u32[]{:S(2)}) async-start(bf16[32,32,2,2,128]{4,3,2,1,0:T(2,128)(2,1)} %copy.61), calls=%async_computation.2 | async-start | bytes 2097152 | tf_op jit(solution)/shard_map/all_to_all | solution.py:86
  77.2 34.0 %collective-permute-start = (bf16[32,192,128]{2,1,0:T(8,128)(2,1)}, bf16[32,192,128]{2,1,0:T(8,128)(2,1)S(1)}, u32[]{:S(2)}, u32[]{:S(2)}) collective-permute-start(bf16[32,192,128]{2,1,0:T(8,128)(2,1)} %all-gather.2.cloned.1.call-done.mine_ref), channel_id=1, source_target_pairs={{0,8},{8,0},{16,24},{24,16},{32,40},{40,32},{48,56},{56,48},{64,72... | collective-permute-start | bytes 4718600 | tf_op jit(solution)/shard_map/ppermute | solution.py:140
  84.9 7.1 %copy-start.8 = (s32[32,2]{0,1:T(2,128)S(1)}, s32[32,2]{0,1:T(2,128)}, u32[]{:S(2)}) copy-start(s32[32,2]{0,1:T(2,128)} %param.8) | copy-start | bytes 772
  84.9 24.2 %all-to-all-start.3 = ((bf16[32,2,32,2,128]{4,2,3,1,0:T(8,128)(2,1)}), bf16[32,2,32,2,128]{4,2,3,1,0:T(8,128)(2,1)S(1)}, u32[]{:S(2)}, u32[]{:S(2)}) async-start(bf16[32,2,32,2,128]{4,2,3,1,0:T(8,128)(2,1)} %bitcast.16), calls=%async_computation.3 | async-start | bytes 2097152 | tf_op jit(solution)/shard_map/all_to_all | solution.py:93
  111.2 1.1 copy-start.1
  120.9 14.2 %all-to-all-start.4 = ((f32[32,1,3072]{2,1,0:T(1,128)}), f32[32,1,3072]{2,1,0:T(1,128)S(1)}, u32[]{:S(2)}, u32[]{:S(2)}) async-start(f32[32,1,3072]{2,1,0:T(1,128)} %reshape.97), calls=%async_computation.4 | async-start | bytes 786432 | tf_op jit(solution)/shard_map/all_to_all | solution.py:151
  137.4 1.1 copy-start.4
  152.1 7.6 %collective-permute-start.1 = (bf16[4,192,128]{2,1,0:T(8,128)(2,1)S(1)}, bf16[4,192,128]{2,1,0:T(8,128)(2,1)S(1)}, u32[]{:S(2)}, u32[]{:S(2)}) collective-permute-start(bf16[4,192,128]{2,1,0:T(8,128)(2,1)S(1)} %get-tuple-element.12), channel_id=1, source_target_pairs={{0,1},{1,2},{2,3},{3,4},{4,5},{5,6},{6,7},{7,0},{8,9},{9,10},{10,1... | collective-permute-start | bytes 589832 | tf_op jit(solution)/shard_map/ppermute | solution.py:118
  152.8 6.9 %collective-permute-start.2 = (bf16[4,192,128]{2,1,0:T(8,128)(2,1)S(1)}, bf16[4,192,128]{2,1,0:T(8,128)(2,1)S(1)}, u32[]{:S(2)}, u32[]{:S(2)}) collective-permute-start(bf16[4,192,128]{2,1,0:T(8,128)(2,1)S(1)} %get-tuple-element.12), channel_id=1, source_target_pairs={{0,7},{1,0},{2,1},{3,2},{4,3},{5,4},{6,5},{7,6},{8,15},{9,8},{10,9... | collective-permute-start | bytes 589832 | tf_op jit(solution)/shard_map/ppermute | solution.py:121
  159.6 6.7 %collective-permute-start.3 = (bf16[4,192,128]{2,1,0:T(8,128)(2,1)S(1)}, bf16[4,192,128]{2,1,0:T(8,128)(2,1)S(1)}, u32[]{:S(2)}, u32[]{:S(2)}) collective-permute-start(bf16[4,192,128]{2,1,0:T(8,128)(2,1)S(1)} %collective-permute-done.1), channel_id=1, source_target_pairs={{0,1},{1,2},{2,3},{3,4},{4,5},{5,6},{6,7},{7,0},{8,9},{9,10},{10,1... | collective-permute-start | bytes 589832 | tf_op jit(solution)/shard_map/ppermute | solution.py:118
  159.6 6.7 %collective-permute-start.4 = (bf16[4,192,128]{2,1,0:T(8,128)(2,1)S(1)}, bf16[4,192,128]{2,1,0:T(8,128)(2,1)S(1)}, u32[]{:S(2)}, u32[]{:S(2)}) collective-permute-start(bf16[4,192,128]{2,1,0:T(8,128)(2,1)S(1)} %collective-permute-done.2), channel_id=1, source_target_pairs={{0,7},{1,0},{2,1},{3,2},{4,3},{5,4},{6,5},{7,6},{8,15},{9,8},{10,9... | collective-permute-start | bytes 589832 | tf_op jit(solution)/shard_map/ppermute | solution.py:121
  166.3 5.7 %collective-permute-start.5 = (bf16[4,192,128]{2,1,0:T(8,128)(2,1)S(1)}, bf16[4,192,128]{2,1,0:T(8,128)(2,1)S(1)}, u32[]{:S(2)}, u32[]{:S(2)}) collective-permute-start(bf16[4,192,128]{2,1,0:T(8,128)(2,1)S(1)} %collective-permute-done.3), channel_id=1, source_target_pairs={{0,1},{1,2},{2,3},{3,4},{4,5},{5,6},{6,7},{7,0},{8,9},{9,10},{10,1... | collective-permute-start | bytes 589832 | tf_op jit(solution)/shard_map/ppermute | solution.py:118
  166.3 5.8 %collective-permute-start.6 = (bf16[4,192,128]{2,1,0:T(8,128)(2,1)S(1)}, bf16[4,192,128]{2,1,0:T(8,128)(2,1)S(1)}, u32[]{:S(2)}, u32[]{:S(2)}) collective-permute-start(bf16[4,192,128]{2,1,0:T(8,128)(2,1)S(1)} %collective-permute-done.4), channel_id=1, source_target_pairs={{0,7},{1,0},{2,1},{3,2},{4,3},{5,4},{6,5},{7,6},{8,15},{9,8},{10,9... | collective-permute-start | bytes 589832 | tf_op jit(solution)/shard_map/ppermute | solution.py:121
  172.0 5.7 %collective-permute-start.7 = (bf16[4,192,128]{2,1,0:T(8,128)(2,1)S(1)}, bf16[4,192,128]{2,1,0:T(8,128)(2,1)S(1)}, u32[]{:S(2)}, u32[]{:S(2)}) collective-permute-start(bf16[4,192,128]{2,1,0:T(8,128)(2,1)S(1)} %collective-permute-done.5), channel_id=1, source_target_pairs={{0,1},{1,2},{2,3},{3,4},{4,5},{5,6},{6,7},{7,0},{8,9},{9,10},{10,1... | collective-permute-start | bytes 589832 | tf_op jit(solution)/shard_map/ppermute | solution.py:118
  177.8 8.7 %copy-start = (bf16[32,192,128]{2,1,0:T(8,128)(2,1)}, bf16[32,192,128]{2,1,0:T(8,128)(2,1)S(1)}, u32[]{:S(2)}) copy-start(bf16[32,192,128]{2,1,0:T(8,128)(2,1)S(1)} %constant_dynamic-update-slice_fusion.mine_ref) | copy-start | bytes 4718596
  177.8 7.5 %collective-permute-start.8 = (bf16[32,192,128]{2,1,0:T(8,128)(2,1)S(1)}, bf16[32,192,128]{2,1,0:T(8,128)(2,1)S(1)}, u32[]{:S(2)}, u32[]{:S(2)}) collective-permute-start(bf16[32,192,128]{2,1,0:T(8,128)(2,1)S(1)} %constant_dynamic-update-slice_fusion.mine_ref), channel_id=1, source_target_pairs={{0,8},{8,0},{16,24},{24,16},{32,40},{40,32},{48,56},{56,48},{64,72... | collective-permute-start | bytes 4718600 | tf_op jit(solution)/shard_map/ppermute | solution.py:140
  185.3 1.1 copy-start.2
Sparse Core Ops, SparseCore 0:
  42.6 34.5 all-gather.1

commit v3 on v1

--- a/solution.py
+++ b/solution.py
@@ -134,13 +134,11 @@
         d, b = prod[:, cols:, :ah], prod[:, cols:, ah:]
         ys_re = a - real_slot * b
         ys_im = real_slot * (c_ + d) + (1.0 - real_slot) * b
-        ys_re = jnp.transpose(ys_re, (1, 0, 2)).reshape(cols, rows_local * ah)
-        ys_im = jnp.transpose(ys_im, (1, 0, 2)).reshape(cols, rows_local * ah)
-        ys = jnp.stack([ys_re, ys_im], 0).reshape(2, ntm, csl, rows_local, block // per_slot)
-        ys = jnp.transpose(ys, (1, 0, 2, 3, 4))
+        ys = jnp.stack([ys_re, ys_im], 0).reshape(2, rows_local, ntm, csl, ah)
+        ys = jnp.transpose(ys, (2, 0, 3, 1, 4)).reshape(ntm, -1, 2 * ah)
         ys = lax.all_to_all(ys, "tm", 0, 0, tiled=True)
-        ys = ys.reshape(half, per_slot, 2, csl, rows_local, block // per_slot)
-        ys = jnp.transpose(ys, (2, 0, 3, 4, 1, 5)).reshape(2, half, csl, states_local)
+        ys = ys.reshape(half, per_slot, 2, csl, rows_local // 2, 2, ah)
+        ys = jnp.transpose(ys, (2, 0, 3, 4, 5, 1, 6)).reshape(2, half, csl, states_local)
         return jnp.einsum("tq,qcn->tcn", inv_table, ys.reshape(length, csl, states_local), precision=HIGH)
 
     field = solution[0].reshape(ntm, csl, states_local)

time: 217 us -> 213 us (0.982)
  other arithmetic: 10.7 us -> 7.44 us
    transpose x4 -> x2, other arithmetic: 3.58 us -> 0.11 us  [respond(): ys = jnp.transpose(ys, (2, 0, 3, 1, 4)).reshape(ntm, -1, 2 * ah)]
    sub x0 -> x2, other arithmetic: none -> 3.31 us  [respond(): ys_re = a - real_slot * b]
    all_to_all x2 -> x0, other arithmetic: 3.14 us -> none  [respond(): ys = lax.all_to_all(ys, 'tm', 0, 0, tiled=True)]
    unnamed x41 -> x37, local copies, waits for them, and re-layouts: 4.34 us -> 2.23 us
where the time goes in v3:
time: 213 us; the launch traced here: 212 us
  waiting for transfers between devices  68.6 us (32%)
  blocking collectives  52.2 us (25%)
  starting transfers between devices  50.6 us (24%)
  local copies, waits for them, and re-layouts  19 us (9%)
  Pallas kernels  10.1 us (5%)
  other arithmetic  7.44 us (3%)
  matrix products  3.63 us (2%)
    ppermute x8, waiting for transfers between devices, ring_gather(): a = lax.ppermute(a, 'state', fwd)  31.4 us
    all_to_all x2, blocking collectives, respond(): xs = lax.all_to_all(xs, 'tm', 0, 0, tiled=True)  23.6 us
    ppermute x6, starting transfers between devices, ring_gather(): b = lax.ppermute(b, 'state', bwd)  17.3 us
    all_to_all x1, waiting for transfers between devices, shards(): kspec = lax.all_to_all(kspec, 'tm', 0, 0, tiled=True)  15.3 us
    all_to_all x1, blocking collectives, shards(): field = lax.all_to_all(field, 'tm', 0, 0, tiled=True)  14.9 us
    all_to_all x1, blocking collectives, respond(): ys = lax.all_to_all(ys, 'tm', 0, 0, tiled=True)  13.6 us
    pallas_call x2, Pallas kernels, block_products(): pl.pallas_call(_products_body, grid_spec=pltpu.PrefetchScalarGridSpec(num...  10.1 us
    all_to_all x1, waiting for transfers between devices, shards(): field = lax.all_to_all(field, 'tm', 0, 0, tiled=True)  9.66 us
  transfers between devices with their start and end apart: 20, of which 11 were waited for; matrix products, arithmetic and copies ran while one was open for 6% of the time, Pallas kernels for 0%

profile of v3, /device:TPU:1, one launch (start us, length us, event | category | flops | bytes accessed | tf_op | source)
XLA Modules:
  0.0 212.1 jit_solution(13202171862107925008)
XLA Ops:
  2.0 8.6 %all-to-all-start = ((f32[32,3,1024]{2,1,0:T(4,128)}), f32[32,3,1024]{2,1,0:T(4,128)S(1)}, u32[]{:S(2)}, u32[]{:S(2)}) async-start(f32[32,3,1024]{2,1,0:T(4,128)} %reshape_squeeze.6), calls=%async_computation | async-start | bytes 1048576 | tf_op jit(solution)/shard_map/all_to_all | solution.py:145
  12.3 9.7 %all-to-all-done = f32[32,3,1024]{2,1,0:T(4,128)S(1)} async-done(((f32[32,3,1024]{2,1,0:T(4,128)}), f32[32,3,1024]{2,1,0:T(4,128)S(1)}, u32[]{:S(2)}, u32[]{:S(2)}) %all-to-all-start) | async-done | bytes 393248 | tf_op jit(solution)/shard_map/all_to_all | solution.py:145
  23.1 11.9 %all_to_all.40 = bf16[32,2,3,512]{3,1,2,0:T(2,128)(2,1)S(1)} all-to-all(bf16[32,2,3,512]{3,1,2,0:T(2,128)(2,1)S(1)} %bitcast.104), channel_id=1, replica_groups=mesh['tm'=32,'state'=8] {'tm'}, dimensions={0} | all-to-all | bytes 393216 | tf_op jit(solution)/shard_map/all_to_all | solution.py:126
  37.5 3.9 %collective-permute-start.1 = (bf16[4,192,128]{2,1,0:T(8,128)(2,1)}, bf16[4,192,128]{2,1,0:T(8,128)(2,1)S(1)}, u32[]{:S(2)}, u32[]{:S(2)}) collective-permute-start(bf16[4,192,128]{2,1,0:T(8,128)(2,1)} %get-tuple-element.11), channel_id=1, source_target_pairs={{0,7},{1,0},{2,1},{3,2},{4,3},{5,4},{6,5},{7,6},{8,15},{9,8},{10,9... | collective-permute-start | bytes 589832 | tf_op jit(solution)/shard_map/ppermute | solution.py:118
  44.2 4.1 %all-to-all-start.2 = ((bf16[32,32,2,2,128]{4,3,2,1,0:T(2,128)(2,1)}), bf16[32,32,2,2,128]{4,3,2,1,0:T(2,128)(2,1)S(1)}, u32[]{:S(2)}, u32[]{:S(2)}) async-start(bf16[32,32,2,2,128]{4,3,2,1,0:T(2,128)(2,1)} %copy.67), calls=%async_computation.2 | async-start | bytes 2097152 | tf_op jit(solution)/shard_map/all_to_all | solution.py:87
  51.1 4.6 %collective-permute-done.2 = bf16[4,192,128]{2,1,0:T(8,128)(2,1)S(1)} collective-permute-done((bf16[4,192,128]{2,1,0:T(8,128)(2,1)S(1)}, bf16[4,192,128]{2,1,0:T(8,128)(2,1)S(1)}, u32[]{:S(2)}, u32[]{:S(2)}) %collective-permute-start.2) | collective-permute-done | bytes 196640 | tf_op jit(solution)/shard_map/ppermute | solution.py:115
  58.5 3.8 %collective-permute-done.4 = bf16[4,192,128]{2,1,0:T(8,128)(2,1)S(1)} collective-permute-done((bf16[4,192,128]{2,1,0:T(8,128)(2,1)S(1)}, bf16[4,192,128]{2,1,0:T(8,128)(2,1)S(1)}, u32[]{:S(2)}, u32[]{:S(2)}) %collective-permute-start.4) | collective-permute-done | bytes 196640 | tf_op jit(solution)/shard_map/ppermute | solution.py:115
  62.4 5.7 %collective-permute-done.6 = bf16[4,192,128]{2,1,0:T(8,128)(2,1)S(1)} collective-permute-done((bf16[4,192,128]{2,1,0:T(8,128)(2,1)S(1)}, bf16[4,192,128]{2,1,0:T(8,128)(2,1)S(1)}, u32[]{:S(2)}, u32[]{:S(2)}) %collective-permute-start.6) | collective-permute-done | bytes 196640 | tf_op jit(solution)/shard_map/ppermute | solution.py:115
  68.1 3.4 %collective-permute-start.7 = (bf16[32,192,128]{2,1,0:T(8,128)(2,1)S(1)}, bf16[32,192,128]{2,1,0:T(8,128)(2,1)}, u32[]{:S(2)}, u32[]{:S(2)}) collective-permute-start(bf16[32,192,128]{2,1,0:T(8,128)(2,1)S(1)} %constant_dynamic-update-slice_fusion.mine_ref), channel_id=1, source_target_pairs={{0,8},{8,0},{16,24},{24,16},{32,40},{40,32},{48,56},{56,48},{64,72... | collective-permute-start | bytes 4718600 | tf_op jit(solution)/shard_map/ppermute | solution.py:130
  74.4 7.2 %all-to-all-start.3 = ((bf16[32,2,32,2,128]{4,2,3,1,0:T(8,128)(2,1)}), bf16[32,2,32,2,128]{4,2,3,1,0:T(8,128)(2,1)S(1)}, u32[]{:S(2)}, u32[]{:S(2)}) async-start(bf16[32,2,32,2,128]{4,2,3,1,0:T(8,128)(2,1)} %bitcast.16), calls=%async_computation.3 | async-start | bytes 2097152 | tf_op jit(solution)/shard_map/all_to_all | solution.py:92
  83.3 15.3 %all-to-all-done.3 = bf16[32,2,32,2,128]{4,2,3,1,0:T(8,128)(2,1)S(1)} async-done(((bf16[32,2,32,2,128]{4,2,3,1,0:T(8,128)(2,1)}), bf16[32,2,32,2,128]{4,2,3,1,0:T(8,128)(2,1)S(1)}, u32[]{:S(2)}, u32[]{:S(2)}) %all-to-all-start.3) | async-done | bytes 1048608 | tf_op jit(solution)/shard_map/all_to_all | solution.py:92
  100.8 5.1 %shard_map.64 = f32[8,192,128]{2,1,0:T(8,128)} custom-call(s32[32]{0:T(128)} %fusion.20.pick_ref, s32[32]{0:T(128)} %compare_convert_fusion.src_ref, s32[32]{0:T(128)} %clamp_bitcast_fusion.row_ref, bf16[32,192,128]{2,1,0:T(8,128)(2,1)} %copy-done, bf16[32,192,128]{2,1,0:T(8,128)(2,1)} %collective-permute-done.7.other_ref, bf16[32,128,128]{2,1,0:T(8,128)(2,1)} %bitcast.93), custom_call_target="tpu_custom_call" | custom-call | tf_op jit(solution)/shard_map/pallas_call | solution.py:53
  109.1 3.9 %all-to-all-start.4 = ((f32[32,24,128]{2,1,0:T(8,128)}), f32[32,24,128]{2,1,0:T(8,128)S(1)}, u32[]{:S(2)}, u32[]{:S(2)}) async-start(f32[32,24,128]{2,1,0:T(8,128)} %reshape.90), calls=%async_computation.4 | async-start | bytes 786432 | tf_op jit(solution)/shard_map/all_to_all | solution.py:139
  114.2 9.1 %all-to-all-done.4 = f32[32,24,128]{2,1,0:T(8,128)S(1)} async-done(((f32[32,24,128]{2,1,0:T(8,128)}), f32[32,24,128]{2,1,0:T(8,128)S(1)}, u32[]{:S(2)}, u32[]{:S(2)}) %all-to-all-start.4) | async-done | bytes 393248 | tf_op jit(solution)/shard_map/all_to_all | solution.py:139
  126.5 11.7 %all_to_all.41 = bf16[32,2,3,512]{3,1,2,0:T(2,128)(2,1)S(1)} all-to-all(bf16[32,2,3,512]{3,1,2,0:T(2,128)(2,1)S(1)} %bitcast.107), channel_id=1, replica_groups=mesh['tm'=32,'state'=8] {'tm'}, dimensions={0} | all-to-all | bytes 393216 | tf_op jit(solution)/shard_map/all_to_all | solution.py:126
  141.2 4.8 %collective-permute-done.8 = bf16[4,192,128]{2,1,0:T(8,128)(2,1)S(1)} collective-permute-done((bf16[4,192,128]{2,1,0:T(8,128)(2,1)S(1)}, bf16[4,192,128]{2,1,0:T(8,128)(2,1)S(1)}, u32[]{:S(2)}, u32[]{:S(2)}) %collective-permute-start.8) | collective-permute-done | bytes 196640 | tf_op jit(solution)/shard_map/ppermute | solution.py:115
  148.8 3.9 %collective-permute-done.10 = bf16[4,192,128]{2,1,0:T(8,128)(2,1)S(1)} collective-permute-done((bf16[4,192,128]{2,1,0:T(8,128)(2,1)S(1)}, bf16[4,192,128]{2,1,0:T(8,128)(2,1)S(1)}, u32[]{:S(2)}, u32[]{:S(2)}) %collective-permute-start.10) | collective-permute-done | bytes 196640 | tf_op jit(solution)/shard_map/ppermute | solution.py:115
  155.5 3.0 %collective-permute-done.12 = bf16[4,192,128]{2,1,0:T(8,128)(2,1)S(1)} collective-permute-done((bf16[4,192,128]{2,1,0:T(8,128)(2,1)S(1)}, bf16[4,192,128]{2,1,0:T(8,128)(2,1)S(1)}, u32[]{:S(2)}, u32[]{:S(2)}) %collective-permute-start.12) | collective-permute-done | bytes 196640 | tf_op jit(solution)/shard_map/ppermute | solution.py:115
  158.5 5.7 %collective-permute-done.14 = bf16[4,192,128]{2,1,0:T(8,128)(2,1)S(1)} collective-permute-done((bf16[4,192,128]{2,1,0:T(8,128)(2,1)S(1)}, bf16[4,192,128]{2,1,0:T(8,128)(2,1)S(1)}, u32[]{:S(2)}, u32[]{:S(2)}) %collective-permute-start.14) | collective-permute-done | bytes 196640 | tf_op jit(solution)/shard_map/ppermute | solution.py:115
  164.2 4.3 %collective-permute-start.15 = (bf16[32,192,128]{2,1,0:T(8,128)(2,1)S(1)}, bf16[32,192,128]{2,1,0:T(8,128)(2,1)S(1)}, u32[]{:S(2)}, u32[]{:S(2)}) collective-permute-start(bf16[32,192,128]{2,1,0:T(8,128)(2,1)S(1)} %constant_dynamic-update-slice_fusion.8.mine_ref), channel_id=1, source_target_pairs={{0,8},{8,0},{16,24},{24,16},{32,40},{40,32},{48,56},{56,48},{64,72... | collective-permute-start | bytes 4718600 | tf_op jit(solution)/shard_map/ppermute | solution.py:130
  168.5 3.0 %collective-permute-done.15.other_ref = bf16[32,192,128]{2,1,0:T(8,128)(2,1)S(1)} collective-permute-done((bf16[32,192,128]{2,1,0:T(8,128)(2,1)S(1)}, bf16[32,192,128]{2,1,0:T(8,128)(2,1)S(1)}, u32[]{:S(2)}, u32[]{:S(2)}) %collective-permute-start.15) | collective-permute-done | bytes 1572896 | tf_op jit(solution)/shard_map/ppermute | solution.py:130
  172.7 5.1 %shard_map.65 = f32[8,192,128]{2,1,0:T(8,128)} custom-call(s32[32]{0:T(128)} %fusion.20.pick_ref, s32[32]{0:T(128)} %compare_convert_fusion.src_ref, s32[32]{0:T(128)} %clamp_bitcast_fusion.row_ref, bf16[32,192,128]{2,1,0:T(8,128)(2,1)} %copy-done.1, bf16[32,192,128]{2,1,0:T(8,128)(2,1)} %copy-done.2, bf16[32,128,128]{2,1,0:T(8,128)(2,1)} %bitcast.94), custom_call_target="tpu_custom_call" | custom-call | tf_op jit(solution)/shard_map/pallas_call | solution.py:53
  180.2 13.6 %all_to_all.42 = f32[32,24,128]{2,1,0:T(8,128)S(1)} all-to-all(f32[32,24,128]{2,1,0:T(8,128)S(1)} %reshape.96), channel_id=1, replica_groups=mesh['tm'=32,'state'=8] {'tm'}, dimensions={0} | all-to-all | bytes 786432 | tf_op jit(solution)/shard_map/all_to_all | solution.py:139
  196.2 14.9 %all_to_all.43 = f32[32,3,1024]{2,1,0:T(4,128)S(1)} all-to-all(f32[32,3,1024]{2,1,0:T(4,128)S(1)} %copy.86), channel_id=1, replica_groups=mesh['tm'=32,'state'=8] {'tm'}, dimensions={0} | all-to-all | bytes 786432 | tf_op jit(solution)/shard_map/all_to_all | solution.py:152
  (106 shorter events, 45.3 us)
Async XLA Ops:
  0.0 22.0 %copy-start.5 = (f32[32,32,1]{1,0,2:T(8,128)S(1)}, f32[32,32,1]{1,0,2:T(8,128)}, u32[]{:S(2)}) copy-start(f32[32,32,1]{1,0,2:T(8,128)} %constant.106) | copy-start | bytes 12292
  0.0 10.6 %copy-start.8 = (s32[2]{0:T(128)S(1)}, s32[2]{0:T(128)}, u32[]{:S(2)}) copy-start(s32[2]{0:T(128)} %param.9) | copy-start | bytes 28
  2.0 20.0 %all-to-all-start = ((f32[32,3,1024]{2,1,0:T(4,128)}), f32[32,3,1024]{2,1,0:T(4,128)S(1)}, u32[]{:S(2)}, u32[]{:S(2)}) async-start(f32[32,3,1024]{2,1,0:T(4,128)} %reshape_squeeze.6), calls=%async_computation | async-start | bytes 1048576 | tf_op jit(solution)/shard_map/all_to_all | solution.py:145
  22.0 19.5 %copy-start.3 = (bf16[32,1,128,128]{3,2,1,0:T(8,128)(2,1)S(1)}, bf16[32,1,128,128]{3,2,1,0:T(8,128)(2,1)}, u32[]{:S(2)}) copy-start(bf16[32,1,128,128]{3,2,1,0:T(8,128)(2,1)} %param.7) | copy-start | bytes 3145732
  35.9 12.4 %collective-permute-start = (bf16[4,192,128]{2,1,0:T(8,128)(2,1)}, bf16[4,192,128]{2,1,0:T(8,128)(2,1)S(1)}, u32[]{:S(2)}, u32[]{:S(2)}) collective-permute-start(bf16[4,192,128]{2,1,0:T(8,128)(2,1)} %get-tuple-element.11), channel_id=1, source_target_pairs={{0,1},{1,2},{2,3},{3,4},{4,5},{5,6},{6,7},{7,0},{8,9},{9,10},{10,1... | collective-permute-start | bytes 589832 | tf_op jit(solution)/shard_map/ppermute | solution.py:115
  37.5 10.9 %collective-permute-start.1 = (bf16[4,192,128]{2,1,0:T(8,128)(2,1)}, bf16[4,192,128]{2,1,0:T(8,128)(2,1)S(1)}, u32[]{:S(2)}, u32[]{:S(2)}) collective-permute-start(bf16[4,192,128]{2,1,0:T(8,128)(2,1)} %get-tuple-element.11), channel_id=1, source_target_pairs={{0,7},{1,0},{2,1},{3,2},{4,3},{5,4},{6,5},{7,6},{8,15},{9,8},{10,9... | collective-permute-start | bytes 589832 | tf_op jit(solution)/shard_map/ppermute | solution.py:118
  44.2 27.3 %all-to-all-start.2 = ((bf16[32,32,2,2,128]{4,3,2,1,0:T(2,128)(2,1)}), bf16[32,32,2,2,128]{4,3,2,1,0:T(2,128)(2,1)S(1)}, u32[]{:S(2)}, u32[]{:S(2)}) async-start(bf16[32,32,2,2,128]{4,3,2,1,0:T(2,128)(2,1)} %copy.67), calls=%async_computation.2 | async-start | bytes 2097152 | tf_op jit(solution)/shard_map/all_to_all | solution.py:87
  48.3 23.2 %copy-start.7 = (f32[2,16,32,1,1,1]{2,1,5,4,3,0:T(8,128)S(1)}, f32[2,16,32,1,1,1]{2,1,5,4,3,0:T(8,128)}, u32[]{:S(2)}) copy-start(f32[2,16,32,1,1,1]{2,1,5,4,3,0:T(8,128)} %constant.107) | copy-start | bytes 12292
  48.3 7.5 %collective-permute-start.2 = (bf16[4,192,128]{2,1,0:T(8,128)(2,1)S(1)}, bf16[4,192,128]{2,1,0:T(8,128)(2,1)S(1)}, u32[]{:S(2)}, u32[]{:S(2)}) collective-permute-start(bf16[4,192,128]{2,1,0:T(8,128)(2,1)S(1)} %collective-permute-done), channel_id=1, source_target_pairs={{0,1},{1,2},{2,3},{3,4},{4,5},{5,6},{6,7},{7,0},{8,9},{9,10},{10,1... | collective-permute-start | bytes 589832 | tf_op jit(solution)/shard_map/ppermute | solution.py:115
  48.4 7.4 %collective-permute-start.3 = (bf16[4,192,128]{2,1,0:T(8,128)(2,1)S(1)}, bf16[4,192,128]{2,1,0:T(8,128)(2,1)S(1)}, u32[]{:S(2)}, u32[]{:S(2)}) collective-permute-start(bf16[4,192,128]{2,1,0:T(8,128)(2,1)S(1)} %collective-permute-done.1), channel_id=1, source_target_pairs={{0,7},{1,0},{2,1},{3,2},{4,3},{5,4},{6,5},{7,6},{8,15},{9,8},{10,9... | collective-permute-start | bytes 589832 | tf_op jit(solution)/shard_map/ppermute | solution.py:118
  55.8 6.5 %collective-permute-start.4 = (bf16[4,192,128]{2,1,0:T(8,128)(2,1)S(1)}, bf16[4,192,128]{2,1,0:T(8,128)(2,1)S(1)}, u32[]{:S(2)}, u32[]{:S(2)}) collective-permute-start(bf16[4,192,128]{2,1,0:T(8,128)(2,1)S(1)} %collective-permute-done.2), channel_id=1, source_target_pairs={{0,1},{1,2},{2,3},{3,4},{4,5},{5,6},{6,7},{7,0},{8,9},{9,10},{10,1... | collective-permute-start | bytes 589832 | tf_op jit(solution)/shard_map/ppermute | solution.py:115
  55.8 6.6 %collective-permute-start.5 = (bf16[4,192,128]{2,1,0:T(8,128)(2,1)S(1)}, bf16[4,192,128]{2,1,0:T(8,128)(2,1)S(1)}, u32[]{:S(2)}, u32[]{:S(2)}) collective-permute-start(bf16[4,192,128]{2,1,0:T(8,128)(2,1)S(1)} %collective-permute-done.3), channel_id=1, source_target_pairs={{0,7},{1,0},{2,1},{3,2},{4,3},{5,4},{6,5},{7,6},{8,15},{9,8},{10,9... | collective-permute-start | bytes 589832 | tf_op jit(solution)/shard_map/ppermute | solution.py:118
  62.3 5.7 %collective-permute-start.6 = (bf16[4,192,128]{2,1,0:T(8,128)(2,1)S(1)}, bf16[4,192,128]{2,1,0:T(8,128)(2,1)S(1)}, u32[]{:S(2)}, u32[]{:S(2)}) collective-permute-start(bf16[4,192,128]{2,1,0:T(8,128)(2,1)S(1)} %collective-permute-done.4), channel_id=1, source_target_pairs={{0,1},{1,2},{2,3},{3,4},{4,5},{5,6},{6,7},{7,0},{8,9},{9,10},{10,1... | collective-permute-start | bytes 589832 | tf_op jit(solution)/shard_map/ppermute | solution.py:115
  68.1 32.8 %collective-permute-start.7 = (bf16[32,192,128]{2,1,0:T(8,128)(2,1)S(1)}, bf16[32,192,128]{2,1,0:T(8,128)(2,1)}, u32[]{:S(2)}, u32[]{:S(2)}) collective-permute-start(bf16[32,192,128]{2,1,0:T(8,128)(2,1)S(1)} %constant_dynamic-update-slice_fusion.mine_ref), channel_id=1, source_target_pairs={{0,8},{8,0},{16,24},{24,16},{32,40},{40,32},{48,56},{56,48},{64,72... | collective-permute-start | bytes 4718600 | tf_op jit(solution)/shard_map/ppermute | solution.py:130
  74.4 24.3 %all-to-all-start.3 = ((bf16[32,2,32,2,128]{4,2,3,1,0:T(8,128)(2,1)}), bf16[32,2,32,2,128]{4,2,3,1,0:T(8,128)(2,1)S(1)}, u32[]{:S(2)}, u32[]{:S(2)}) async-start(bf16[32,2,32,2,128]{4,2,3,1,0:T(8,128)(2,1)} %bitcast.16), calls=%async_computation.3 | async-start | bytes 2097152 | tf_op jit(solution)/shard_map/all_to_all | solution.py:92
  109.1 14.2 %all-to-all-start.4 = ((f32[32,24,128]{2,1,0:T(8,128)}), f32[32,24,128]{2,1,0:T(8,128)S(1)}, u32[]{:S(2)}, u32[]{:S(2)}) async-start(f32[32,24,128]{2,1,0:T(8,128)} %reshape.90), calls=%async_computation.4 | async-start | bytes 786432 | tf_op jit(solution)/shard_map/all_to_all | solution.py:139
  138.5 7.6 %collective-permute-start.8 = (bf16[4,192,128]{2,1,0:T(8,128)(2,1)S(1)}, bf16[4,192,128]{2,1,0:T(8,128)(2,1)S(1)}, u32[]{:S(2)}, u32[]{:S(2)}) collective-permute-start(bf16[4,192,128]{2,1,0:T(8,128)(2,1)S(1)} %get-tuple-element.9), channel_id=1, source_target_pairs={{0,1},{1,2},{2,3},{3,4},{4,5},{5,6},{6,7},{7,0},{8,9},{9,10},{10,1... | collective-permute-start | bytes 589832 | tf_op jit(solution)/shard_map/ppermute | solution.py:115
  138.6 7.5 %collective-permute-start.9 = (bf16[4,192,128]{2,1,0:T(8,128)(2,1)S(1)}, bf16[4,192,128]{2,1,0:T(8,128)(2,1)S(1)}, u32[]{:S(2)}, u32[]{:S(2)}) collective-permute-start(bf16[4,192,128]{2,1,0:T(8,128)(2,1)S(1)} %get-tuple-element.9), channel_id=1, source_target_pairs={{0,7},{1,0},{2,1},{3,2},{4,3},{5,4},{6,5},{7,6},{8,15},{9,8},{10,9... | collective-permute-start | bytes 589832 | tf_op jit(solution)/shard_map/ppermute | solution.py:118
  146.1 6.7 %collective-permute-start.10 = (bf16[4,192,128]{2,1,0:T(8,128)(2,1)S(1)}, bf16[4,192,128]{2,1,0:T(8,128)(2,1)S(1)}, u32[]{:S(2)}, u32[]{:S(2)}) collective-permute-start(bf16[4,192,128]{2,1,0:T(8,128)(2,1)S(1)} %collective-permute-done.8), channel_id=1, source_target_pairs={{0,1},{1,2},{2,3},{3,4},{4,5},{5,6},{6,7},{7,0},{8,9},{9,10},{10,1... | collective-permute-start | bytes 589832 | tf_op jit(solution)/shard_map/ppermute | solution.py:115
  146.1 6.7 %collective-permute-start.11 = (bf16[4,192,128]{2,1,0:T(8,128)(2,1)S(1)}, bf16[4,192,128]{2,1,0:T(8,128)(2,1)S(1)}, u32[]{:S(2)}, u32[]{:S(2)}) collective-permute-start(bf16[4,192,128]{2,1,0:T(8,128)(2,1)S(1)} %collective-permute-done.9), channel_id=1, source_target_pairs={{0,7},{1,0},{2,1},{3,2},{4,3},{5,4},{6,5},{7,6},{8,15},{9,8},{10,9... | collective-permute-start | bytes 589832 | tf_op jit(solution)/shard_map/ppermute | solution.py:118
  152.7 5.7 %collective-permute-start.12 = (bf16[4,192,128]{2,1,0:T(8,128)(2,1)S(1)}, bf16[4,192,128]{2,1,0:T(8,128)(2,1)S(1)}, u32[]{:S(2)}, u32[]{:S(2)}) collective-permute-start(bf16[4,192,128]{2,1,0:T(8,128)(2,1)S(1)} %collective-permute-done.10), channel_id=1, source_target_pairs={{0,1},{1,2},{2,3},{3,4},{4,5},{5,6},{6,7},{7,0},{8,9},{9,10},{10,1... | collective-permute-start | bytes 589832 | tf_op jit(solution)/shard_map/ppermute | solution.py:115
  152.7 5.8 %collective-permute-start.13 = (bf16[4,192,128]{2,1,0:T(8,128)(2,1)S(1)}, bf16[4,192,128]{2,1,0:T(8,128)(2,1)S(1)}, u32[]{:S(2)}, u32[]{:S(2)}) collective-permute-start(bf16[4,192,128]{2,1,0:T(8,128)(2,1)S(1)} %collective-permute-done.11), channel_id=1, source_target_pairs={{0,7},{1,0},{2,1},{3,2},{4,3},{5,4},{6,5},{7,6},{8,15},{9,8},{10,9... | collective-permute-start | bytes 589832 | tf_op jit(solution)/shard_map/ppermute | solution.py:118
  158.4 5.7 %collective-permute-start.14 = (bf16[4,192,128]{2,1,0:T(8,128)(2,1)S(1)}, bf16[4,192,128]{2,1,0:T(8,128)(2,1)S(1)}, u32[]{:S(2)}, u32[]{:S(2)}) collective-permute-start(bf16[4,192,128]{2,1,0:T(8,128)(2,1)S(1)} %collective-permute-done.12), channel_id=1, source_target_pairs={{0,1},{1,2},{2,3},{3,4},{4,5},{5,6},{6,7},{7,0},{8,9},{9,10},{10,1... | collective-permute-start | bytes 589832 | tf_op jit(solution)/shard_map/ppermute | solution.py:115
  164.2 7.3 %collective-permute-start.15 = (bf16[32,192,128]{2,1,0:T(8,128)(2,1)S(1)}, bf16[32,192,128]{2,1,0:T(8,128)(2,1)S(1)}, u32[]{:S(2)}, u32[]{:S(2)}) collective-permute-start(bf16[32,192,128]{2,1,0:T(8,128)(2,1)S(1)} %constant_dynamic-update-slice_fusion.8.mine_ref), channel_id=1, source_target_pairs={{0,8},{8,0},{16,24},{24,16},{32,40},{40,32},{48,56},{56,48},{64,72... | collective-permute-start | bytes 4718600 | tf_op jit(solution)/shard_map/ppermute | solution.py:130
  (8 other events, 26.8 us)

commit v4 on v3

--- a/solution.py
+++ b/solution.py
@@ -121,8 +121,8 @@
 
     def respond(left):
         xs = jnp.einsum("qt,tcn->qcn", fwd_table, left, precision=HIGH).astype(jnp.bfloat16)
-        xs = xs.reshape(2, half, csl, per_slot, sh)
-        xs = jnp.transpose(xs, (1, 3, 0, 2, 4)).reshape(ntm, 2, csl, sh)
+        xs = xs.reshape(2, half, csl, per_slot, blocks_half, block)
+        xs = jnp.transpose(xs, (1, 3, 0, 2, 4, 5)).reshape(ntm, -1, block)
         xs = lax.all_to_all(xs, "tm", 0, 0, tiled=True)
         xs = xs.reshape(ntm, 2, csl, blocks_half, block)
         xs = jnp.transpose(xs, (3, 1, 0, 2, 4)).reshape(blocks_half, 2 * cols, block)
@@ -138,10 +138,10 @@
         ys = jnp.transpose(ys, (2, 0, 3, 1, 4)).reshape(ntm, -1, 2 * ah)
         ys = lax.all_to_all(ys, "tm", 0, 0, tiled=True)
         ys = ys.reshape(half, per_slot, 2, csl, rows_local // 2, 2, ah)
-        ys = jnp.transpose(ys, (2, 0, 3, 4, 5, 1, 6)).reshape(2, half, csl, states_local)
-        return jnp.einsum("tq,qcn->tcn", inv_table, ys.reshape(length, csl, states_local), precision=HIGH)
+        ys = jnp.transpose(ys, (2, 0, 3, 4, 5, 1, 6)).reshape(length, csl * rows_local, block)
+        return jnp.einsum("tq,qcn->tcn", inv_table, ys, precision=HIGH)
 
-    field = solution[0].reshape(ntm, csl, states_local)
+    field = solution[0].reshape(ntm, csl * rows_local, block)
     field = lax.all_to_all(field, "tm", 0, 0, tiled=True)
     times = jnp.arange(length, dtype=jnp.int32)[:, None, None]
     for level_index in range(LEVELS):

time: 213 us -> 208 us (0.977)
  no operation moved by 1% of the time
where the time goes in v4:
time: 208 us
  waiting for transfers between devices  67.9 us (33%)
  blocking collectives  50.8 us (24%)
  starting transfers between devices  50.6 us (24%)
  local copies, waits for them, and re-layouts  17.6 us (8%)
  Pallas kernels  10.2 us (5%)
  other arithmetic  6.9 us (3%)
  matrix products  3.35 us (2%)
    ppermute x8, waiting for transfers between devices, ring_gather(): a = lax.ppermute(a, 'state', fwd)  31.4 us
    all_to_all x2, blocking collectives, respond(): xs = lax.all_to_all(xs, 'tm', 0, 0, tiled=True)  23.5 us
    ppermute x6, starting transfers between devices, ring_gather(): b = lax.ppermute(b, 'state', bwd)  17.3 us
    all_to_all x1, waiting for transfers between devices, shards(): kspec = lax.all_to_all(kspec, 'tm', 0, 0, tiled=True)  15.3 us
    all_to_all x1, blocking collectives, shards(): field = lax.all_to_all(field, 'tm', 0, 0, tiled=True)  13.7 us
    all_to_all x1, blocking collectives, respond(): ys = lax.all_to_all(ys, 'tm', 0, 0, tiled=True)  13.6 us
    pallas_call x2, Pallas kernels, block_products(): pl.pallas_call(_products_body, grid_spec=pltpu.PrefetchScalarGridSpec(num...  10.2 us
    all_to_all x1, waiting for transfers between devices, respond(): ys = lax.all_to_all(ys, 'tm', 0, 0, tiled=True)  9.1 us
  transfers between devices with their start and end apart: 20, of which 11 were waited for; matrix products, arithmetic and copies ran while one was open for 6% of the time, Pallas kernels for 0%

profile of v4, /device:TPU:1, one launch (start us, length us, event | category | flops | bytes accessed | tf_op | source)
XLA Modules:
  0.0 207.7 jit_solution(7699284327741006227)
XLA Ops:
  1.8 8.6 %all-to-all-start = ((f32[32,24,128]{2,1,0:T(8,128)}), f32[32,24,128]{2,1,0:T(8,128)S(1)}, u32[]{:S(2)}, u32[]{:S(2)}) async-start(f32[32,24,128]{2,1,0:T(8,128)} %reshape_squeeze.6), calls=%async_computation | async-start | bytes 786432 | tf_op jit(solution)/shard_map/all_to_all | solution.py:145
  11.7 8.9 %all-to-all-done = f32[32,24,128]{2,1,0:T(8,128)S(1)} async-done(((f32[32,24,128]{2,1,0:T(8,128)}), f32[32,24,128]{2,1,0:T(8,128)S(1)}, u32[]{:S(2)}, u32[]{:S(2)}) %all-to-all-start) | async-done | bytes 393248 | tf_op jit(solution)/shard_map/all_to_all | solution.py:145
  21.3 11.7 %all_to_all.40 = bf16[32,24,128]{2,1,0:T(8,128)(2,1)S(1)} all-to-all(bf16[32,24,128]{2,1,0:T(8,128)(2,1)S(1)} %bitcast.101), channel_id=1, replica_groups=mesh['tm'=32,'state'=8] {'tm'}, dimensions={0} | all-to-all | bytes 393216 | tf_op jit(solution)/shard_map/all_to_all | solution.py:126
  35.5 3.9 %collective-permute-start.1 = (bf16[4,192,128]{2,1,0:T(8,128)(2,1)}, bf16[4,192,128]{2,1,0:T(8,128)(2,1)S(1)}, u32[]{:S(2)}, u32[]{:S(2)}) collective-permute-start(bf16[4,192,128]{2,1,0:T(8,128)(2,1)} %get-tuple-element.11), channel_id=1, source_target_pairs={{0,7},{1,0},{2,1},{3,2},{4,3},{5,4},{6,5},{7,6},{8,15},{9,8},{10,9... | collective-permute-start | bytes 589832 | tf_op jit(solution)/shard_map/ppermute | solution.py:118
  42.2 4.1 %all-to-all-start.2 = ((bf16[32,32,2,2,128]{4,3,2,1,0:T(2,128)(2,1)}), bf16[32,32,2,2,128]{4,3,2,1,0:T(2,128)(2,1)S(1)}, u32[]{:S(2)}, u32[]{:S(2)}) async-start(bf16[32,32,2,2,128]{4,3,2,1,0:T(2,128)(2,1)} %copy.41), calls=%async_computation.2 | async-start | bytes 2097152 | tf_op jit(solution)/shard_map/all_to_all | solution.py:87
  49.1 4.6 %collective-permute-done.2 = bf16[4,192,128]{2,1,0:T(8,128)(2,1)S(1)} collective-permute-done((bf16[4,192,128]{2,1,0:T(8,128)(2,1)S(1)}, bf16[4,192,128]{2,1,0:T(8,128)(2,1)S(1)}, u32[]{:S(2)}, u32[]{:S(2)}) %collective-permute-start.2) | collective-permute-done | bytes 196640 | tf_op jit(solution)/shard_map/ppermute | solution.py:115
  56.5 3.8 %collective-permute-done.4 = bf16[4,192,128]{2,1,0:T(8,128)(2,1)S(1)} collective-permute-done((bf16[4,192,128]{2,1,0:T(8,128)(2,1)S(1)}, bf16[4,192,128]{2,1,0:T(8,128)(2,1)S(1)}, u32[]{:S(2)}, u32[]{:S(2)}) %collective-permute-start.4) | collective-permute-done | bytes 196640 | tf_op jit(solution)/shard_map/ppermute | solution.py:115
  60.4 5.7 %collective-permute-done.6 = bf16[4,192,128]{2,1,0:T(8,128)(2,1)S(1)} collective-permute-done((bf16[4,192,128]{2,1,0:T(8,128)(2,1)S(1)}, bf16[4,192,128]{2,1,0:T(8,128)(2,1)S(1)}, u32[]{:S(2)}, u32[]{:S(2)}) %collective-permute-start.6) | collective-permute-done | bytes 196640 | tf_op jit(solution)/shard_map/ppermute | solution.py:115
  66.1 3.4 %collective-permute-start.7 = (bf16[32,192,128]{2,1,0:T(8,128)(2,1)S(1)}, bf16[32,192,128]{2,1,0:T(8,128)(2,1)}, u32[]{:S(2)}, u32[]{:S(2)}) collective-permute-start(bf16[32,192,128]{2,1,0:T(8,128)(2,1)S(1)} %constant_dynamic-update-slice_fusion.mine_ref), channel_id=1, source_target_pairs={{0,8},{8,0},{16,24},{24,16},{32,40},{40,32},{48,56},{56,48},{64,72... | collective-permute-start | bytes 4718600 | tf_op jit(solution)/shard_map/ppermute | solution.py:130
  72.4 7.2 %all-to-all-start.3 = ((bf16[32,2,32,2,128]{4,2,3,1,0:T(8,128)(2,1)}), bf16[32,2,32,2,128]{4,2,3,1,0:T(8,128)(2,1)S(1)}, u32[]{:S(2)}, u32[]{:S(2)}) async-start(bf16[32,2,32,2,128]{4,2,3,1,0:T(8,128)(2,1)} %bitcast.17), calls=%async_computation.3 | async-start | bytes 2097152 | tf_op jit(solution)/shard_map/all_to_all | solution.py:92
  81.4 15.3 %all-to-all-done.3 = bf16[32,2,32,2,128]{4,2,3,1,0:T(8,128)(2,1)S(1)} async-done(((bf16[32,2,32,2,128]{4,2,3,1,0:T(8,128)(2,1)}), bf16[32,2,32,2,128]{4,2,3,1,0:T(8,128)(2,1)S(1)}, u32[]{:S(2)}, u32[]{:S(2)}) %all-to-all-start.3) | async-done | bytes 1048608 | tf_op jit(solution)/shard_map/all_to_all | solution.py:92
  98.9 5.1 %shard_map.64 = f32[8,192,128]{2,1,0:T(8,128)} custom-call(s32[32]{0:T(128)} %fusion.18.pick_ref, s32[32]{0:T(128)} %compare_convert_fusion.src_ref, s32[32]{0:T(128)} %clamp_bitcast_fusion.row_ref, bf16[32,192,128]{2,1,0:T(8,128)(2,1)} %copy-done, bf16[32,192,128]{2,1,0:T(8,128)(2,1)} %collective-permute-done.7.other_ref, bf16[32,128,128]{2,1,0:T(8,128)(2,1)} %bitcast.91), custom_call_target="tpu_custom_call" | custom-call | tf_op jit(solution)/shard_map/pallas_call | solution.py:53
  107.2 3.9 %all-to-all-start.4 = ((f32[32,24,128]{2,1,0:T(8,128)}), f32[32,24,128]{2,1,0:T(8,128)S(1)}, u32[]{:S(2)}, u32[]{:S(2)}) async-start(f32[32,24,128]{2,1,0:T(8,128)} %reshape.96), calls=%async_computation.4 | async-start | bytes 786432 | tf_op jit(solution)/shard_map/all_to_all | solution.py:139
  112.2 9.1 %all-to-all-done.4 = f32[32,24,128]{2,1,0:T(8,128)S(1)} async-done(((f32[32,24,128]{2,1,0:T(8,128)}), f32[32,24,128]{2,1,0:T(8,128)S(1)}, u32[]{:S(2)}, u32[]{:S(2)}) %all-to-all-start.4) | async-done | bytes 393248 | tf_op jit(solution)/shard_map/all_to_all | solution.py:139
  123.9 11.7 %all_to_all.41 = bf16[32,24,128]{2,1,0:T(8,128)(2,1)S(1)} all-to-all(bf16[32,24,128]{2,1,0:T(8,128)(2,1)S(1)} %bitcast.103), channel_id=1, replica_groups=mesh['tm'=32,'state'=8] {'tm'}, dimensions={0} | all-to-all | bytes 393216 | tf_op jit(solution)/shard_map/all_to_all | solution.py:126
  138.6 4.8 %collective-permute-done.8 = bf16[4,192,128]{2,1,0:T(8,128)(2,1)S(1)} collective-permute-done((bf16[4,192,128]{2,1,0:T(8,128)(2,1)S(1)}, bf16[4,192,128]{2,1,0:T(8,128)(2,1)S(1)}, u32[]{:S(2)}, u32[]{:S(2)}) %collective-permute-start.8) | collective-permute-done | bytes 196640 | tf_op jit(solution)/shard_map/ppermute | solution.py:115
  146.2 3.9 %collective-permute-done.10 = bf16[4,192,128]{2,1,0:T(8,128)(2,1)S(1)} collective-permute-done((bf16[4,192,128]{2,1,0:T(8,128)(2,1)S(1)}, bf16[4,192,128]{2,1,0:T(8,128)(2,1)S(1)}, u32[]{:S(2)}, u32[]{:S(2)}) %collective-permute-start.10) | collective-permute-done | bytes 196640 | tf_op jit(solution)/shard_map/ppermute | solution.py:115
  152.8 3.0 %collective-permute-done.12 = bf16[4,192,128]{2,1,0:T(8,128)(2,1)S(1)} collective-permute-done((bf16[4,192,128]{2,1,0:T(8,128)(2,1)S(1)}, bf16[4,192,128]{2,1,0:T(8,128)(2,1)S(1)}, u32[]{:S(2)}, u32[]{:S(2)}) %collective-permute-start.12) | collective-permute-done | bytes 196640 | tf_op jit(solution)/shard_map/ppermute | solution.py:115
  155.9 5.7 %collective-permute-done.14 = bf16[4,192,128]{2,1,0:T(8,128)(2,1)S(1)} collective-permute-done((bf16[4,192,128]{2,1,0:T(8,128)(2,1)S(1)}, bf16[4,192,128]{2,1,0:T(8,128)(2,1)S(1)}, u32[]{:S(2)}, u32[]{:S(2)}) %collective-permute-start.14) | collective-permute-done | bytes 196640 | tf_op jit(solution)/shard_map/ppermute | solution.py:115
  161.6 4.3 %collective-permute-start.15 = (bf16[32,192,128]{2,1,0:T(8,128)(2,1)S(1)}, bf16[32,192,128]{2,1,0:T(8,128)(2,1)S(1)}, u32[]{:S(2)}, u32[]{:S(2)}) collective-permute-start(bf16[32,192,128]{2,1,0:T(8,128)(2,1)S(1)} %constant_dynamic-update-slice_fusion.8.mine_ref), channel_id=1, source_target_pairs={{0,8},{8,0},{16,24},{24,16},{32,40},{40,32},{48,56},{56,48},{64,72... | collective-permute-start | bytes 4718600 | tf_op jit(solution)/shard_map/ppermute | solution.py:130
  165.9 3.0 %collective-permute-done.15.other_ref = bf16[32,192,128]{2,1,0:T(8,128)(2,1)S(1)} collective-permute-done((bf16[32,192,128]{2,1,0:T(8,128)(2,1)S(1)}, bf16[32,192,128]{2,1,0:T(8,128)(2,1)S(1)}, u32[]{:S(2)}, u32[]{:S(2)}) %collective-permute-start.15) | collective-permute-done | bytes 1572896 | tf_op jit(solution)/shard_map/ppermute | solution.py:130
  170.0 5.1 %shard_map.65 = f32[8,192,128]{2,1,0:T(8,128)} custom-call(s32[32]{0:T(128)} %fusion.18.pick_ref, s32[32]{0:T(128)} %compare_convert_fusion.src_ref, s32[32]{0:T(128)} %clamp_bitcast_fusion.row_ref, bf16[32,192,128]{2,1,0:T(8,128)(2,1)} %copy-done.1, bf16[32,192,128]{2,1,0:T(8,128)(2,1)} %copy-done.2, bf16[32,128,128]{2,1,0:T(8,128)(2,1)} %bitcast.92), custom_call_target="tpu_custom_call" | custom-call | tf_op jit(solution)/shard_map/pallas_call | solution.py:53
  177.6 13.6 %all_to_all.42 = f32[32,24,128]{2,1,0:T(8,128)S(1)} all-to-all(f32[32,24,128]{2,1,0:T(8,128)S(1)} %reshape.103), channel_id=1, replica_groups=mesh['tm'=32,'state'=8] {'tm'}, dimensions={0} | all-to-all | bytes 786432 | tf_op jit(solution)/shard_map/all_to_all | solution.py:139
  193.3 13.7 %all_to_all.43 = f32[32,24,128]{2,1,0:T(8,128)S(1)} all-to-all(f32[32,24,128]{2,1,0:T(8,128)S(1)} %copy.60), channel_id=1, replica_groups=mesh['tm'=32,'state'=8] {'tm'}, dimensions={0} | all-to-all | bytes 786432 | tf_op jit(solution)/shard_map/all_to_all | solution.py:152
  (100 shorter events, 43.0 us)
Async XLA Ops:
  0.0 20.6 %copy-start.5 = (f32[32,32,1]{1,0,2:T(8,128)S(1)}, f32[32,32,1]{1,0,2:T(8,128)}, u32[]{:S(2)}) copy-start(f32[32,32,1]{1,0,2:T(8,128)} %constant.106) | copy-start | bytes 12292
  0.0 10.4 %copy-start.7 = (s32[2]{0:T(128)S(1)}, s32[2]{0:T(128)}, u32[]{:S(2)}) copy-start(s32[2]{0:T(128)} %param.9) | copy-start | bytes 28
  1.8 18.7 %all-to-all-start = ((f32[32,24,128]{2,1,0:T(8,128)}), f32[32,24,128]{2,1,0:T(8,128)S(1)}, u32[]{:S(2)}, u32[]{:S(2)}) async-start(f32[32,24,128]{2,1,0:T(8,128)} %reshape_squeeze.6), calls=%async_computation | async-start | bytes 786432 | tf_op jit(solution)/shard_map/all_to_all | solution.py:145
  10.4 29.0 %copy-start.3 = (bf16[32,1,128,128]{3,2,1,0:T(8,128)(2,1)S(1)}, bf16[32,1,128,128]{3,2,1,0:T(8,128)(2,1)}, u32[]{:S(2)}) copy-start(bf16[32,1,128,128]{3,2,1,0:T(8,128)(2,1)} %param.7) | copy-start | bytes 3145732
  33.9 12.4 %collective-permute-start = (bf16[4,192,128]{2,1,0:T(8,128)(2,1)}, bf16[4,192,128]{2,1,0:T(8,128)(2,1)S(1)}, u32[]{:S(2)}, u32[]{:S(2)}) collective-permute-start(bf16[4,192,128]{2,1,0:T(8,128)(2,1)} %get-tuple-element.11), channel_id=1, source_target_pairs={{0,1},{1,2},{2,3},{3,4},{4,5},{5,6},{6,7},{7,0},{8,9},{9,10},{10,1... | collective-permute-start | bytes 589832 | tf_op jit(solution)/shard_map/ppermute | solution.py:115
  35.5 10.9 %collective-permute-start.1 = (bf16[4,192,128]{2,1,0:T(8,128)(2,1)}, bf16[4,192,128]{2,1,0:T(8,128)(2,1)S(1)}, u32[]{:S(2)}, u32[]{:S(2)}) collective-permute-start(bf16[4,192,128]{2,1,0:T(8,128)(2,1)} %get-tuple-element.11), channel_id=1, source_target_pairs={{0,7},{1,0},{2,1},{3,2},{4,3},{5,4},{6,5},{7,6},{8,15},{9,8},{10,9... | collective-permute-start | bytes 589832 | tf_op jit(solution)/shard_map/ppermute | solution.py:118
  42.2 27.3 %all-to-all-start.2 = ((bf16[32,32,2,2,128]{4,3,2,1,0:T(2,128)(2,1)}), bf16[32,32,2,2,128]{4,3,2,1,0:T(2,128)(2,1)S(1)}, u32[]{:S(2)}, u32[]{:S(2)}) async-start(bf16[32,32,2,2,128]{4,3,2,1,0:T(2,128)(2,1)} %copy.41), calls=%async_computation.2 | async-start | bytes 2097152 | tf_op jit(solution)/shard_map/all_to_all | solution.py:87
  46.3 23.2 %copy-start.6 = (f32[2,16,32,1,1,1]{2,1,5,4,3,0:T(8,128)S(1)}, f32[2,16,32,1,1,1]{2,1,5,4,3,0:T(8,128)}, u32[]{:S(2)}) copy-start(f32[2,16,32,1,1,1]{2,1,5,4,3,0:T(8,128)} %constant.107) | copy-start | bytes 12292
  46.3 7.5 %collective-permute-start.2 = (bf16[4,192,128]{2,1,0:T(8,128)(2,1)S(1)}, bf16[4,192,128]{2,1,0:T(8,128)(2,1)S(1)}, u32[]{:S(2)}, u32[]{:S(2)}) collective-permute-start(bf16[4,192,128]{2,1,0:T(8,128)(2,1)S(1)} %collective-permute-done), channel_id=1, source_target_pairs={{0,1},{1,2},{2,3},{3,4},{4,5},{5,6},{6,7},{7,0},{8,9},{9,10},{10,1... | collective-permute-start | bytes 589832 | tf_op jit(solution)/shard_map/ppermute | solution.py:115
  46.4 7.4 %collective-permute-start.3 = (bf16[4,192,128]{2,1,0:T(8,128)(2,1)S(1)}, bf16[4,192,128]{2,1,0:T(8,128)(2,1)S(1)}, u32[]{:S(2)}, u32[]{:S(2)}) collective-permute-start(bf16[4,192,128]{2,1,0:T(8,128)(2,1)S(1)} %collective-permute-done.1), channel_id=1, source_target_pairs={{0,7},{1,0},{2,1},{3,2},{4,3},{5,4},{6,5},{7,6},{8,15},{9,8},{10,9... | collective-permute-start | bytes 589832 | tf_op jit(solution)/shard_map/ppermute | solution.py:118
  53.8 6.5 %collective-permute-start.4 = (bf16[4,192,128]{2,1,0:T(8,128)(2,1)S(1)}, bf16[4,192,128]{2,1,0:T(8,128)(2,1)S(1)}, u32[]{:S(2)}, u32[]{:S(2)}) collective-permute-start(bf16[4,192,128]{2,1,0:T(8,128)(2,1)S(1)} %collective-permute-done.2), channel_id=1, source_target_pairs={{0,1},{1,2},{2,3},{3,4},{4,5},{5,6},{6,7},{7,0},{8,9},{9,10},{10,1... | collective-permute-start | bytes 589832 | tf_op jit(solution)/shard_map/ppermute | solution.py:115
  53.8 6.6 %collective-permute-start.5 = (bf16[4,192,128]{2,1,0:T(8,128)(2,1)S(1)}, bf16[4,192,128]{2,1,0:T(8,128)(2,1)S(1)}, u32[]{:S(2)}, u32[]{:S(2)}) collective-permute-start(bf16[4,192,128]{2,1,0:T(8,128)(2,1)S(1)} %collective-permute-done.3), channel_id=1, source_target_pairs={{0,7},{1,0},{2,1},{3,2},{4,3},{5,4},{6,5},{7,6},{8,15},{9,8},{10,9... | collective-permute-start | bytes 589832 | tf_op jit(solution)/shard_map/ppermute | solution.py:118
  60.3 5.7 %collective-permute-start.6 = (bf16[4,192,128]{2,1,0:T(8,128)(2,1)S(1)}, bf16[4,192,128]{2,1,0:T(8,128)(2,1)S(1)}, u32[]{:S(2)}, u32[]{:S(2)}) collective-permute-start(bf16[4,192,128]{2,1,0:T(8,128)(2,1)S(1)} %collective-permute-done.4), channel_id=1, source_target_pairs={{0,1},{1,2},{2,3},{3,4},{4,5},{5,6},{6,7},{7,0},{8,9},{9,10},{10,1... | collective-permute-start | bytes 589832 | tf_op jit(solution)/shard_map/ppermute | solution.py:115
  66.1 32.8 %collective-permute-start.7 = (bf16[32,192,128]{2,1,0:T(8,128)(2,1)S(1)}, bf16[32,192,128]{2,1,0:T(8,128)(2,1)}, u32[]{:S(2)}, u32[]{:S(2)}) collective-permute-start(bf16[32,192,128]{2,1,0:T(8,128)(2,1)S(1)} %constant_dynamic-update-slice_fusion.mine_ref), channel_id=1, source_target_pairs={{0,8},{8,0},{16,24},{24,16},{32,40},{40,32},{48,56},{56,48},{64,72... | collective-permute-start | bytes 4718600 | tf_op jit(solution)/shard_map/ppermute | solution.py:130
  72.4 24.3 %all-to-all-start.3 = ((bf16[32,2,32,2,128]{4,2,3,1,0:T(8,128)(2,1)}), bf16[32,2,32,2,128]{4,2,3,1,0:T(8,128)(2,1)S(1)}, u32[]{:S(2)}, u32[]{:S(2)}) async-start(bf16[32,2,32,2,128]{4,2,3,1,0:T(8,128)(2,1)} %bitcast.17), calls=%async_computation.3 | async-start | bytes 2097152 | tf_op jit(solution)/shard_map/all_to_all | solution.py:92
  107.2 14.2 %all-to-all-start.4 = ((f32[32,24,128]{2,1,0:T(8,128)}), f32[32,24,128]{2,1,0:T(8,128)S(1)}, u32[]{:S(2)}, u32[]{:S(2)}) async-start(f32[32,24,128]{2,1,0:T(8,128)} %reshape.96), calls=%async_computation.4 | async-start | bytes 786432 | tf_op jit(solution)/shard_map/all_to_all | solution.py:139
  135.8 7.6 %collective-permute-start.8 = (bf16[4,192,128]{2,1,0:T(8,128)(2,1)S(1)}, bf16[4,192,128]{2,1,0:T(8,128)(2,1)S(1)}, u32[]{:S(2)}, u32[]{:S(2)}) collective-permute-start(bf16[4,192,128]{2,1,0:T(8,128)(2,1)S(1)} %get-tuple-element.9), channel_id=1, source_target_pairs={{0,1},{1,2},{2,3},{3,4},{4,5},{5,6},{6,7},{7,0},{8,9},{9,10},{10,1... | collective-permute-start | bytes 589832 | tf_op jit(solution)/shard_map/ppermute | solution.py:115
  135.9 7.5 %collective-permute-start.9 = (bf16[4,192,128]{2,1,0:T(8,128)(2,1)S(1)}, bf16[4,192,128]{2,1,0:T(8,128)(2,1)S(1)}, u32[]{:S(2)}, u32[]{:S(2)}) collective-permute-start(bf16[4,192,128]{2,1,0:T(8,128)(2,1)S(1)} %get-tuple-element.9), channel_id=1, source_target_pairs={{0,7},{1,0},{2,1},{3,2},{4,3},{5,4},{6,5},{7,6},{8,15},{9,8},{10,9... | collective-permute-start | bytes 589832 | tf_op jit(solution)/shard_map/ppermute | solution.py:118
  143.4 6.7 %collective-permute-start.10 = (bf16[4,192,128]{2,1,0:T(8,128)(2,1)S(1)}, bf16[4,192,128]{2,1,0:T(8,128)(2,1)S(1)}, u32[]{:S(2)}, u32[]{:S(2)}) collective-permute-start(bf16[4,192,128]{2,1,0:T(8,128)(2,1)S(1)} %collective-permute-done.8), channel_id=1, source_target_pairs={{0,1},{1,2},{2,3},{3,4},{4,5},{5,6},{6,7},{7,0},{8,9},{9,10},{10,1... | collective-permute-start | bytes 589832 | tf_op jit(solution)/shard_map/ppermute | solution.py:115
  143.4 6.7 %collective-permute-start.11 = (bf16[4,192,128]{2,1,0:T(8,128)(2,1)S(1)}, bf16[4,192,128]{2,1,0:T(8,128)(2,1)S(1)}, u32[]{:S(2)}, u32[]{:S(2)}) collective-permute-start(bf16[4,192,128]{2,1,0:T(8,128)(2,1)S(1)} %collective-permute-done.9), channel_id=1, source_target_pairs={{0,7},{1,0},{2,1},{3,2},{4,3},{5,4},{6,5},{7,6},{8,15},{9,8},{10,9... | collective-permute-start | bytes 589832 | tf_op jit(solution)/shard_map/ppermute | solution.py:118
  150.1 5.7 %collective-permute-start.12 = (bf16[4,192,128]{2,1,0:T(8,128)(2,1)S(1)}, bf16[4,192,128]{2,1,0:T(8,128)(2,1)S(1)}, u32[]{:S(2)}, u32[]{:S(2)}) collective-permute-start(bf16[4,192,128]{2,1,0:T(8,128)(2,1)S(1)} %collective-permute-done.10), channel_id=1, source_target_pairs={{0,1},{1,2},{2,3},{3,4},{4,5},{5,6},{6,7},{7,0},{8,9},{9,10},{10,1... | collective-permute-start | bytes 589832 | tf_op jit(solution)/shard_map/ppermute | solution.py:115
  150.1 5.8 %collective-permute-start.13 = (bf16[4,192,128]{2,1,0:T(8,128)(2,1)S(1)}, bf16[4,192,128]{2,1,0:T(8,128)(2,1)S(1)}, u32[]{:S(2)}, u32[]{:S(2)}) collective-permute-start(bf16[4,192,128]{2,1,0:T(8,128)(2,1)S(1)} %collective-permute-done.11), channel_id=1, source_target_pairs={{0,7},{1,0},{2,1},{3,2},{4,3},{5,4},{6,5},{7,6},{8,15},{9,8},{10,9... | collective-permute-start | bytes 589832 | tf_op jit(solution)/shard_map/ppermute | solution.py:118
  155.8 5.7 %collective-permute-start.14 = (bf16[4,192,128]{2,1,0:T(8,128)(2,1)S(1)}, bf16[4,192,128]{2,1,0:T(8,128)(2,1)S(1)}, u32[]{:S(2)}, u32[]{:S(2)}) collective-permute-start(bf16[4,192,128]{2,1,0:T(8,128)(2,1)S(1)} %collective-permute-done.12), channel_id=1, source_target_pairs={{0,1},{1,2},{2,3},{3,4},{4,5},{5,6},{6,7},{7,0},{8,9},{9,10},{10,1... | collective-permute-start | bytes 589832 | tf_op jit(solution)/shard_map/ppermute | solution.py:115
  161.6 7.3 %collective-permute-start.15 = (bf16[32,192,128]{2,1,0:T(8,128)(2,1)S(1)}, bf16[32,192,128]{2,1,0:T(8,128)(2,1)S(1)}, u32[]{:S(2)}, u32[]{:S(2)}) collective-permute-start(bf16[32,192,128]{2,1,0:T(8,128)(2,1)S(1)} %constant_dynamic-update-slice_fusion.8.mine_ref), channel_id=1, source_target_pairs={{0,8},{8,0},{16,24},{24,16},{32,40},{40,32},{48,56},{56,48},{64,72... | collective-permute-start | bytes 4718600 | tf_op jit(solution)/shard_map/ppermute | solution.py:130
  (6 other events, 23.8 us)

commit v5 on v4

--- a/solution.py
+++ b/solution.py
@@ -43,7 +43,7 @@
         out_ref[r] = out_ref[r] + prod
         return carry
 
-    lax.fori_loop(0, kk_ref.shape[0], step, 0, unroll=8)
+    lax.fori_loop(0, kk_ref.shape[0], step, 0, unroll=16)
 
 
 def block_products(pick, src, row, mine, other, kk, rows_local):
@@ -82,16 +82,19 @@
     my_half = me % per_slot
     swap = [(i, i ^ 1) for i in range(ntm)]
 
-    ksrc = kernel[:, 0].reshape(nnz, per_slot, ntm, block // (per_slot * ntm), block)
-    ksrc = jnp.transpose(ksrc, (2, 0, 1, 3, 4))
+    rows_dev = block // (per_slot * ntm)
+    ksrc = kernel[:, 0].reshape(nnz, per_slot, ntm, rows_dev, block)
+    ksrc = jnp.transpose(ksrc, (2, 1, 0, 3, 4)).reshape(ntm, -1, block)
     klags = lax.all_to_all(ksrc, "tm", 0, 0, tiled=True).astype(jnp.float32)
+    klags = klags.reshape(length, per_slot, nnz * rows_dev, block)
     kspec = jnp.einsum(
-        "xqt,tkhij->qhxkij", fwd_table.reshape(2, half, length), klags, precision=HIGH
+        "xqt,thrj->qhxrj", fwd_table.reshape(2, half, length), klags, precision=HIGH
     ).astype(jnp.bfloat16)
-    kspec = kspec.reshape(ntm, 2, nnz, block // (per_slot * ntm), block)
+    kspec = kspec.reshape(ntm, -1, block)
     kspec = lax.all_to_all(kspec, "tm", 0, 0, tiled=True)
+    kspec = kspec.reshape(ntm, 2, nnz, rows_dev, block)
+    kk = jnp.transpose(kspec, (2, 1, 0, 3, 4)).reshape(nnz, block, block)
     local_rows = pattern[:, 0] - my_state * rows_local
-    kk = jnp.transpose(kspec, (2, 1, 0, 3, 4)).reshape(nnz, block, block)
     row_of = jnp.clip(local_rows, 0, rows_local - 1)
     real_slot = (my_slot != 0).astype(jnp.float32)
 

time: 208 us -> 208 us (level)
    another operation x0 -> x1, local copies, waits for them, and re-layouts: none -> 2.17 us  [shards(): ksrc = kernel[:, 0].reshape(nnz, per_slot, ntm, rows_dev, block)]
where the time goes in v5:
time: 208 us; the launch traced here: 207 us
  waiting for transfers between devices  67.8 us (33%)
  blocking collectives  50.8 us (24%)
  starting transfers between devices  50.4 us (24%)
  local copies, waits for them, and re-layouts  17.9 us (9%)
  Pallas kernels  9.58 us (5%)
  other arithmetic  6.9 us (3%)
  matrix products  3.06 us (1%)
    ppermute x8, waiting for transfers between devices, ring_gather(): a = lax.ppermute(a, 'state', fwd)  31.4 us
    all_to_all x2, blocking collectives, respond(): xs = lax.all_to_all(xs, 'tm', 0, 0, tiled=True)  23.5 us
    ppermute x6, starting transfers between devices, ring_gather(): b = lax.ppermute(b, 'state', bwd)  17.3 us
    all_to_all x1, waiting for transfers between devices, shards(): kspec = lax.all_to_all(kspec, 'tm', 0, 0, tiled=True)  15.3 us
    all_to_all x1, blocking collectives, shards(): field = lax.all_to_all(field, 'tm', 0, 0, tiled=True)  13.7 us
    all_to_all x1, blocking collectives, respond(): ys = lax.all_to_all(ys, 'tm', 0, 0, tiled=True)  13.6 us
    pallas_call x2, Pallas kernels, block_products(): pl.pallas_call(_products_body, grid_spec=pltpu.PrefetchScalarGridSpec(num...  9.58 us
    all_to_all x1, waiting for transfers between devices, respond(): ys = lax.all_to_all(ys, 'tm', 0, 0, tiled=True)  9.1 us
  transfers between devices with their start and end apart: 20, of which 11 were waited for; matrix products, arithmetic and copies ran while one was open for 6% of the time, Pallas kernels for 0%

profile of v5, /device:TPU:1, one launch (start us, length us, event | category | flops | bytes accessed | tf_op | source)
XLA Modules:
  0.0 207.0 jit_solution(8502986006519635039)
XLA Ops:
  1.8 8.6 %all-to-all-start = ((f32[32,24,128]{2,1,0:T(8,128)}), f32[32,24,128]{2,1,0:T(8,128)S(1)}, u32[]{:S(2)}, u32[]{:S(2)}) async-start(f32[32,24,128]{2,1,0:T(8,128)} %reshape_squeeze.6), calls=%async_computation | async-start | bytes 786432 | tf_op jit(solution)/shard_map/all_to_all | solution.py:148
  11.7 8.9 %all-to-all-done = f32[32,24,128]{2,1,0:T(8,128)S(1)} async-done(((f32[32,24,128]{2,1,0:T(8,128)}), f32[32,24,128]{2,1,0:T(8,128)S(1)}, u32[]{:S(2)}, u32[]{:S(2)}) %all-to-all-start) | async-done | bytes 393248 | tf_op jit(solution)/shard_map/all_to_all | solution.py:148
  21.3 11.7 %all_to_all.40 = bf16[32,24,128]{2,1,0:T(8,128)(2,1)S(1)} all-to-all(bf16[32,24,128]{2,1,0:T(8,128)(2,1)S(1)} %bitcast.106), channel_id=1, replica_groups=mesh['tm'=32,'state'=8] {'tm'}, dimensions={0} | all-to-all | bytes 393216 | tf_op jit(solution)/shard_map/all_to_all | solution.py:129
  35.5 3.9 %collective-permute-start.1 = (bf16[4,192,128]{2,1,0:T(8,128)(2,1)}, bf16[4,192,128]{2,1,0:T(8,128)(2,1)S(1)}, u32[]{:S(2)}, u32[]{:S(2)}) collective-permute-start(bf16[4,192,128]{2,1,0:T(8,128)(2,1)} %get-tuple-element.11), channel_id=1, source_target_pairs={{0,7},{1,0},{2,1},{3,2},{4,3},{5,4},{6,5},{7,6},{8,15},{9,8},{10,9... | collective-permute-start | bytes 589832 | tf_op jit(solution)/shard_map/ppermute | solution.py:121
  41.6 4.1 %all-to-all-start.2 = ((bf16[32,128,128]{2,1,0:T(8,128)(2,1)}), bf16[32,128,128]{2,1,0:T(8,128)(2,1)S(1)}, u32[]{:S(2)}, u32[]{:S(2)}) async-start(bf16[32,128,128]{2,1,0:T(8,128)(2,1)} %bitcast.15), calls=%async_computation.2 | async-start | bytes 2097152 | tf_op jit(solution)/shard_map/all_to_all | solution.py:88
  48.6 4.6 %collective-permute-done.2 = bf16[4,192,128]{2,1,0:T(8,128)(2,1)S(1)} collective-permute-done((bf16[4,192,128]{2,1,0:T(8,128)(2,1)S(1)}, bf16[4,192,128]{2,1,0:T(8,128)(2,1)S(1)}, u32[]{:S(2)}, u32[]{:S(2)}) %collective-permute-start.2) | collective-permute-done | bytes 196640 | tf_op jit(solution)/shard_map/ppermute | solution.py:118
  55.9 3.8 %collective-permute-done.4 = bf16[4,192,128]{2,1,0:T(8,128)(2,1)S(1)} collective-permute-done((bf16[4,192,128]{2,1,0:T(8,128)(2,1)S(1)}, bf16[4,192,128]{2,1,0:T(8,128)(2,1)S(1)}, u32[]{:S(2)}, u32[]{:S(2)}) %collective-permute-start.4) | collective-permute-done | bytes 196640 | tf_op jit(solution)/shard_map/ppermute | solution.py:118
  59.8 5.7 %collective-permute-done.6 = bf16[4,192,128]{2,1,0:T(8,128)(2,1)S(1)} collective-permute-done((bf16[4,192,128]{2,1,0:T(8,128)(2,1)S(1)}, bf16[4,192,128]{2,1,0:T(8,128)(2,1)S(1)}, u32[]{:S(2)}, u32[]{:S(2)}) %collective-permute-start.6) | collective-permute-done | bytes 196640 | tf_op jit(solution)/shard_map/ppermute | solution.py:118
  65.5 3.2 %collective-permute-start.7 = (bf16[32,192,128]{2,1,0:T(8,128)(2,1)S(1)}, bf16[32,192,128]{2,1,0:T(8,128)(2,1)}, u32[]{:S(2)}, u32[]{:S(2)}) collective-permute-start(bf16[32,192,128]{2,1,0:T(8,128)(2,1)S(1)} %constant_dynamic-update-slice_fusion.mine_ref), channel_id=1, source_target_pairs={{0,8},{8,0},{16,24},{24,16},{32,40},{40,32},{48,56},{56,48},{64,72... | collective-permute-start | bytes 4718600 | tf_op jit(solution)/shard_map/ppermute | solution.py:133
  71.7 7.2 %all-to-all-start.3 = ((bf16[32,128,128]{2,1,0:T(8,128)(2,1)}), bf16[32,128,128]{2,1,0:T(8,128)(2,1)S(1)}, u32[]{:S(2)}, u32[]{:S(2)}) async-start(bf16[32,128,128]{2,1,0:T(8,128)(2,1)} %bitcast.19), calls=%async_computation.3 | async-start | bytes 2097152 | tf_op jit(solution)/shard_map/all_to_all | solution.py:94
  80.6 15.3 %all-to-all-done.3 = bf16[32,128,128]{2,1,0:T(8,128)(2,1)S(1)} async-done(((bf16[32,128,128]{2,1,0:T(8,128)(2,1)}), bf16[32,128,128]{2,1,0:T(8,128)(2,1)S(1)}, u32[]{:S(2)}, u32[]{:S(2)}) %all-to-all-start.3) | async-done | bytes 1048608 | tf_op jit(solution)/shard_map/all_to_all | solution.py:94
  98.7 4.8 %shard_map.64 = f32[8,192,128]{2,1,0:T(8,128)} custom-call(s32[32]{0:T(128)} %fusion.16.pick_ref, s32[32]{0:T(128)} %compare_convert_fusion.src_ref, s32[32]{0:T(128)} %clamp_bitcast_fusion.row_ref, bf16[32,192,128]{2,1,0:T(8,128)(2,1)} %copy-done, bf16[32,192,128]{2,1,0:T(8,128)(2,1)} %collective-permute-done.7.other_ref, bf16[32,128,128]{2,1,0:T(8,128)(2,1)} %bitcast.95), custom_call_target="tpu_custom_call" | custom-call | tf_op jit(solution)/shard_map/pallas_call | solution.py:53
  106.7 3.9 %all-to-all-start.4 = ((f32[32,24,128]{2,1,0:T(8,128)}), f32[32,24,128]{2,1,0:T(8,128)S(1)}, u32[]{:S(2)}, u32[]{:S(2)}) async-start(f32[32,24,128]{2,1,0:T(8,128)} %reshape.108), calls=%async_computation.4 | async-start | bytes 786432 | tf_op jit(solution)/shard_map/all_to_all | solution.py:142
  111.8 9.1 %all-to-all-done.4 = f32[32,24,128]{2,1,0:T(8,128)S(1)} async-done(((f32[32,24,128]{2,1,0:T(8,128)}), f32[32,24,128]{2,1,0:T(8,128)S(1)}, u32[]{:S(2)}, u32[]{:S(2)}) %all-to-all-start.4) | async-done | bytes 393248 | tf_op jit(solution)/shard_map/all_to_all | solution.py:142
  123.5 11.7 %all_to_all.41 = bf16[32,24,128]{2,1,0:T(8,128)(2,1)S(1)} all-to-all(bf16[32,24,128]{2,1,0:T(8,128)(2,1)S(1)} %bitcast.108), channel_id=1, replica_groups=mesh['tm'=32,'state'=8] {'tm'}, dimensions={0} | all-to-all | bytes 393216 | tf_op jit(solution)/shard_map/all_to_all | solution.py:129
  138.2 4.8 %collective-permute-done.8 = bf16[4,192,128]{2,1,0:T(8,128)(2,1)S(1)} collective-permute-done((bf16[4,192,128]{2,1,0:T(8,128)(2,1)S(1)}, bf16[4,192,128]{2,1,0:T(8,128)(2,1)S(1)}, u32[]{:S(2)}, u32[]{:S(2)}) %collective-permute-start.8) | collective-permute-done | bytes 196640 | tf_op jit(solution)/shard_map/ppermute | solution.py:118
  145.7 3.9 %collective-permute-done.10 = bf16[4,192,128]{2,1,0:T(8,128)(2,1)S(1)} collective-permute-done((bf16[4,192,128]{2,1,0:T(8,128)(2,1)S(1)}, bf16[4,192,128]{2,1,0:T(8,128)(2,1)S(1)}, u32[]{:S(2)}, u32[]{:S(2)}) %collective-permute-start.10) | collective-permute-done | bytes 196640 | tf_op jit(solution)/shard_map/ppermute | solution.py:118
  152.4 3.0 %collective-permute-done.12 = bf16[4,192,128]{2,1,0:T(8,128)(2,1)S(1)} collective-permute-done((bf16[4,192,128]{2,1,0:T(8,128)(2,1)S(1)}, bf16[4,192,128]{2,1,0:T(8,128)(2,1)S(1)}, u32[]{:S(2)}, u32[]{:S(2)}) %collective-permute-start.12) | collective-permute-done | bytes 196640 | tf_op jit(solution)/shard_map/ppermute | solution.py:118
  155.5 5.7 %collective-permute-done.14 = bf16[4,192,128]{2,1,0:T(8,128)(2,1)S(1)} collective-permute-done((bf16[4,192,128]{2,1,0:T(8,128)(2,1)S(1)}, bf16[4,192,128]{2,1,0:T(8,128)(2,1)S(1)}, u32[]{:S(2)}, u32[]{:S(2)}) %collective-permute-start.14) | collective-permute-done | bytes 196640 | tf_op jit(solution)/shard_map/ppermute | solution.py:118
  161.1 4.3 %collective-permute-start.15 = (bf16[32,192,128]{2,1,0:T(8,128)(2,1)S(1)}, bf16[32,192,128]{2,1,0:T(8,128)(2,1)S(1)}, u32[]{:S(2)}, u32[]{:S(2)}) collective-permute-start(bf16[32,192,128]{2,1,0:T(8,128)(2,1)S(1)} %constant_dynamic-update-slice_fusion.8.mine_ref), channel_id=1, source_target_pairs={{0,8},{8,0},{16,24},{24,16},{32,40},{40,32},{48,56},{56,48},{64,72... | collective-permute-start | bytes 4718600 | tf_op jit(solution)/shard_map/ppermute | solution.py:133
  165.4 3.0 %collective-permute-done.15.other_ref = bf16[32,192,128]{2,1,0:T(8,128)(2,1)S(1)} collective-permute-done((bf16[32,192,128]{2,1,0:T(8,128)(2,1)S(1)}, bf16[32,192,128]{2,1,0:T(8,128)(2,1)S(1)}, u32[]{:S(2)}, u32[]{:S(2)}) %collective-permute-start.15) | collective-permute-done | bytes 1572896 | tf_op jit(solution)/shard_map/ppermute | solution.py:133
  169.6 4.8 %shard_map.65 = f32[8,192,128]{2,1,0:T(8,128)} custom-call(s32[32]{0:T(128)} %fusion.16.pick_ref, s32[32]{0:T(128)} %compare_convert_fusion.src_ref, s32[32]{0:T(128)} %clamp_bitcast_fusion.row_ref, bf16[32,192,128]{2,1,0:T(8,128)(2,1)} %copy-done.1, bf16[32,192,128]{2,1,0:T(8,128)(2,1)} %copy-done.2, bf16[32,128,128]{2,1,0:T(8,128)(2,1)} %bitcast.96), custom_call_target="tpu_custom_call" | custom-call | tf_op jit(solution)/shard_map/pallas_call | solution.py:53
  176.8 13.6 %all_to_all.42 = f32[32,24,128]{2,1,0:T(8,128)S(1)} all-to-all(f32[32,24,128]{2,1,0:T(8,128)S(1)} %reshape.115), channel_id=1, replica_groups=mesh['tm'=32,'state'=8] {'tm'}, dimensions={0} | all-to-all | bytes 786432 | tf_op jit(solution)/shard_map/all_to_all | solution.py:142
  192.5 13.7 %all_to_all.43 = f32[32,24,128]{2,1,0:T(8,128)S(1)} all-to-all(f32[32,24,128]{2,1,0:T(8,128)S(1)} %copy.61), channel_id=1, replica_groups=mesh['tm'=32,'state'=8] {'tm'}, dimensions={0} | all-to-all | bytes 786432 | tf_op jit(solution)/shard_map/all_to_all | solution.py:155
  (101 shorter events, 43.1 us)
Async XLA Ops:
  0.0 20.6 %copy-start.5 = (f32[32,32,1]{1,0,2:T(8,128)S(1)}, f32[32,32,1]{1,0,2:T(8,128)}, u32[]{:S(2)}) copy-start(f32[32,32,1]{1,0,2:T(8,128)} %constant.106) | copy-start | bytes 12292
  0.0 10.4 %copy-start.7 = (s32[2]{0:T(128)S(1)}, s32[2]{0:T(128)}, u32[]{:S(2)}) copy-start(s32[2]{0:T(128)} %param.9) | copy-start | bytes 28
  1.8 18.7 %all-to-all-start = ((f32[32,24,128]{2,1,0:T(8,128)}), f32[32,24,128]{2,1,0:T(8,128)S(1)}, u32[]{:S(2)}, u32[]{:S(2)}) async-start(f32[32,24,128]{2,1,0:T(8,128)} %reshape_squeeze.6), calls=%async_computation | async-start | bytes 786432 | tf_op jit(solution)/shard_map/all_to_all | solution.py:148
  10.4 29.0 %copy-start.3 = (bf16[32,1,128,128]{3,2,1,0:T(8,128)(2,1)S(1)}, bf16[32,1,128,128]{3,2,1,0:T(8,128)(2,1)}, u32[]{:S(2)}) copy-start(bf16[32,1,128,128]{3,2,1,0:T(8,128)(2,1)} %param.7) | copy-start | bytes 3145732
  33.9 11.8 %collective-permute-start = (bf16[4,192,128]{2,1,0:T(8,128)(2,1)}, bf16[4,192,128]{2,1,0:T(8,128)(2,1)S(1)}, u32[]{:S(2)}, u32[]{:S(2)}) collective-permute-start(bf16[4,192,128]{2,1,0:T(8,128)(2,1)} %get-tuple-element.11), channel_id=1, source_target_pairs={{0,1},{1,2},{2,3},{3,4},{4,5},{5,6},{6,7},{7,0},{8,9},{9,10},{10,1... | collective-permute-start | bytes 589832 | tf_op jit(solution)/shard_map/ppermute | solution.py:118
  35.5 10.3 %collective-permute-start.1 = (bf16[4,192,128]{2,1,0:T(8,128)(2,1)}, bf16[4,192,128]{2,1,0:T(8,128)(2,1)S(1)}, u32[]{:S(2)}, u32[]{:S(2)}) collective-permute-start(bf16[4,192,128]{2,1,0:T(8,128)(2,1)} %get-tuple-element.11), channel_id=1, source_target_pairs={{0,7},{1,0},{2,1},{3,2},{4,3},{5,4},{6,5},{7,6},{8,15},{9,8},{10,9... | collective-permute-start | bytes 589832 | tf_op jit(solution)/shard_map/ppermute | solution.py:121
  41.6 27.1 %all-to-all-start.2 = ((bf16[32,128,128]{2,1,0:T(8,128)(2,1)}), bf16[32,128,128]{2,1,0:T(8,128)(2,1)S(1)}, u32[]{:S(2)}, u32[]{:S(2)}) async-start(bf16[32,128,128]{2,1,0:T(8,128)(2,1)} %bitcast.15), calls=%async_computation.2 | async-start | bytes 2097152 | tf_op jit(solution)/shard_map/all_to_all | solution.py:88
  45.7 7.5 %collective-permute-start.2 = (bf16[4,192,128]{2,1,0:T(8,128)(2,1)S(1)}, bf16[4,192,128]{2,1,0:T(8,128)(2,1)S(1)}, u32[]{:S(2)}, u32[]{:S(2)}) collective-permute-start(bf16[4,192,128]{2,1,0:T(8,128)(2,1)S(1)} %collective-permute-done), channel_id=1, source_target_pairs={{0,1},{1,2},{2,3},{3,4},{4,5},{5,6},{6,7},{7,0},{8,9},{9,10},{10,1... | collective-permute-start | bytes 589832 | tf_op jit(solution)/shard_map/ppermute | solution.py:118
  45.8 7.4 %collective-permute-start.3 = (bf16[4,192,128]{2,1,0:T(8,128)(2,1)S(1)}, bf16[4,192,128]{2,1,0:T(8,128)(2,1)S(1)}, u32[]{:S(2)}, u32[]{:S(2)}) collective-permute-start(bf16[4,192,128]{2,1,0:T(8,128)(2,1)S(1)} %collective-permute-done.1), channel_id=1, source_target_pairs={{0,7},{1,0},{2,1},{3,2},{4,3},{5,4},{6,5},{7,6},{8,15},{9,8},{10,9... | collective-permute-start | bytes 589832 | tf_op jit(solution)/shard_map/ppermute | solution.py:121
  53.2 6.5 %collective-permute-start.4 = (bf16[4,192,128]{2,1,0:T(8,128)(2,1)S(1)}, bf16[4,192,128]{2,1,0:T(8,128)(2,1)S(1)}, u32[]{:S(2)}, u32[]{:S(2)}) collective-permute-start(bf16[4,192,128]{2,1,0:T(8,128)(2,1)S(1)} %collective-permute-done.2), channel_id=1, source_target_pairs={{0,1},{1,2},{2,3},{3,4},{4,5},{5,6},{6,7},{7,0},{8,9},{9,10},{10,1... | collective-permute-start | bytes 589832 | tf_op jit(solution)/shard_map/ppermute | solution.py:118
  53.2 6.6 %collective-permute-start.5 = (bf16[4,192,128]{2,1,0:T(8,128)(2,1)S(1)}, bf16[4,192,128]{2,1,0:T(8,128)(2,1)S(1)}, u32[]{:S(2)}, u32[]{:S(2)}) collective-permute-start(bf16[4,192,128]{2,1,0:T(8,128)(2,1)S(1)} %collective-permute-done.3), channel_id=1, source_target_pairs={{0,7},{1,0},{2,1},{3,2},{4,3},{5,4},{6,5},{7,6},{8,15},{9,8},{10,9... | collective-permute-start | bytes 589832 | tf_op jit(solution)/shard_map/ppermute | solution.py:121
  55.9 13.5 %copy-start.6 = (f32[2,16,32,1,1]{2,1,4,3,0:T(8,128)S(1)}, f32[2,16,32,1,1]{2,1,4,3,0:T(8,128)}, u32[]{:S(2)}) copy-start(f32[2,16,32,1,1]{2,1,4,3,0:T(8,128)} %constant.107) | copy-start | bytes 12292
  59.7 5.7 %collective-permute-start.6 = (bf16[4,192,128]{2,1,0:T(8,128)(2,1)S(1)}, bf16[4,192,128]{2,1,0:T(8,128)(2,1)S(1)}, u32[]{:S(2)}, u32[]{:S(2)}) collective-permute-start(bf16[4,192,128]{2,1,0:T(8,128)(2,1)S(1)} %collective-permute-done.4), channel_id=1, source_target_pairs={{0,1},{1,2},{2,3},{3,4},{4,5},{5,6},{6,7},{7,0},{8,9},{9,10},{10,1... | collective-permute-start | bytes 589832 | tf_op jit(solution)/shard_map/ppermute | solution.py:118
  65.5 33.2 %collective-permute-start.7 = (bf16[32,192,128]{2,1,0:T(8,128)(2,1)S(1)}, bf16[32,192,128]{2,1,0:T(8,128)(2,1)}, u32[]{:S(2)}, u32[]{:S(2)}) collective-permute-start(bf16[32,192,128]{2,1,0:T(8,128)(2,1)S(1)} %constant_dynamic-update-slice_fusion.mine_ref), channel_id=1, source_target_pairs={{0,8},{8,0},{16,24},{24,16},{32,40},{40,32},{48,56},{56,48},{64,72... | collective-permute-start | bytes 4718600 | tf_op jit(solution)/shard_map/ppermute | solution.py:133
  71.7 24.2 %all-to-all-start.3 = ((bf16[32,128,128]{2,1,0:T(8,128)(2,1)}), bf16[32,128,128]{2,1,0:T(8,128)(2,1)S(1)}, u32[]{:S(2)}, u32[]{:S(2)}) async-start(bf16[32,128,128]{2,1,0:T(8,128)(2,1)} %bitcast.19), calls=%async_computation.3 | async-start | bytes 2097152 | tf_op jit(solution)/shard_map/all_to_all | solution.py:94
  106.7 14.2 %all-to-all-start.4 = ((f32[32,24,128]{2,1,0:T(8,128)}), f32[32,24,128]{2,1,0:T(8,128)S(1)}, u32[]{:S(2)}, u32[]{:S(2)}) async-start(f32[32,24,128]{2,1,0:T(8,128)} %reshape.108), calls=%async_computation.4 | async-start | bytes 786432 | tf_op jit(solution)/shard_map/all_to_all | solution.py:142
  135.4 7.6 %collective-permute-start.8 = (bf16[4,192,128]{2,1,0:T(8,128)(2,1)S(1)}, bf16[4,192,128]{2,1,0:T(8,128)(2,1)S(1)}, u32[]{:S(2)}, u32[]{:S(2)}) collective-permute-start(bf16[4,192,128]{2,1,0:T(8,128)(2,1)S(1)} %get-tuple-element.9), channel_id=1, source_target_pairs={{0,1},{1,2},{2,3},{3,4},{4,5},{5,6},{6,7},{7,0},{8,9},{9,10},{10,1... | collective-permute-start | bytes 589832 | tf_op jit(solution)/shard_map/ppermute | solution.py:118
  135.5 7.5 %collective-permute-start.9 = (bf16[4,192,128]{2,1,0:T(8,128)(2,1)S(1)}, bf16[4,192,128]{2,1,0:T(8,128)(2,1)S(1)}, u32[]{:S(2)}, u32[]{:S(2)}) collective-permute-start(bf16[4,192,128]{2,1,0:T(8,128)(2,1)S(1)} %get-tuple-element.9), channel_id=1, source_target_pairs={{0,7},{1,0},{2,1},{3,2},{4,3},{5,4},{6,5},{7,6},{8,15},{9,8},{10,9... | collective-permute-start | bytes 589832 | tf_op jit(solution)/shard_map/ppermute | solution.py:121
  143.0 6.7 %collective-permute-start.10 = (bf16[4,192,128]{2,1,0:T(8,128)(2,1)S(1)}, bf16[4,192,128]{2,1,0:T(8,128)(2,1)S(1)}, u32[]{:S(2)}, u32[]{:S(2)}) collective-permute-start(bf16[4,192,128]{2,1,0:T(8,128)(2,1)S(1)} %collective-permute-done.8), channel_id=1, source_target_pairs={{0,1},{1,2},{2,3},{3,4},{4,5},{5,6},{6,7},{7,0},{8,9},{9,10},{10,1... | collective-permute-start | bytes 589832 | tf_op jit(solution)/shard_map/ppermute | solution.py:118
  143.0 6.7 %collective-permute-start.11 = (bf16[4,192,128]{2,1,0:T(8,128)(2,1)S(1)}, bf16[4,192,128]{2,1,0:T(8,128)(2,1)S(1)}, u32[]{:S(2)}, u32[]{:S(2)}) collective-permute-start(bf16[4,192,128]{2,1,0:T(8,128)(2,1)S(1)} %collective-permute-done.9), channel_id=1, source_target_pairs={{0,7},{1,0},{2,1},{3,2},{4,3},{5,4},{6,5},{7,6},{8,15},{9,8},{10,9... | collective-permute-start | bytes 589832 | tf_op jit(solution)/shard_map/ppermute | solution.py:121
  149.6 5.7 %collective-permute-start.12 = (bf16[4,192,128]{2,1,0:T(8,128)(2,1)S(1)}, bf16[4,192,128]{2,1,0:T(8,128)(2,1)S(1)}, u32[]{:S(2)}, u32[]{:S(2)}) collective-permute-start(bf16[4,192,128]{2,1,0:T(8,128)(2,1)S(1)} %collective-permute-done.10), channel_id=1, source_target_pairs={{0,1},{1,2},{2,3},{3,4},{4,5},{5,6},{6,7},{7,0},{8,9},{9,10},{10,1... | collective-permute-start | bytes 589832 | tf_op jit(solution)/shard_map/ppermute | solution.py:118
  149.7 5.8 %collective-permute-start.13 = (bf16[4,192,128]{2,1,0:T(8,128)(2,1)S(1)}, bf16[4,192,128]{2,1,0:T(8,128)(2,1)S(1)}, u32[]{:S(2)}, u32[]{:S(2)}) collective-permute-start(bf16[4,192,128]{2,1,0:T(8,128)(2,1)S(1)} %collective-permute-done.11), channel_id=1, source_target_pairs={{0,7},{1,0},{2,1},{3,2},{4,3},{5,4},{6,5},{7,6},{8,15},{9,8},{10,9... | collective-permute-start | bytes 589832 | tf_op jit(solution)/shard_map/ppermute | solution.py:121
  155.4 5.7 %collective-permute-start.14 = (bf16[4,192,128]{2,1,0:T(8,128)(2,1)S(1)}, bf16[4,192,128]{2,1,0:T(8,128)(2,1)S(1)}, u32[]{:S(2)}, u32[]{:S(2)}) collective-permute-start(bf16[4,192,128]{2,1,0:T(8,128)(2,1)S(1)} %collective-permute-done.12), channel_id=1, source_target_pairs={{0,1},{1,2},{2,3},{3,4},{4,5},{5,6},{6,7},{7,0},{8,9},{9,10},{10,1... | collective-permute-start | bytes 589832 | tf_op jit(solution)/shard_map/ppermute | solution.py:118
  161.1 7.3 %collective-permute-start.15 = (bf16[32,192,128]{2,1,0:T(8,128)(2,1)S(1)}, bf16[32,192,128]{2,1,0:T(8,128)(2,1)S(1)}, u32[]{:S(2)}, u32[]{:S(2)}) collective-permute-start(bf16[32,192,128]{2,1,0:T(8,128)(2,1)S(1)} %constant_dynamic-update-slice_fusion.8.mine_ref), channel_id=1, source_target_pairs={{0,8},{8,0},{16,24},{24,16},{32,40},{40,32},{48,56},{56,48},{64,72... | collective-permute-start | bytes 4718600 | tf_op jit(solution)/shard_map/ppermute | solution.py:133
  (6 other events, 22.4 us)

commit v6 on v5

--- a/solution.py
+++ b/solution.py
@@ -85,6 +85,9 @@
     rows_dev = block // (per_slot * ntm)
     ksrc = kernel[:, 0].reshape(nnz, per_slot, ntm, rows_dev, block)
     ksrc = jnp.transpose(ksrc, (2, 1, 0, 3, 4)).reshape(ntm, -1, block)
+    field = solution[0].reshape(ntm, csl * rows_local, block)
+    field = lax.all_to_all(field, "tm", 0, 0, tiled=True)
+    field, ksrc = lax.optimization_barrier((field, ksrc))
     klags = lax.all_to_all(ksrc, "tm", 0, 0, tiled=True).astype(jnp.float32)
     klags = klags.reshape(length, per_slot, nnz * rows_dev, block)
     kspec = jnp.einsum(
@@ -144,8 +147,6 @@
         ys = jnp.transpose(ys, (2, 0, 3, 4, 5, 1, 6)).reshape(length, csl * rows_local, block)
         return jnp.einsum("tq,qcn->tcn", inv_table, ys, precision=HIGH)
 
-    field = solution[0].reshape(ntm, csl * rows_local, block)
-    field = lax.all_to_all(field, "tm", 0, 0, tiled=True)
     times = jnp.arange(length, dtype=jnp.int32)[:, None, None]
     for level_index in range(LEVELS):
         boundary = offsets[level_index]

time: 208 us -> 206 us (level)
    all_to_all x1, waiting for transfers between devices: 8.92 us -> 6.67 us  [shards(): field = lax.all_to_all(field, 'tm', 0, 0, tiled=True)]
  transfers between devices with their start and end apart: 20 -> 20, of which waited for: 11 -> 12; matrix products, arithmetic and copies ran while one was open for 6% -> 6% of each run, Pallas kernels for 0% -> 0%
where the time goes in v6:
time: 206 us; the launch traced here: 205 us
  waiting for transfers between devices  65.9 us (32%)
  blocking collectives  50.8 us (25%)
  starting transfers between devices  50.2 us (24%)
  local copies, waits for them, and re-layouts  18.1 us (9%)
  Pallas kernels  9.57 us (5%)
  other arithmetic  6.97 us (3%)
  matrix products  3.06 us (1%)
    ppermute x8, waiting for transfers between devices, ring_gather(): a = lax.ppermute(a, 'state', fwd)  31.8 us
    all_to_all x2, blocking collectives, respond(): xs = lax.all_to_all(xs, 'tm', 0, 0, tiled=True)  23.5 us
    ppermute x6, starting transfers between devices, ring_gather(): b = lax.ppermute(b, 'state', bwd)  17.3 us
    all_to_all x1, waiting for transfers between devices, shards(): kspec = lax.all_to_all(kspec, 'tm', 0, 0, tiled=True)  15.3 us
    all_to_all x1, blocking collectives, shards(): field = lax.all_to_all(field, 'tm', 0, 0, tiled=True)  13.7 us
    all_to_all x1, blocking collectives, respond(): ys = lax.all_to_all(ys, 'tm', 0, 0, tiled=True)  13.6 us
    pallas_call x2, Pallas kernels, block_products(): pl.pallas_call(_products_body, grid_spec=pltpu.PrefetchScalarGridSpec(num...  9.57 us
    all_to_all x1, waiting for transfers between devices, respond(): ys = lax.all_to_all(ys, 'tm', 0, 0, tiled=True)  9.1 us
  transfers between devices with their start and end apart: 20, of which 12 were waited for; matrix products, arithmetic and copies ran while one was open for 6% of the time, Pallas kernels for 0%

profile of v6, /device:TPU:1, one launch (start us, length us, event | category | flops | bytes accessed | tf_op | source)
XLA Modules:
  0.0 205.1 jit_solution(4850184344048247886)
XLA Ops:
  1.9 8.7 %all-to-all-start = ((f32[32,24,128]{2,1,0:T(8,128)}), f32[32,24,128]{2,1,0:T(8,128)S(1)}, u32[]{:S(2)}, u32[]{:S(2)}) async-start(f32[32,24,128]{2,1,0:T(8,128)} %reshape_squeeze.6), calls=%async_computation | async-start | bytes 786432 | tf_op jit(solution)/shard_map/all_to_all | solution.py:89
  14.1 6.7 %all-to-all-done = f32[32,24,128]{2,1,0:T(8,128)S(1)} async-done(((f32[32,24,128]{2,1,0:T(8,128)}), f32[32,24,128]{2,1,0:T(8,128)S(1)}, u32[]{:S(2)}, u32[]{:S(2)}) %all-to-all-start) | async-done | bytes 393248 | tf_op jit(solution)/shard_map/all_to_all | solution.py:89
  21.4 11.7 %all_to_all.40 = bf16[32,24,128]{2,1,0:T(8,128)(2,1)S(1)} all-to-all(bf16[32,24,128]{2,1,0:T(8,128)(2,1)S(1)} %bitcast.108), channel_id=1, replica_groups=mesh['tm'=32,'state'=8] {'tm'}, dimensions={0} | all-to-all | bytes 393216 | tf_op jit(solution)/shard_map/all_to_all | solution.py:132
  35.7 3.9 %collective-permute-start.1 = (bf16[4,192,128]{2,1,0:T(8,128)(2,1)}, bf16[4,192,128]{2,1,0:T(8,128)(2,1)S(1)}, u32[]{:S(2)}, u32[]{:S(2)}) collective-permute-start(bf16[4,192,128]{2,1,0:T(8,128)(2,1)} %get-tuple-element.15), channel_id=1, source_target_pairs={{0,7},{1,0},{2,1},{3,2},{4,3},{5,4},{6,5},{7,6},{8,15},{9,8},{10,9... | collective-permute-start | bytes 589832 | tf_op jit(solution)/shard_map/ppermute | solution.py:124
  39.7 4.1 %all-to-all-start.2 = ((bf16[32,128,128]{2,1,0:T(8,128)(2,1)}), bf16[32,128,128]{2,1,0:T(8,128)(2,1)S(1)}, u32[]{:S(2)}, u32[]{:S(2)}) async-start(bf16[32,128,128]{2,1,0:T(8,128)(2,1)} %bitcast.2), calls=%async_computation.2 | async-start | bytes 2097152 | tf_op jit(solution)/shard_map/all_to_all | solution.py:91
  47.7 4.2 %collective-permute-done.2 = bf16[4,192,128]{2,1,0:T(8,128)(2,1)S(1)} collective-permute-done((bf16[4,192,128]{2,1,0:T(8,128)(2,1)S(1)}, bf16[4,192,128]{2,1,0:T(8,128)(2,1)S(1)}, u32[]{:S(2)}, u32[]{:S(2)}) %collective-permute-start.2) | collective-permute-done | bytes 196640 | tf_op jit(solution)/shard_map/ppermute | solution.py:121
  54.7 3.3 %collective-permute-done.4 = bf16[4,192,128]{2,1,0:T(8,128)(2,1)S(1)} collective-permute-done((bf16[4,192,128]{2,1,0:T(8,128)(2,1)S(1)}, bf16[4,192,128]{2,1,0:T(8,128)(2,1)S(1)}, u32[]{:S(2)}, u32[]{:S(2)}) %collective-permute-start.4) | collective-permute-done | bytes 196640 | tf_op jit(solution)/shard_map/ppermute | solution.py:121
  58.1 5.7 %collective-permute-done.6 = bf16[4,192,128]{2,1,0:T(8,128)(2,1)S(1)} collective-permute-done((bf16[4,192,128]{2,1,0:T(8,128)(2,1)S(1)}, bf16[4,192,128]{2,1,0:T(8,128)(2,1)S(1)}, u32[]{:S(2)}, u32[]{:S(2)}) %collective-permute-start.6) | collective-permute-done | bytes 196640 | tf_op jit(solution)/shard_map/ppermute | solution.py:121
  63.8 3.7 %collective-permute-start.7 = (bf16[32,192,128]{2,1,0:T(8,128)(2,1)S(1)}, bf16[32,192,128]{2,1,0:T(8,128)(2,1)}, u32[]{:S(2)}, u32[]{:S(2)}) collective-permute-start(bf16[32,192,128]{2,1,0:T(8,128)(2,1)S(1)} %constant_dynamic-update-slice_fusion.mine_ref), channel_id=1, source_target_pairs={{0,8},{8,0},{16,24},{24,16},{32,40},{40,32},{48,56},{56,48},{64,72... | collective-permute-start | bytes 4718600 | tf_op jit(solution)/shard_map/ppermute | solution.py:136
  70.5 6.5 %all-to-all-start.3 = ((bf16[32,128,128]{2,1,0:T(8,128)(2,1)}), bf16[32,128,128]{2,1,0:T(8,128)(2,1)S(1)}, u32[]{:S(2)}, u32[]{:S(2)}) async-start(bf16[32,128,128]{2,1,0:T(8,128)(2,1)} %bitcast.20), calls=%async_computation.3 | async-start | bytes 2097152 | tf_op jit(solution)/shard_map/all_to_all | solution.py:97
  78.7 15.3 %all-to-all-done.3 = bf16[32,128,128]{2,1,0:T(8,128)(2,1)S(1)} async-done(((bf16[32,128,128]{2,1,0:T(8,128)(2,1)}), bf16[32,128,128]{2,1,0:T(8,128)(2,1)S(1)}, u32[]{:S(2)}, u32[]{:S(2)}) %all-to-all-start.3) | async-done | bytes 1048608 | tf_op jit(solution)/shard_map/all_to_all | solution.py:97
  96.9 4.8 %shard_map.64 = f32[8,192,128]{2,1,0:T(8,128)} custom-call(s32[32]{0:T(128)} %fusion.16.pick_ref, s32[32]{0:T(128)} %compare_convert_fusion.src_ref, s32[32]{0:T(128)} %clamp_bitcast_fusion.row_ref, bf16[32,192,128]{2,1,0:T(8,128)(2,1)} %copy-done, bf16[32,192,128]{2,1,0:T(8,128)(2,1)} %collective-permute-done.7.other_ref, bf16[32,128,128]{2,1,0:T(8,128)(2,1)} %bitcast.97), custom_call_target="tpu_custom_call" | custom-call | tf_op jit(solution)/shard_map/pallas_call | solution.py:53
  104.9 3.9 %all-to-all-start.4 = ((f32[32,24,128]{2,1,0:T(8,128)}), f32[32,24,128]{2,1,0:T(8,128)S(1)}, u32[]{:S(2)}, u32[]{:S(2)}) async-start(f32[32,24,128]{2,1,0:T(8,128)} %reshape.108), calls=%async_computation.4 | async-start | bytes 786432 | tf_op jit(solution)/shard_map/all_to_all | solution.py:145
  109.9 9.1 %all-to-all-done.4 = f32[32,24,128]{2,1,0:T(8,128)S(1)} async-done(((f32[32,24,128]{2,1,0:T(8,128)}), f32[32,24,128]{2,1,0:T(8,128)S(1)}, u32[]{:S(2)}, u32[]{:S(2)}) %all-to-all-start.4) | async-done | bytes 393248 | tf_op jit(solution)/shard_map/all_to_all | solution.py:145
  121.6 11.7 %all_to_all.41 = bf16[32,24,128]{2,1,0:T(8,128)(2,1)S(1)} all-to-all(bf16[32,24,128]{2,1,0:T(8,128)(2,1)S(1)} %bitcast.110), channel_id=1, replica_groups=mesh['tm'=32,'state'=8] {'tm'}, dimensions={0} | all-to-all | bytes 393216 | tf_op jit(solution)/shard_map/all_to_all | solution.py:132
  136.3 4.8 %collective-permute-done.8 = bf16[4,192,128]{2,1,0:T(8,128)(2,1)S(1)} collective-permute-done((bf16[4,192,128]{2,1,0:T(8,128)(2,1)S(1)}, bf16[4,192,128]{2,1,0:T(8,128)(2,1)S(1)}, u32[]{:S(2)}, u32[]{:S(2)}) %collective-permute-start.8) | collective-permute-done | bytes 196640 | tf_op jit(solution)/shard_map/ppermute | solution.py:121
  143.9 3.9 %collective-permute-done.10 = bf16[4,192,128]{2,1,0:T(8,128)(2,1)S(1)} collective-permute-done((bf16[4,192,128]{2,1,0:T(8,128)(2,1)S(1)}, bf16[4,192,128]{2,1,0:T(8,128)(2,1)S(1)}, u32[]{:S(2)}, u32[]{:S(2)}) %collective-permute-start.10) | collective-permute-done | bytes 196640 | tf_op jit(solution)/shard_map/ppermute | solution.py:121
  150.5 3.0 %collective-permute-done.12 = bf16[4,192,128]{2,1,0:T(8,128)(2,1)S(1)} collective-permute-done((bf16[4,192,128]{2,1,0:T(8,128)(2,1)S(1)}, bf16[4,192,128]{2,1,0:T(8,128)(2,1)S(1)}, u32[]{:S(2)}, u32[]{:S(2)}) %collective-permute-start.12) | collective-permute-done | bytes 196640 | tf_op jit(solution)/shard_map/ppermute | solution.py:121
  153.6 5.7 %collective-permute-done.14 = bf16[4,192,128]{2,1,0:T(8,128)(2,1)S(1)} collective-permute-done((bf16[4,192,128]{2,1,0:T(8,128)(2,1)S(1)}, bf16[4,192,128]{2,1,0:T(8,128)(2,1)S(1)}, u32[]{:S(2)}, u32[]{:S(2)}) %collective-permute-start.14) | collective-permute-done | bytes 196640 | tf_op jit(solution)/shard_map/ppermute | solution.py:121
  159.3 4.3 %collective-permute-start.15 = (bf16[32,192,128]{2,1,0:T(8,128)(2,1)S(1)}, bf16[32,192,128]{2,1,0:T(8,128)(2,1)S(1)}, u32[]{:S(2)}, u32[]{:S(2)}) collective-permute-start(bf16[32,192,128]{2,1,0:T(8,128)(2,1)S(1)} %constant_dynamic-update-slice_fusion.8.mine_ref), channel_id=1, source_target_pairs={{0,8},{8,0},{16,24},{24,16},{32,40},{40,32},{48,56},{56,48},{64,72... | collective-permute-start | bytes 4718600 | tf_op jit(solution)/shard_map/ppermute | solution.py:136
  163.6 3.0 %collective-permute-done.15.other_ref = bf16[32,192,128]{2,1,0:T(8,128)(2,1)S(1)} collective-permute-done((bf16[32,192,128]{2,1,0:T(8,128)(2,1)S(1)}, bf16[32,192,128]{2,1,0:T(8,128)(2,1)S(1)}, u32[]{:S(2)}, u32[]{:S(2)}) %collective-permute-start.15) | collective-permute-done | bytes 1572896 | tf_op jit(solution)/shard_map/ppermute | solution.py:136
  167.7 4.8 %shard_map.65 = f32[8,192,128]{2,1,0:T(8,128)} custom-call(s32[32]{0:T(128)} %fusion.16.pick_ref, s32[32]{0:T(128)} %compare_convert_fusion.src_ref, s32[32]{0:T(128)} %clamp_bitcast_fusion.row_ref, bf16[32,192,128]{2,1,0:T(8,128)(2,1)} %copy-done.1, bf16[32,192,128]{2,1,0:T(8,128)(2,1)} %copy-done.2, bf16[32,128,128]{2,1,0:T(8,128)(2,1)} %bitcast.98), custom_call_target="tpu_custom_call" | custom-call | tf_op jit(solution)/shard_map/pallas_call | solution.py:53
  175.0 13.6 %all_to_all.42 = f32[32,24,128]{2,1,0:T(8,128)S(1)} all-to-all(f32[32,24,128]{2,1,0:T(8,128)S(1)} %reshape.115), channel_id=1, replica_groups=mesh['tm'=32,'state'=8] {'tm'}, dimensions={0} | all-to-all | bytes 786432 | tf_op jit(solution)/shard_map/all_to_all | solution.py:145
  190.7 13.7 %all_to_all.43 = f32[32,24,128]{2,1,0:T(8,128)S(1)} all-to-all(f32[32,24,128]{2,1,0:T(8,128)S(1)} %copy.61), channel_id=1, replica_groups=mesh['tm'=32,'state'=8] {'tm'}, dimensions={0} | all-to-all | bytes 786432 | tf_op jit(solution)/shard_map/all_to_all | solution.py:156
  (101 shorter events, 44.5 us)
Async XLA Ops:
  0.0 10.6 %copy-start.3 = (bf16[32,1,128,128]{3,2,1,0:T(8,128)(2,1)S(1)}, bf16[32,1,128,128]{3,2,1,0:T(8,128)(2,1)}, u32[]{:S(2)}) copy-start(bf16[32,1,128,128]{3,2,1,0:T(8,128)(2,1)} %param.7) | copy-start | bytes 3145732
  1.9 10.9 %copy-start.7 = (s32[2]{0:T(128)S(1)}, s32[2]{0:T(128)}, u32[]{:S(2)}) copy-start(s32[2]{0:T(128)} %param.9) | copy-start | bytes 28
  1.9 18.9 %copy-start.5 = (f32[32,32,1]{1,0,2:T(8,128)S(1)}, f32[32,32,1]{1,0,2:T(8,128)}, u32[]{:S(2)}) copy-start(f32[32,32,1]{1,0,2:T(8,128)} %constant.106) | copy-start | bytes 12292
  1.9 18.9 %all-to-all-start = ((f32[32,24,128]{2,1,0:T(8,128)}), f32[32,24,128]{2,1,0:T(8,128)S(1)}, u32[]{:S(2)}, u32[]{:S(2)}) async-start(f32[32,24,128]{2,1,0:T(8,128)} %reshape_squeeze.6), calls=%async_computation | async-start | bytes 786432 | tf_op jit(solution)/shard_map/all_to_all | solution.py:89
  34.1 10.9 %collective-permute-start = (bf16[4,192,128]{2,1,0:T(8,128)(2,1)}, bf16[4,192,128]{2,1,0:T(8,128)(2,1)S(1)}, u32[]{:S(2)}, u32[]{:S(2)}) collective-permute-start(bf16[4,192,128]{2,1,0:T(8,128)(2,1)} %get-tuple-element.15), channel_id=1, source_target_pairs={{0,1},{1,2},{2,3},{3,4},{4,5},{5,6},{6,7},{7,0},{8,9},{9,10},{10,1... | collective-permute-start | bytes 589832 | tf_op jit(solution)/shard_map/ppermute | solution.py:121
  35.7 9.3 %collective-permute-start.1 = (bf16[4,192,128]{2,1,0:T(8,128)(2,1)}, bf16[4,192,128]{2,1,0:T(8,128)(2,1)S(1)}, u32[]{:S(2)}, u32[]{:S(2)}) collective-permute-start(bf16[4,192,128]{2,1,0:T(8,128)(2,1)} %get-tuple-element.15), channel_id=1, source_target_pairs={{0,7},{1,0},{2,1},{3,2},{4,3},{5,4},{6,5},{7,6},{8,15},{9,8},{10,9... | collective-permute-start | bytes 589832 | tf_op jit(solution)/shard_map/ppermute | solution.py:124
  39.7 27.8 %all-to-all-start.2 = ((bf16[32,128,128]{2,1,0:T(8,128)(2,1)}), bf16[32,128,128]{2,1,0:T(8,128)(2,1)S(1)}, u32[]{:S(2)}, u32[]{:S(2)}) async-start(bf16[32,128,128]{2,1,0:T(8,128)(2,1)} %bitcast.2), calls=%async_computation.2 | async-start | bytes 2097152 | tf_op jit(solution)/shard_map/all_to_all | solution.py:91
  45.0 6.9 %collective-permute-start.2 = (bf16[4,192,128]{2,1,0:T(8,128)(2,1)S(1)}, bf16[4,192,128]{2,1,0:T(8,128)(2,1)S(1)}, u32[]{:S(2)}, u32[]{:S(2)}) collective-permute-start(bf16[4,192,128]{2,1,0:T(8,128)(2,1)S(1)} %collective-permute-done), channel_id=1, source_target_pairs={{0,1},{1,2},{2,3},{3,4},{4,5},{5,6},{6,7},{7,0},{8,9},{9,10},{10,1... | collective-permute-start | bytes 589832 | tf_op jit(solution)/shard_map/ppermute | solution.py:121
  45.0 6.9 %collective-permute-start.3 = (bf16[4,192,128]{2,1,0:T(8,128)(2,1)S(1)}, bf16[4,192,128]{2,1,0:T(8,128)(2,1)S(1)}, u32[]{:S(2)}, u32[]{:S(2)}) collective-permute-start(bf16[4,192,128]{2,1,0:T(8,128)(2,1)S(1)} %collective-permute-done.1), channel_id=1, source_target_pairs={{0,7},{1,0},{2,1},{3,2},{4,3},{5,4},{6,5},{7,6},{8,15},{9,8},{10,9... | collective-permute-start | bytes 589832 | tf_op jit(solution)/shard_map/ppermute | solution.py:124
  51.9 6.1 %collective-permute-start.4 = (bf16[4,192,128]{2,1,0:T(8,128)(2,1)S(1)}, bf16[4,192,128]{2,1,0:T(8,128)(2,1)S(1)}, u32[]{:S(2)}, u32[]{:S(2)}) collective-permute-start(bf16[4,192,128]{2,1,0:T(8,128)(2,1)S(1)} %collective-permute-done.2), channel_id=1, source_target_pairs={{0,1},{1,2},{2,3},{3,4},{4,5},{5,6},{6,7},{7,0},{8,9},{9,10},{10,1... | collective-permute-start | bytes 589832 | tf_op jit(solution)/shard_map/ppermute | solution.py:121
  51.9 6.1 %collective-permute-start.5 = (bf16[4,192,128]{2,1,0:T(8,128)(2,1)S(1)}, bf16[4,192,128]{2,1,0:T(8,128)(2,1)S(1)}, u32[]{:S(2)}, u32[]{:S(2)}) collective-permute-start(bf16[4,192,128]{2,1,0:T(8,128)(2,1)S(1)} %collective-permute-done.3), channel_id=1, source_target_pairs={{0,7},{1,0},{2,1},{3,2},{4,3},{5,4},{6,5},{7,6},{8,15},{9,8},{10,9... | collective-permute-start | bytes 589832 | tf_op jit(solution)/shard_map/ppermute | solution.py:124
  54.6 13.5 %copy-start.6 = (f32[2,16,32,1,1]{2,1,0,4,3:T(8,128)S(1)}, f32[2,16,32,1,1]{2,1,0,4,3:T(8,128)}, u32[]{:S(2)}) copy-start(f32[2,16,32,1,1]{2,1,0,4,3:T(8,128)} %constant.107) | copy-start | bytes 12292
  58.0 5.7 %collective-permute-start.6 = (bf16[4,192,128]{2,1,0:T(8,128)(2,1)S(1)}, bf16[4,192,128]{2,1,0:T(8,128)(2,1)S(1)}, u32[]{:S(2)}, u32[]{:S(2)}) collective-permute-start(bf16[4,192,128]{2,1,0:T(8,128)(2,1)S(1)} %collective-permute-done.4), channel_id=1, source_target_pairs={{0,1},{1,2},{2,3},{3,4},{4,5},{5,6},{6,7},{7,0},{8,9},{9,10},{10,1... | collective-permute-start | bytes 589832 | tf_op jit(solution)/shard_map/ppermute | solution.py:121
  63.8 33.1 %collective-permute-start.7 = (bf16[32,192,128]{2,1,0:T(8,128)(2,1)S(1)}, bf16[32,192,128]{2,1,0:T(8,128)(2,1)}, u32[]{:S(2)}, u32[]{:S(2)}) collective-permute-start(bf16[32,192,128]{2,1,0:T(8,128)(2,1)S(1)} %constant_dynamic-update-slice_fusion.mine_ref), channel_id=1, source_target_pairs={{0,8},{8,0},{16,24},{24,16},{32,40},{40,32},{48,56},{56,48},{64,72... | collective-permute-start | bytes 4718600 | tf_op jit(solution)/shard_map/ppermute | solution.py:136
  70.5 23.5 %all-to-all-start.3 = ((bf16[32,128,128]{2,1,0:T(8,128)(2,1)}), bf16[32,128,128]{2,1,0:T(8,128)(2,1)S(1)}, u32[]{:S(2)}, u32[]{:S(2)}) async-start(bf16[32,128,128]{2,1,0:T(8,128)(2,1)} %bitcast.20), calls=%async_computation.3 | async-start | bytes 2097152 | tf_op jit(solution)/shard_map/all_to_all | solution.py:97
  104.9 14.2 %all-to-all-start.4 = ((f32[32,24,128]{2,1,0:T(8,128)}), f32[32,24,128]{2,1,0:T(8,128)S(1)}, u32[]{:S(2)}, u32[]{:S(2)}) async-start(f32[32,24,128]{2,1,0:T(8,128)} %reshape.108), calls=%async_computation.4 | async-start | bytes 786432 | tf_op jit(solution)/shard_map/all_to_all | solution.py:145
  133.5 7.6 %collective-permute-start.8 = (bf16[4,192,128]{2,1,0:T(8,128)(2,1)S(1)}, bf16[4,192,128]{2,1,0:T(8,128)(2,1)S(1)}, u32[]{:S(2)}, u32[]{:S(2)}) collective-permute-start(bf16[4,192,128]{2,1,0:T(8,128)(2,1)S(1)} %get-tuple-element.13), channel_id=1, source_target_pairs={{0,1},{1,2},{2,3},{3,4},{4,5},{5,6},{6,7},{7,0},{8,9},{9,10},{10,1... | collective-permute-start | bytes 589832 | tf_op jit(solution)/shard_map/ppermute | solution.py:121
  133.6 7.5 %collective-permute-start.9 = (bf16[4,192,128]{2,1,0:T(8,128)(2,1)S(1)}, bf16[4,192,128]{2,1,0:T(8,128)(2,1)S(1)}, u32[]{:S(2)}, u32[]{:S(2)}) collective-permute-start(bf16[4,192,128]{2,1,0:T(8,128)(2,1)S(1)} %get-tuple-element.13), channel_id=1, source_target_pairs={{0,7},{1,0},{2,1},{3,2},{4,3},{5,4},{6,5},{7,6},{8,15},{9,8},{10,9... | collective-permute-start | bytes 589832 | tf_op jit(solution)/shard_map/ppermute | solution.py:124
  141.1 6.7 %collective-permute-start.10 = (bf16[4,192,128]{2,1,0:T(8,128)(2,1)S(1)}, bf16[4,192,128]{2,1,0:T(8,128)(2,1)S(1)}, u32[]{:S(2)}, u32[]{:S(2)}) collective-permute-start(bf16[4,192,128]{2,1,0:T(8,128)(2,1)S(1)} %collective-permute-done.8), channel_id=1, source_target_pairs={{0,1},{1,2},{2,3},{3,4},{4,5},{5,6},{6,7},{7,0},{8,9},{9,10},{10,1... | collective-permute-start | bytes 589832 | tf_op jit(solution)/shard_map/ppermute | solution.py:121
  141.1 6.7 %collective-permute-start.11 = (bf16[4,192,128]{2,1,0:T(8,128)(2,1)S(1)}, bf16[4,192,128]{2,1,0:T(8,128)(2,1)S(1)}, u32[]{:S(2)}, u32[]{:S(2)}) collective-permute-start(bf16[4,192,128]{2,1,0:T(8,128)(2,1)S(1)} %collective-permute-done.9), channel_id=1, source_target_pairs={{0,7},{1,0},{2,1},{3,2},{4,3},{5,4},{6,5},{7,6},{8,15},{9,8},{10,9... | collective-permute-start | bytes 589832 | tf_op jit(solution)/shard_map/ppermute | solution.py:124
  147.8 5.7 %collective-permute-start.12 = (bf16[4,192,128]{2,1,0:T(8,128)(2,1)S(1)}, bf16[4,192,128]{2,1,0:T(8,128)(2,1)S(1)}, u32[]{:S(2)}, u32[]{:S(2)}) collective-permute-start(bf16[4,192,128]{2,1,0:T(8,128)(2,1)S(1)} %collective-permute-done.10), channel_id=1, source_target_pairs={{0,1},{1,2},{2,3},{3,4},{4,5},{5,6},{6,7},{7,0},{8,9},{9,10},{10,1... | collective-permute-start | bytes 589832 | tf_op jit(solution)/shard_map/ppermute | solution.py:121
  147.8 5.8 %collective-permute-start.13 = (bf16[4,192,128]{2,1,0:T(8,128)(2,1)S(1)}, bf16[4,192,128]{2,1,0:T(8,128)(2,1)S(1)}, u32[]{:S(2)}, u32[]{:S(2)}) collective-permute-start(bf16[4,192,128]{2,1,0:T(8,128)(2,1)S(1)} %collective-permute-done.11), channel_id=1, source_target_pairs={{0,7},{1,0},{2,1},{3,2},{4,3},{5,4},{6,5},{7,6},{8,15},{9,8},{10,9... | collective-permute-start | bytes 589832 | tf_op jit(solution)/shard_map/ppermute | solution.py:124
  153.5 5.7 %collective-permute-start.14 = (bf16[4,192,128]{2,1,0:T(8,128)(2,1)S(1)}, bf16[4,192,128]{2,1,0:T(8,128)(2,1)S(1)}, u32[]{:S(2)}, u32[]{:S(2)}) collective-permute-start(bf16[4,192,128]{2,1,0:T(8,128)(2,1)S(1)} %collective-permute-done.12), channel_id=1, source_target_pairs={{0,1},{1,2},{2,3},{3,4},{4,5},{5,6},{6,7},{7,0},{8,9},{9,10},{10,1... | collective-permute-start | bytes 589832 | tf_op jit(solution)/shard_map/ppermute | solution.py:121
  159.3 7.3 %collective-permute-start.15 = (bf16[32,192,128]{2,1,0:T(8,128)(2,1)S(1)}, bf16[32,192,128]{2,1,0:T(8,128)(2,1)S(1)}, u32[]{:S(2)}, u32[]{:S(2)}) collective-permute-start(bf16[32,192,128]{2,1,0:T(8,128)(2,1)S(1)} %constant_dynamic-update-slice_fusion.8.mine_ref), channel_id=1, source_target_pairs={{0,8},{8,0},{16,24},{24,16},{32,40},{40,32},{48,56},{56,48},{64,72... | collective-permute-start | bytes 4718600 | tf_op jit(solution)/shard_map/ppermute | solution.py:136
  (6 other events, 22.1 us)

commit v7 on v6

--- a/solution.py
+++ b/solution.py
@@ -141,8 +141,8 @@
         ys_re = a - real_slot * b
         ys_im = real_slot * (c_ + d) + (1.0 - real_slot) * b
         ys = jnp.stack([ys_re, ys_im], 0).reshape(2, rows_local, ntm, csl, ah)
-        ys = jnp.transpose(ys, (2, 0, 3, 1, 4)).reshape(ntm, -1, 2 * ah)
-        ys = lax.all_to_all(ys, "tm", 0, 0, tiled=True)
+        ys = jnp.transpose(ys, (2, 0, 3, 1, 4)).reshape(ntm, -1, 2 * ah).astype(jnp.bfloat16)
+        ys = lax.all_to_all(ys, "tm", 0, 0, tiled=True).astype(jnp.float32)
         ys = ys.reshape(half, per_slot, 2, csl, rows_local // 2, 2, ah)
         ys = jnp.transpose(ys, (2, 0, 3, 4, 5, 1, 6)).reshape(length, csl * rows_local, block)
         return jnp.einsum("tq,qcn->tcn", inv_table, ys, precision=HIGH)

time: 206 us -> 200 us (0.971)
    another operation x0 -> x2, other arithmetic: none -> 3.34 us
    sub x2 -> x0, other arithmetic: 3.34 us -> none  [respond(): ys_re = a - real_slot * b]
where the time goes in v7:
time: 200 us
  waiting for transfers between devices  64 us (32%)
  starting transfers between devices  50.4 us (25%)
  blocking collectives  49.1 us (25%)
  local copies, waits for them, and re-layouts  16.4 us (8%)
  Pallas kernels  9.58 us (5%)
  other arithmetic  7.03 us (4%)
  matrix products  2.74 us (1%)
    ppermute x8, waiting for transfers between devices, ring_gather(): a = lax.ppermute(a, 'state', fwd)  31.8 us
    all_to_all x2, blocking collectives, respond(): xs = lax.all_to_all(xs, 'tm', 0, 0, tiled=True)  23.6 us
    ppermute x6, starting transfers between devices, ring_gather(): b = lax.ppermute(b, 'state', bwd)  17.3 us
    all_to_all x1, waiting for transfers between devices, shards(): kspec = lax.all_to_all(kspec, 'tm', 0, 0, tiled=True)  15.3 us
    all_to_all x1, blocking collectives, shards(): field = lax.all_to_all(field, 'tm', 0, 0, tiled=True)  13.8 us
    all_to_all x1, blocking collectives, respond(): ys = lax.all_to_all(ys, 'tm', 0, 0, tiled=True).astype(jnp.float32)  11.7 us
    pallas_call x2, Pallas kernels, block_products(): pl.pallas_call(_products_body, grid_spec=pltpu.PrefetchScalarGridSpec(num...  9.58 us
    all_to_all x1, starting transfers between devices, shards(): field = lax.all_to_all(field, 'tm', 0, 0, tiled=True)  8.71 us
  transfers between devices with their start and end apart: 20, of which 12 were waited for; matrix products, arithmetic and copies ran while one was open for 6% of the time, Pallas kernels for 0%

profile of v7, /device:TPU:1, one launch (start us, length us, event | category | flops | bytes accessed | tf_op | source)
XLA Modules:
  0.0 199.7 jit_solution(15584139928597608567)
XLA Ops:
  1.9 8.7 %all-to-all-start = ((f32[32,24,128]{2,1,0:T(8,128)}), f32[32,24,128]{2,1,0:T(8,128)S(1)}, u32[]{:S(2)}, u32[]{:S(2)}) async-start(f32[32,24,128]{2,1,0:T(8,128)} %reshape_squeeze.6), calls=%async_computation | async-start | bytes 786432 | tf_op jit(solution)/shard_map/all_to_all | solution.py:89
  14.1 6.7 %all-to-all-done = f32[32,24,128]{2,1,0:T(8,128)S(1)} async-done(((f32[32,24,128]{2,1,0:T(8,128)}), f32[32,24,128]{2,1,0:T(8,128)S(1)}, u32[]{:S(2)}, u32[]{:S(2)}) %all-to-all-start) | async-done | bytes 393248 | tf_op jit(solution)/shard_map/all_to_all | solution.py:89
  21.4 11.7 %all_to_all.40 = bf16[32,24,128]{2,1,0:T(8,128)(2,1)S(1)} all-to-all(bf16[32,24,128]{2,1,0:T(8,128)(2,1)S(1)} %bitcast.104), channel_id=1, replica_groups=mesh['tm'=32,'state'=8] {'tm'}, dimensions={0} | all-to-all | bytes 393216 | tf_op jit(solution)/shard_map/all_to_all | solution.py:132
  35.7 3.9 %collective-permute-start.1 = (bf16[4,192,128]{2,1,0:T(8,128)(2,1)}, bf16[4,192,128]{2,1,0:T(8,128)(2,1)S(1)}, u32[]{:S(2)}, u32[]{:S(2)}) collective-permute-start(bf16[4,192,128]{2,1,0:T(8,128)(2,1)} %get-tuple-element.15), channel_id=1, source_target_pairs={{0,7},{1,0},{2,1},{3,2},{4,3},{5,4},{6,5},{7,6},{8,15},{9,8},{10,9... | collective-permute-start | bytes 589832 | tf_op jit(solution)/shard_map/ppermute | solution.py:124
  39.7 4.1 %all-to-all-start.2 = ((bf16[32,128,128]{2,1,0:T(8,128)(2,1)}), bf16[32,128,128]{2,1,0:T(8,128)(2,1)S(1)}, u32[]{:S(2)}, u32[]{:S(2)}) async-start(bf16[32,128,128]{2,1,0:T(8,128)(2,1)} %bitcast.2), calls=%async_computation.2 | async-start | bytes 2097152 | tf_op jit(solution)/shard_map/all_to_all | solution.py:91
  47.7 4.2 %collective-permute-done.2 = bf16[4,192,128]{2,1,0:T(8,128)(2,1)S(1)} collective-permute-done((bf16[4,192,128]{2,1,0:T(8,128)(2,1)S(1)}, bf16[4,192,128]{2,1,0:T(8,128)(2,1)S(1)}, u32[]{:S(2)}, u32[]{:S(2)}) %collective-permute-start.2) | collective-permute-done | bytes 196640 | tf_op jit(solution)/shard_map/ppermute | solution.py:121
  54.7 3.3 %collective-permute-done.4 = bf16[4,192,128]{2,1,0:T(8,128)(2,1)S(1)} collective-permute-done((bf16[4,192,128]{2,1,0:T(8,128)(2,1)S(1)}, bf16[4,192,128]{2,1,0:T(8,128)(2,1)S(1)}, u32[]{:S(2)}, u32[]{:S(2)}) %collective-permute-start.4) | collective-permute-done | bytes 196640 | tf_op jit(solution)/shard_map/ppermute | solution.py:121
  58.1 5.7 %collective-permute-done.6 = bf16[4,192,128]{2,1,0:T(8,128)(2,1)S(1)} collective-permute-done((bf16[4,192,128]{2,1,0:T(8,128)(2,1)S(1)}, bf16[4,192,128]{2,1,0:T(8,128)(2,1)S(1)}, u32[]{:S(2)}, u32[]{:S(2)}) %collective-permute-start.6) | collective-permute-done | bytes 196640 | tf_op jit(solution)/shard_map/ppermute | solution.py:121
  63.8 3.7 %collective-permute-start.7 = (bf16[32,192,128]{2,1,0:T(8,128)(2,1)S(1)}, bf16[32,192,128]{2,1,0:T(8,128)(2,1)}, u32[]{:S(2)}, u32[]{:S(2)}) collective-permute-start(bf16[32,192,128]{2,1,0:T(8,128)(2,1)S(1)} %constant_dynamic-update-slice_fusion.mine_ref), channel_id=1, source_target_pairs={{0,8},{8,0},{16,24},{24,16},{32,40},{40,32},{48,56},{56,48},{64,72... | collective-permute-start | bytes 4718600 | tf_op jit(solution)/shard_map/ppermute | solution.py:136
  70.5 6.5 %all-to-all-start.3 = ((bf16[32,128,128]{2,1,0:T(8,128)(2,1)}), bf16[32,128,128]{2,1,0:T(8,128)(2,1)S(1)}, u32[]{:S(2)}, u32[]{:S(2)}) async-start(bf16[32,128,128]{2,1,0:T(8,128)(2,1)} %bitcast.20), calls=%async_computation.3 | async-start | bytes 2097152 | tf_op jit(solution)/shard_map/all_to_all | solution.py:97
  78.7 15.3 %all-to-all-done.3 = bf16[32,128,128]{2,1,0:T(8,128)(2,1)S(1)} async-done(((bf16[32,128,128]{2,1,0:T(8,128)(2,1)}), bf16[32,128,128]{2,1,0:T(8,128)(2,1)S(1)}, u32[]{:S(2)}, u32[]{:S(2)}) %all-to-all-start.3) | async-done | bytes 1048608 | tf_op jit(solution)/shard_map/all_to_all | solution.py:97
  96.9 4.8 %shard_map.64 = f32[8,192,128]{2,1,0:T(8,128)} custom-call(s32[32]{0:T(128)} %fusion.20.pick_ref, s32[32]{0:T(128)} %compare_convert_fusion.src_ref, s32[32]{0:T(128)} %clamp_bitcast_fusion.row_ref, bf16[32,192,128]{2,1,0:T(8,128)(2,1)} %copy-done, bf16[32,192,128]{2,1,0:T(8,128)(2,1)} %collective-permute-done.7.other_ref, bf16[32,128,128]{2,1,0:T(8,128)(2,1)} %bitcast.97), custom_call_target="tpu_custom_call" | custom-call | tf_op jit(solution)/shard_map/pallas_call | solution.py:53
  104.5 3.9 %all-to-all-start.4 = ((bf16[32,24,128]{2,1,0:T(8,128)(2,1)}), bf16[32,24,128]{2,1,0:T(8,128)(2,1)S(1)}, u32[]{:S(2)}, u32[]{:S(2)}) async-start(bf16[32,24,128]{2,1,0:T(8,128)(2,1)} %convert_element_type.48), calls=%async_computation.4 | async-start | bytes 393216 | tf_op jit(solution)/shard_map/all_to_all | solution.py:145
  109.6 7.2 %all-to-all-done.4 = bf16[32,24,128]{2,1,0:T(8,128)(2,1)S(1)} async-done(((bf16[32,24,128]{2,1,0:T(8,128)(2,1)}), bf16[32,24,128]{2,1,0:T(8,128)(2,1)S(1)}, u32[]{:S(2)}, u32[]{:S(2)}) %all-to-all-start.4) | async-done | bytes 196640 | tf_op jit(solution)/shard_map/all_to_all | solution.py:145
  118.6 11.8 %all_to_all.41 = bf16[32,24,128]{2,1,0:T(8,128)(2,1)S(1)} all-to-all(bf16[32,24,128]{2,1,0:T(8,128)(2,1)S(1)} %bitcast.106), channel_id=1, replica_groups=mesh['tm'=32,'state'=8] {'tm'}, dimensions={0} | all-to-all | bytes 393216 | tf_op jit(solution)/shard_map/all_to_all | solution.py:132
  133.4 4.8 %collective-permute-done.8 = bf16[4,192,128]{2,1,0:T(8,128)(2,1)S(1)} collective-permute-done((bf16[4,192,128]{2,1,0:T(8,128)(2,1)S(1)}, bf16[4,192,128]{2,1,0:T(8,128)(2,1)S(1)}, u32[]{:S(2)}, u32[]{:S(2)}) %collective-permute-start.8) | collective-permute-done | bytes 196640 | tf_op jit(solution)/shard_map/ppermute | solution.py:121
  141.0 3.9 %collective-permute-done.10 = bf16[4,192,128]{2,1,0:T(8,128)(2,1)S(1)} collective-permute-done((bf16[4,192,128]{2,1,0:T(8,128)(2,1)S(1)}, bf16[4,192,128]{2,1,0:T(8,128)(2,1)S(1)}, u32[]{:S(2)}, u32[]{:S(2)}) %collective-permute-start.10) | collective-permute-done | bytes 196640 | tf_op jit(solution)/shard_map/ppermute | solution.py:121
  147.7 3.0 %collective-permute-done.12 = bf16[4,192,128]{2,1,0:T(8,128)(2,1)S(1)} collective-permute-done((bf16[4,192,128]{2,1,0:T(8,128)(2,1)S(1)}, bf16[4,192,128]{2,1,0:T(8,128)(2,1)S(1)}, u32[]{:S(2)}, u32[]{:S(2)}) %collective-permute-start.12) | collective-permute-done | bytes 196640 | tf_op jit(solution)/shard_map/ppermute | solution.py:121
  150.7 5.7 %collective-permute-done.14 = bf16[4,192,128]{2,1,0:T(8,128)(2,1)S(1)} collective-permute-done((bf16[4,192,128]{2,1,0:T(8,128)(2,1)S(1)}, bf16[4,192,128]{2,1,0:T(8,128)(2,1)S(1)}, u32[]{:S(2)}, u32[]{:S(2)}) %collective-permute-start.14) | collective-permute-done | bytes 196640 | tf_op jit(solution)/shard_map/ppermute | solution.py:121
  156.4 4.5 %collective-permute-start.15 = (bf16[32,192,128]{2,1,0:T(8,128)(2,1)S(1)}, bf16[32,192,128]{2,1,0:T(8,128)(2,1)S(1)}, u32[]{:S(2)}, u32[]{:S(2)}) collective-permute-start(bf16[32,192,128]{2,1,0:T(8,128)(2,1)S(1)} %constant_dynamic-update-slice_fusion.8.mine_ref), channel_id=1, source_target_pairs={{0,8},{8,0},{16,24},{24,16},{32,40},{40,32},{48,56},{56,48},{64,72... | collective-permute-start | bytes 4718600 | tf_op jit(solution)/shard_map/ppermute | solution.py:136
  160.9 3.0 %collective-permute-done.15.other_ref = bf16[32,192,128]{2,1,0:T(8,128)(2,1)S(1)} collective-permute-done((bf16[32,192,128]{2,1,0:T(8,128)(2,1)S(1)}, bf16[32,192,128]{2,1,0:T(8,128)(2,1)S(1)}, u32[]{:S(2)}, u32[]{:S(2)}) %collective-permute-start.15) | collective-permute-done | bytes 1572896 | tf_op jit(solution)/shard_map/ppermute | solution.py:136
  165.1 4.8 %shard_map.65 = f32[8,192,128]{2,1,0:T(8,128)} custom-call(s32[32]{0:T(128)} %fusion.20.pick_ref, s32[32]{0:T(128)} %compare_convert_fusion.src_ref, s32[32]{0:T(128)} %clamp_bitcast_fusion.row_ref, bf16[32,192,128]{2,1,0:T(8,128)(2,1)} %copy-done.1, bf16[32,192,128]{2,1,0:T(8,128)(2,1)} %copy-done.2, bf16[32,128,128]{2,1,0:T(8,128)(2,1)} %bitcast.98), custom_call_target="tpu_custom_call" | custom-call | tf_op jit(solution)/shard_map/pallas_call | solution.py:53
  172.1 11.7 %all_to_all.42 = bf16[32,24,128]{2,1,0:T(8,128)(2,1)S(1)} all-to-all(bf16[32,24,128]{2,1,0:T(8,128)(2,1)S(1)} %convert_element_type.52), channel_id=1, replica_groups=mesh['tm'=32,'state'=8] {'tm'}, dimensions={0} | all-to-all | bytes 393216 | tf_op jit(solution)/shard_map/all_to_all | solution.py:145
  185.2 13.8 %all_to_all.43 = f32[32,24,128]{2,1,0:T(8,128)S(1)} all-to-all(f32[32,24,128]{2,1,0:T(8,128)S(1)} %copy.61), channel_id=1, replica_groups=mesh['tm'=32,'state'=8] {'tm'}, dimensions={0} | all-to-all | bytes 786432 | tf_op jit(solution)/shard_map/all_to_all | solution.py:156
  (101 shorter events, 42.5 us)
Async XLA Ops:
  1.9 18.9 %copy-start.5 = (f32[32,32,1]{1,0,2:T(8,128)S(1)}, f32[32,32,1]{1,0,2:T(8,128)}, u32[]{:S(2)}) copy-start(f32[32,32,1]{1,0,2:T(8,128)} %constant.106) | copy-start | bytes 12292
  1.9 18.9 %all-to-all-start = ((f32[32,24,128]{2,1,0:T(8,128)}), f32[32,24,128]{2,1,0:T(8,128)S(1)}, u32[]{:S(2)}, u32[]{:S(2)}) async-start(f32[32,24,128]{2,1,0:T(8,128)} %reshape_squeeze.6), calls=%async_computation | async-start | bytes 786432 | tf_op jit(solution)/shard_map/all_to_all | solution.py:89
  34.1 10.9 %collective-permute-start = (bf16[4,192,128]{2,1,0:T(8,128)(2,1)}, bf16[4,192,128]{2,1,0:T(8,128)(2,1)S(1)}, u32[]{:S(2)}, u32[]{:S(2)}) collective-permute-start(bf16[4,192,128]{2,1,0:T(8,128)(2,1)} %get-tuple-element.15), channel_id=1, source_target_pairs={{0,1},{1,2},{2,3},{3,4},{4,5},{5,6},{6,7},{7,0},{8,9},{9,10},{10,1... | collective-permute-start | bytes 589832 | tf_op jit(solution)/shard_map/ppermute | solution.py:121
  35.7 9.3 %collective-permute-start.1 = (bf16[4,192,128]{2,1,0:T(8,128)(2,1)}, bf16[4,192,128]{2,1,0:T(8,128)(2,1)S(1)}, u32[]{:S(2)}, u32[]{:S(2)}) collective-permute-start(bf16[4,192,128]{2,1,0:T(8,128)(2,1)} %get-tuple-element.15), channel_id=1, source_target_pairs={{0,7},{1,0},{2,1},{3,2},{4,3},{5,4},{6,5},{7,6},{8,15},{9,8},{10,9... | collective-permute-start | bytes 589832 | tf_op jit(solution)/shard_map/ppermute | solution.py:124
  39.7 27.8 %all-to-all-start.2 = ((bf16[32,128,128]{2,1,0:T(8,128)(2,1)}), bf16[32,128,128]{2,1,0:T(8,128)(2,1)S(1)}, u32[]{:S(2)}, u32[]{:S(2)}) async-start(bf16[32,128,128]{2,1,0:T(8,128)(2,1)} %bitcast.2), calls=%async_computation.2 | async-start | bytes 2097152 | tf_op jit(solution)/shard_map/all_to_all | solution.py:91
  45.0 6.9 %collective-permute-start.2 = (bf16[4,192,128]{2,1,0:T(8,128)(2,1)S(1)}, bf16[4,192,128]{2,1,0:T(8,128)(2,1)S(1)}, u32[]{:S(2)}, u32[]{:S(2)}) collective-permute-start(bf16[4,192,128]{2,1,0:T(8,128)(2,1)S(1)} %collective-permute-done), channel_id=1, source_target_pairs={{0,1},{1,2},{2,3},{3,4},{4,5},{5,6},{6,7},{7,0},{8,9},{9,10},{10,1... | collective-permute-start | bytes 589832 | tf_op jit(solution)/shard_map/ppermute | solution.py:121
  45.0 6.9 %collective-permute-start.3 = (bf16[4,192,128]{2,1,0:T(8,128)(2,1)S(1)}, bf16[4,192,128]{2,1,0:T(8,128)(2,1)S(1)}, u32[]{:S(2)}, u32[]{:S(2)}) collective-permute-start(bf16[4,192,128]{2,1,0:T(8,128)(2,1)S(1)} %collective-permute-done.1), channel_id=1, source_target_pairs={{0,7},{1,0},{2,1},{3,2},{4,3},{5,4},{6,5},{7,6},{8,15},{9,8},{10,9... | collective-permute-start | bytes 589832 | tf_op jit(solution)/shard_map/ppermute | solution.py:124
  51.9 6.1 %collective-permute-start.4 = (bf16[4,192,128]{2,1,0:T(8,128)(2,1)S(1)}, bf16[4,192,128]{2,1,0:T(8,128)(2,1)S(1)}, u32[]{:S(2)}, u32[]{:S(2)}) collective-permute-start(bf16[4,192,128]{2,1,0:T(8,128)(2,1)S(1)} %collective-permute-done.2), channel_id=1, source_target_pairs={{0,1},{1,2},{2,3},{3,4},{4,5},{5,6},{6,7},{7,0},{8,9},{9,10},{10,1... | collective-permute-start | bytes 589832 | tf_op jit(solution)/shard_map/ppermute | solution.py:121
  51.9 6.1 %collective-permute-start.5 = (bf16[4,192,128]{2,1,0:T(8,128)(2,1)S(1)}, bf16[4,192,128]{2,1,0:T(8,128)(2,1)S(1)}, u32[]{:S(2)}, u32[]{:S(2)}) collective-permute-start(bf16[4,192,128]{2,1,0:T(8,128)(2,1)S(1)} %collective-permute-done.3), channel_id=1, source_target_pairs={{0,7},{1,0},{2,1},{3,2},{4,3},{5,4},{6,5},{7,6},{8,15},{9,8},{10,9... | collective-permute-start | bytes 589832 | tf_op jit(solution)/shard_map/ppermute | solution.py:124
  54.6 13.5 %copy-start.6 = (f32[2,16,32,1,1]{2,1,0,4,3:T(8,128)S(1)}, f32[2,16,32,1,1]{2,1,0,4,3:T(8,128)}, u32[]{:S(2)}) copy-start(f32[2,16,32,1,1]{2,1,0,4,3:T(8,128)} %constant.107) | copy-start | bytes 12292
  58.0 5.7 %collective-permute-start.6 = (bf16[4,192,128]{2,1,0:T(8,128)(2,1)S(1)}, bf16[4,192,128]{2,1,0:T(8,128)(2,1)S(1)}, u32[]{:S(2)}, u32[]{:S(2)}) collective-permute-start(bf16[4,192,128]{2,1,0:T(8,128)(2,1)S(1)} %collective-permute-done.4), channel_id=1, source_target_pairs={{0,1},{1,2},{2,3},{3,4},{4,5},{5,6},{6,7},{7,0},{8,9},{9,10},{10,1... | collective-permute-start | bytes 589832 | tf_op jit(solution)/shard_map/ppermute | solution.py:121
  63.8 33.1 %collective-permute-start.7 = (bf16[32,192,128]{2,1,0:T(8,128)(2,1)S(1)}, bf16[32,192,128]{2,1,0:T(8,128)(2,1)}, u32[]{:S(2)}, u32[]{:S(2)}) collective-permute-start(bf16[32,192,128]{2,1,0:T(8,128)(2,1)S(1)} %constant_dynamic-update-slice_fusion.mine_ref), channel_id=1, source_target_pairs={{0,8},{8,0},{16,24},{24,16},{32,40},{40,32},{48,56},{56,48},{64,72... | collective-permute-start | bytes 4718600 | tf_op jit(solution)/shard_map/ppermute | solution.py:136
  70.5 23.5 %all-to-all-start.3 = ((bf16[32,128,128]{2,1,0:T(8,128)(2,1)}), bf16[32,128,128]{2,1,0:T(8,128)(2,1)S(1)}, u32[]{:S(2)}, u32[]{:S(2)}) async-start(bf16[32,128,128]{2,1,0:T(8,128)(2,1)} %bitcast.20), calls=%async_computation.3 | async-start | bytes 2097152 | tf_op jit(solution)/shard_map/all_to_all | solution.py:97
  103.7 14.0 %copy-start.4 = (f32[32,32,1]{1,0,2:T(8,128)S(1)}, f32[32,32,1]{1,0,2:T(8,128)}, u32[]{:S(2)}) copy-start(f32[32,32,1]{1,0,2:T(8,128)} %constant.108) | copy-start | bytes 12292
  104.5 12.3 %all-to-all-start.4 = ((bf16[32,24,128]{2,1,0:T(8,128)(2,1)}), bf16[32,24,128]{2,1,0:T(8,128)(2,1)S(1)}, u32[]{:S(2)}, u32[]{:S(2)}) async-start(bf16[32,24,128]{2,1,0:T(8,128)(2,1)} %convert_element_type.48), calls=%async_computation.4 | async-start | bytes 393216 | tf_op jit(solution)/shard_map/all_to_all | solution.py:145
  130.7 7.6 %collective-permute-start.8 = (bf16[4,192,128]{2,1,0:T(8,128)(2,1)S(1)}, bf16[4,192,128]{2,1,0:T(8,128)(2,1)S(1)}, u32[]{:S(2)}, u32[]{:S(2)}) collective-permute-start(bf16[4,192,128]{2,1,0:T(8,128)(2,1)S(1)} %get-tuple-element.13), channel_id=1, source_target_pairs={{0,1},{1,2},{2,3},{3,4},{4,5},{5,6},{6,7},{7,0},{8,9},{9,10},{10,1... | collective-permute-start | bytes 589832 | tf_op jit(solution)/shard_map/ppermute | solution.py:121
  130.8 7.5 %collective-permute-start.9 = (bf16[4,192,128]{2,1,0:T(8,128)(2,1)S(1)}, bf16[4,192,128]{2,1,0:T(8,128)(2,1)S(1)}, u32[]{:S(2)}, u32[]{:S(2)}) collective-permute-start(bf16[4,192,128]{2,1,0:T(8,128)(2,1)S(1)} %get-tuple-element.13), channel_id=1, source_target_pairs={{0,7},{1,0},{2,1},{3,2},{4,3},{5,4},{6,5},{7,6},{8,15},{9,8},{10,9... | collective-permute-start | bytes 589832 | tf_op jit(solution)/shard_map/ppermute | solution.py:124
  138.3 6.7 %collective-permute-start.10 = (bf16[4,192,128]{2,1,0:T(8,128)(2,1)S(1)}, bf16[4,192,128]{2,1,0:T(8,128)(2,1)S(1)}, u32[]{:S(2)}, u32[]{:S(2)}) collective-permute-start(bf16[4,192,128]{2,1,0:T(8,128)(2,1)S(1)} %collective-permute-done.8), channel_id=1, source_target_pairs={{0,1},{1,2},{2,3},{3,4},{4,5},{5,6},{6,7},{7,0},{8,9},{9,10},{10,1... | collective-permute-start | bytes 589832 | tf_op jit(solution)/shard_map/ppermute | solution.py:121
  138.3 6.7 %collective-permute-start.11 = (bf16[4,192,128]{2,1,0:T(8,128)(2,1)S(1)}, bf16[4,192,128]{2,1,0:T(8,128)(2,1)S(1)}, u32[]{:S(2)}, u32[]{:S(2)}) collective-permute-start(bf16[4,192,128]{2,1,0:T(8,128)(2,1)S(1)} %collective-permute-done.9), channel_id=1, source_target_pairs={{0,7},{1,0},{2,1},{3,2},{4,3},{5,4},{6,5},{7,6},{8,15},{9,8},{10,9... | collective-permute-start | bytes 589832 | tf_op jit(solution)/shard_map/ppermute | solution.py:124
  144.9 5.7 %collective-permute-start.12 = (bf16[4,192,128]{2,1,0:T(8,128)(2,1)S(1)}, bf16[4,192,128]{2,1,0:T(8,128)(2,1)S(1)}, u32[]{:S(2)}, u32[]{:S(2)}) collective-permute-start(bf16[4,192,128]{2,1,0:T(8,128)(2,1)S(1)} %collective-permute-done.10), channel_id=1, source_target_pairs={{0,1},{1,2},{2,3},{3,4},{4,5},{5,6},{6,7},{7,0},{8,9},{9,10},{10,1... | collective-permute-start | bytes 589832 | tf_op jit(solution)/shard_map/ppermute | solution.py:121
  144.9 5.8 %collective-permute-start.13 = (bf16[4,192,128]{2,1,0:T(8,128)(2,1)S(1)}, bf16[4,192,128]{2,1,0:T(8,128)(2,1)S(1)}, u32[]{:S(2)}, u32[]{:S(2)}) collective-permute-start(bf16[4,192,128]{2,1,0:T(8,128)(2,1)S(1)} %collective-permute-done.11), channel_id=1, source_target_pairs={{0,7},{1,0},{2,1},{3,2},{4,3},{5,4},{6,5},{7,6},{8,15},{9,8},{10,9... | collective-permute-start | bytes 589832 | tf_op jit(solution)/shard_map/ppermute | solution.py:124
  150.7 5.7 %collective-permute-start.14 = (bf16[4,192,128]{2,1,0:T(8,128)(2,1)S(1)}, bf16[4,192,128]{2,1,0:T(8,128)(2,1)S(1)}, u32[]{:S(2)}, u32[]{:S(2)}) collective-permute-start(bf16[4,192,128]{2,1,0:T(8,128)(2,1)S(1)} %collective-permute-done.12), channel_id=1, source_target_pairs={{0,1},{1,2},{2,3},{3,4},{4,5},{5,6},{6,7},{7,0},{8,9},{9,10},{10,1... | collective-permute-start | bytes 589832 | tf_op jit(solution)/shard_map/ppermute | solution.py:121
  156.4 7.5 %collective-permute-start.15 = (bf16[32,192,128]{2,1,0:T(8,128)(2,1)S(1)}, bf16[32,192,128]{2,1,0:T(8,128)(2,1)S(1)}, u32[]{:S(2)}, u32[]{:S(2)}) collective-permute-start(bf16[32,192,128]{2,1,0:T(8,128)(2,1)S(1)} %constant_dynamic-update-slice_fusion.8.mine_ref), channel_id=1, source_target_pairs={{0,8},{8,0},{16,24},{24,16},{32,40},{40,32},{48,56},{56,48},{64,72... | collective-permute-start | bytes 4718600 | tf_op jit(solution)/shard_map/ppermute | solution.py:136
  171.9 12.7 %copy-start.8 = (pred[32]{0:T(512)(128)(4,1)S(1)}, pred[32]{0:T(512)(128)(4,1)}, u32[]{:S(2)}) copy-start(pred[32]{0:T(512)(128)(4,1)} %get-tuple-element.22) | copy-start | bytes 100
  (6 other events, 42.1 us)

commit v8 on v6

--- a/solution.py
+++ b/solution.py
@@ -35,7 +35,7 @@
 
     def step(k, carry):
         p = pick_ref[k]
-        x = jnp.where(src_ref[k] == 1, other_ref[p], mine_ref[p])
+        x = lax.cond(src_ref[k] == 1, lambda: other_ref[p], lambda: mine_ref[p])
         prod = lax.dot_general(
             x, kk_ref[k], (((1,), (1,)), ((), ())), preferred_element_type=jnp.float32
         )

time: 206 us -> 206 us (level)
  no operation moved by 1% of the time
where the time goes in v8:
time: 206 us; the launch traced here: 205 us
  waiting for transfers between devices  65.9 us (32%)
  blocking collectives  50.8 us (25%)
  starting transfers between devices  50.2 us (24%)
  local copies, waits for them, and re-layouts  18.1 us (9%)
  Pallas kernels  9.51 us (5%)
  other arithmetic  6.97 us (3%)
  matrix products  3.06 us (1%)
    ppermute x8, waiting for transfers between devices, ring_gather(): a = lax.ppermute(a, 'state', fwd)  31.8 us
    all_to_all x2, blocking collectives, respond(): xs = lax.all_to_all(xs, 'tm', 0, 0, tiled=True)  23.5 us
    ppermute x6, starting transfers between devices, ring_gather(): b = lax.ppermute(b, 'state', bwd)  17.3 us
    all_to_all x1, waiting for transfers between devices, shards(): kspec = lax.all_to_all(kspec, 'tm', 0, 0, tiled=True)  15.3 us
    all_to_all x1, blocking collectives, shards(): field = lax.all_to_all(field, 'tm', 0, 0, tiled=True)  13.7 us
    all_to_all x1, blocking collectives, respond(): ys = lax.all_to_all(ys, 'tm', 0, 0, tiled=True)  13.6 us
    pallas_call x2, Pallas kernels, block_products(): pl.pallas_call(_products_body, grid_spec=pltpu.PrefetchScalarGridSpec(num...  9.51 us
    all_to_all x1, waiting for transfers between devices, respond(): ys = lax.all_to_all(ys, 'tm', 0, 0, tiled=True)  9.1 us
  transfers between devices with their start and end apart: 20, of which 12 were waited for; matrix products, arithmetic and copies ran while one was open for 6% of the time, Pallas kernels for 0%

profile of v8, /device:TPU:1, one launch (start us, length us, event | category | flops | bytes accessed | tf_op | source)
XLA Modules:
  0.0 205.1 jit_solution(17654765037574332868)
XLA Ops:
  1.9 8.7 %all-to-all-start = ((f32[32,24,128]{2,1,0:T(8,128)}), f32[32,24,128]{2,1,0:T(8,128)S(1)}, u32[]{:S(2)}, u32[]{:S(2)}) async-start(f32[32,24,128]{2,1,0:T(8,128)} %reshape_squeeze.6), calls=%async_computation | async-start | bytes 786432 | tf_op jit(solution)/shard_map/all_to_all | solution.py:89
  14.1 6.7 %all-to-all-done = f32[32,24,128]{2,1,0:T(8,128)S(1)} async-done(((f32[32,24,128]{2,1,0:T(8,128)}), f32[32,24,128]{2,1,0:T(8,128)S(1)}, u32[]{:S(2)}, u32[]{:S(2)}) %all-to-all-start) | async-done | bytes 393248 | tf_op jit(solution)/shard_map/all_to_all | solution.py:89
  21.4 11.7 %all_to_all.40 = bf16[32,24,128]{2,1,0:T(8,128)(2,1)S(1)} all-to-all(bf16[32,24,128]{2,1,0:T(8,128)(2,1)S(1)} %bitcast.108), channel_id=1, replica_groups=mesh['tm'=32,'state'=8] {'tm'}, dimensions={0} | all-to-all | bytes 393216 | tf_op jit(solution)/shard_map/all_to_all | solution.py:132
  35.7 3.9 %collective-permute-start.1 = (bf16[4,192,128]{2,1,0:T(8,128)(2,1)}, bf16[4,192,128]{2,1,0:T(8,128)(2,1)S(1)}, u32[]{:S(2)}, u32[]{:S(2)}) collective-permute-start(bf16[4,192,128]{2,1,0:T(8,128)(2,1)} %get-tuple-element.15), channel_id=1, source_target_pairs={{0,7},{1,0},{2,1},{3,2},{4,3},{5,4},{6,5},{7,6},{8,15},{9,8},{10,9... | collective-permute-start | bytes 589832 | tf_op jit(solution)/shard_map/ppermute | solution.py:124
  39.7 4.1 %all-to-all-start.2 = ((bf16[32,128,128]{2,1,0:T(8,128)(2,1)}), bf16[32,128,128]{2,1,0:T(8,128)(2,1)S(1)}, u32[]{:S(2)}, u32[]{:S(2)}) async-start(bf16[32,128,128]{2,1,0:T(8,128)(2,1)} %bitcast.2), calls=%async_computation.2 | async-start | bytes 2097152 | tf_op jit(solution)/shard_map/all_to_all | solution.py:91
  47.7 4.2 %collective-permute-done.2 = bf16[4,192,128]{2,1,0:T(8,128)(2,1)S(1)} collective-permute-done((bf16[4,192,128]{2,1,0:T(8,128)(2,1)S(1)}, bf16[4,192,128]{2,1,0:T(8,128)(2,1)S(1)}, u32[]{:S(2)}, u32[]{:S(2)}) %collective-permute-start.2) | collective-permute-done | bytes 196640 | tf_op jit(solution)/shard_map/ppermute | solution.py:121
  54.7 3.3 %collective-permute-done.4 = bf16[4,192,128]{2,1,0:T(8,128)(2,1)S(1)} collective-permute-done((bf16[4,192,128]{2,1,0:T(8,128)(2,1)S(1)}, bf16[4,192,128]{2,1,0:T(8,128)(2,1)S(1)}, u32[]{:S(2)}, u32[]{:S(2)}) %collective-permute-start.4) | collective-permute-done | bytes 196640 | tf_op jit(solution)/shard_map/ppermute | solution.py:121
  58.1 5.7 %collective-permute-done.6 = bf16[4,192,128]{2,1,0:T(8,128)(2,1)S(1)} collective-permute-done((bf16[4,192,128]{2,1,0:T(8,128)(2,1)S(1)}, bf16[4,192,128]{2,1,0:T(8,128)(2,1)S(1)}, u32[]{:S(2)}, u32[]{:S(2)}) %collective-permute-start.6) | collective-permute-done | bytes 196640 | tf_op jit(solution)/shard_map/ppermute | solution.py:121
  63.8 3.7 %collective-permute-start.7 = (bf16[32,192,128]{2,1,0:T(8,128)(2,1)S(1)}, bf16[32,192,128]{2,1,0:T(8,128)(2,1)}, u32[]{:S(2)}, u32[]{:S(2)}) collective-permute-start(bf16[32,192,128]{2,1,0:T(8,128)(2,1)S(1)} %constant_dynamic-update-slice_fusion.mine_ref), channel_id=1, source_target_pairs={{0,8},{8,0},{16,24},{24,16},{32,40},{40,32},{48,56},{56,48},{64,72... | collective-permute-start | bytes 4718600 | tf_op jit(solution)/shard_map/ppermute | solution.py:136
  70.5 6.5 %all-to-all-start.3 = ((bf16[32,128,128]{2,1,0:T(8,128)(2,1)}), bf16[32,128,128]{2,1,0:T(8,128)(2,1)S(1)}, u32[]{:S(2)}, u32[]{:S(2)}) async-start(bf16[32,128,128]{2,1,0:T(8,128)(2,1)} %bitcast.20), calls=%async_computation.3 | async-start | bytes 2097152 | tf_op jit(solution)/shard_map/all_to_all | solution.py:97
  78.7 15.3 %all-to-all-done.3 = bf16[32,128,128]{2,1,0:T(8,128)(2,1)S(1)} async-done(((bf16[32,128,128]{2,1,0:T(8,128)(2,1)}), bf16[32,128,128]{2,1,0:T(8,128)(2,1)S(1)}, u32[]{:S(2)}, u32[]{:S(2)}) %all-to-all-start.3) | async-done | bytes 1048608 | tf_op jit(solution)/shard_map/all_to_all | solution.py:97
  96.9 4.8 %shard_map.64 = f32[8,192,128]{2,1,0:T(8,128)} custom-call(s32[32]{0:T(128)} %fusion.16.pick_ref, s32[32]{0:T(128)} %compare_convert_fusion.src_ref, s32[32]{0:T(128)} %clamp_bitcast_fusion.row_ref, bf16[32,192,128]{2,1,0:T(8,128)(2,1)} %copy-done, bf16[32,192,128]{2,1,0:T(8,128)(2,1)} %collective-permute-done.7.other_ref, bf16[32,128,128]{2,1,0:T(8,128)(2,1)} %bitcast.97), custom_call_target="tpu_custom_call" | custom-call | tf_op jit(solution)/shard_map/pallas_call | solution.py:53
  104.8 3.9 %all-to-all-start.4 = ((f32[32,24,128]{2,1,0:T(8,128)}), f32[32,24,128]{2,1,0:T(8,128)S(1)}, u32[]{:S(2)}, u32[]{:S(2)}) async-start(f32[32,24,128]{2,1,0:T(8,128)} %reshape.108), calls=%async_computation.4 | async-start | bytes 786432 | tf_op jit(solution)/shard_map/all_to_all | solution.py:145
  109.9 9.1 %all-to-all-done.4 = f32[32,24,128]{2,1,0:T(8,128)S(1)} async-done(((f32[32,24,128]{2,1,0:T(8,128)}), f32[32,24,128]{2,1,0:T(8,128)S(1)}, u32[]{:S(2)}, u32[]{:S(2)}) %all-to-all-start.4) | async-done | bytes 393248 | tf_op jit(solution)/shard_map/all_to_all | solution.py:145
  121.6 11.7 %all_to_all.41 = bf16[32,24,128]{2,1,0:T(8,128)(2,1)S(1)} all-to-all(bf16[32,24,128]{2,1,0:T(8,128)(2,1)S(1)} %bitcast.110), channel_id=1, replica_groups=mesh['tm'=32,'state'=8] {'tm'}, dimensions={0} | all-to-all | bytes 393216 | tf_op jit(solution)/shard_map/all_to_all | solution.py:132
  136.3 4.8 %collective-permute-done.8 = bf16[4,192,128]{2,1,0:T(8,128)(2,1)S(1)} collective-permute-done((bf16[4,192,128]{2,1,0:T(8,128)(2,1)S(1)}, bf16[4,192,128]{2,1,0:T(8,128)(2,1)S(1)}, u32[]{:S(2)}, u32[]{:S(2)}) %collective-permute-start.8) | collective-permute-done | bytes 196640 | tf_op jit(solution)/shard_map/ppermute | solution.py:121
  143.8 3.9 %collective-permute-done.10 = bf16[4,192,128]{2,1,0:T(8,128)(2,1)S(1)} collective-permute-done((bf16[4,192,128]{2,1,0:T(8,128)(2,1)S(1)}, bf16[4,192,128]{2,1,0:T(8,128)(2,1)S(1)}, u32[]{:S(2)}, u32[]{:S(2)}) %collective-permute-start.10) | collective-permute-done | bytes 196640 | tf_op jit(solution)/shard_map/ppermute | solution.py:121
  150.5 3.0 %collective-permute-done.12 = bf16[4,192,128]{2,1,0:T(8,128)(2,1)S(1)} collective-permute-done((bf16[4,192,128]{2,1,0:T(8,128)(2,1)S(1)}, bf16[4,192,128]{2,1,0:T(8,128)(2,1)S(1)}, u32[]{:S(2)}, u32[]{:S(2)}) %collective-permute-start.12) | collective-permute-done | bytes 196640 | tf_op jit(solution)/shard_map/ppermute | solution.py:121
  153.6 5.7 %collective-permute-done.14 = bf16[4,192,128]{2,1,0:T(8,128)(2,1)S(1)} collective-permute-done((bf16[4,192,128]{2,1,0:T(8,128)(2,1)S(1)}, bf16[4,192,128]{2,1,0:T(8,128)(2,1)S(1)}, u32[]{:S(2)}, u32[]{:S(2)}) %collective-permute-start.14) | collective-permute-done | bytes 196640 | tf_op jit(solution)/shard_map/ppermute | solution.py:121
  159.3 4.3 %collective-permute-start.15 = (bf16[32,192,128]{2,1,0:T(8,128)(2,1)S(1)}, bf16[32,192,128]{2,1,0:T(8,128)(2,1)S(1)}, u32[]{:S(2)}, u32[]{:S(2)}) collective-permute-start(bf16[32,192,128]{2,1,0:T(8,128)(2,1)S(1)} %constant_dynamic-update-slice_fusion.8.mine_ref), channel_id=1, source_target_pairs={{0,8},{8,0},{16,24},{24,16},{32,40},{40,32},{48,56},{56,48},{64,72... | collective-permute-start | bytes 4718600 | tf_op jit(solution)/shard_map/ppermute | solution.py:136
  163.5 3.0 %collective-permute-done.15.other_ref = bf16[32,192,128]{2,1,0:T(8,128)(2,1)S(1)} collective-permute-done((bf16[32,192,128]{2,1,0:T(8,128)(2,1)S(1)}, bf16[32,192,128]{2,1,0:T(8,128)(2,1)S(1)}, u32[]{:S(2)}, u32[]{:S(2)}) %collective-permute-start.15) | collective-permute-done | bytes 1572896 | tf_op jit(solution)/shard_map/ppermute | solution.py:136
  167.7 4.8 %shard_map.65 = f32[8,192,128]{2,1,0:T(8,128)} custom-call(s32[32]{0:T(128)} %fusion.16.pick_ref, s32[32]{0:T(128)} %compare_convert_fusion.src_ref, s32[32]{0:T(128)} %clamp_bitcast_fusion.row_ref, bf16[32,192,128]{2,1,0:T(8,128)(2,1)} %copy-done.1, bf16[32,192,128]{2,1,0:T(8,128)(2,1)} %copy-done.2, bf16[32,128,128]{2,1,0:T(8,128)(2,1)} %bitcast.98), custom_call_target="tpu_custom_call" | custom-call | tf_op jit(solution)/shard_map/pallas_call | solution.py:53
  174.9 13.6 %all_to_all.42 = f32[32,24,128]{2,1,0:T(8,128)S(1)} all-to-all(f32[32,24,128]{2,1,0:T(8,128)S(1)} %reshape.115), channel_id=1, replica_groups=mesh['tm'=32,'state'=8] {'tm'}, dimensions={0} | all-to-all | bytes 786432 | tf_op jit(solution)/shard_map/all_to_all | solution.py:145
  190.6 13.7 %all_to_all.43 = f32[32,24,128]{2,1,0:T(8,128)S(1)} all-to-all(f32[32,24,128]{2,1,0:T(8,128)S(1)} %copy.61), channel_id=1, replica_groups=mesh['tm'=32,'state'=8] {'tm'}, dimensions={0} | all-to-all | bytes 786432 | tf_op jit(solution)/shard_map/all_to_all | solution.py:156
  (101 shorter events, 44.5 us)
Async XLA Ops:
  0.0 10.6 %copy-start.3 = (bf16[32,1,128,128]{3,2,1,0:T(8,128)(2,1)S(1)}, bf16[32,1,128,128]{3,2,1,0:T(8,128)(2,1)}, u32[]{:S(2)}) copy-start(bf16[32,1,128,128]{3,2,1,0:T(8,128)(2,1)} %param.7) | copy-start | bytes 3145732
  1.9 10.9 %copy-start.7 = (s32[2]{0:T(128)S(1)}, s32[2]{0:T(128)}, u32[]{:S(2)}) copy-start(s32[2]{0:T(128)} %param.9) | copy-start | bytes 28
  1.9 18.9 %copy-start.5 = (f32[32,32,1]{1,0,2:T(8,128)S(1)}, f32[32,32,1]{1,0,2:T(8,128)}, u32[]{:S(2)}) copy-start(f32[32,32,1]{1,0,2:T(8,128)} %constant.106) | copy-start | bytes 12292
  1.9 18.9 %all-to-all-start = ((f32[32,24,128]{2,1,0:T(8,128)}), f32[32,24,128]{2,1,0:T(8,128)S(1)}, u32[]{:S(2)}, u32[]{:S(2)}) async-start(f32[32,24,128]{2,1,0:T(8,128)} %reshape_squeeze.6), calls=%async_computation | async-start | bytes 786432 | tf_op jit(solution)/shard_map/all_to_all | solution.py:89
  34.1 10.9 %collective-permute-start = (bf16[4,192,128]{2,1,0:T(8,128)(2,1)}, bf16[4,192,128]{2,1,0:T(8,128)(2,1)S(1)}, u32[]{:S(2)}, u32[]{:S(2)}) collective-permute-start(bf16[4,192,128]{2,1,0:T(8,128)(2,1)} %get-tuple-element.15), channel_id=1, source_target_pairs={{0,1},{1,2},{2,3},{3,4},{4,5},{5,6},{6,7},{7,0},{8,9},{9,10},{10,1... | collective-permute-start | bytes 589832 | tf_op jit(solution)/shard_map/ppermute | solution.py:121
  35.7 9.3 %collective-permute-start.1 = (bf16[4,192,128]{2,1,0:T(8,128)(2,1)}, bf16[4,192,128]{2,1,0:T(8,128)(2,1)S(1)}, u32[]{:S(2)}, u32[]{:S(2)}) collective-permute-start(bf16[4,192,128]{2,1,0:T(8,128)(2,1)} %get-tuple-element.15), channel_id=1, source_target_pairs={{0,7},{1,0},{2,1},{3,2},{4,3},{5,4},{6,5},{7,6},{8,15},{9,8},{10,9... | collective-permute-start | bytes 589832 | tf_op jit(solution)/shard_map/ppermute | solution.py:124
  39.7 27.8 %all-to-all-start.2 = ((bf16[32,128,128]{2,1,0:T(8,128)(2,1)}), bf16[32,128,128]{2,1,0:T(8,128)(2,1)S(1)}, u32[]{:S(2)}, u32[]{:S(2)}) async-start(bf16[32,128,128]{2,1,0:T(8,128)(2,1)} %bitcast.2), calls=%async_computation.2 | async-start | bytes 2097152 | tf_op jit(solution)/shard_map/all_to_all | solution.py:91
  45.0 6.9 %collective-permute-start.2 = (bf16[4,192,128]{2,1,0:T(8,128)(2,1)S(1)}, bf16[4,192,128]{2,1,0:T(8,128)(2,1)S(1)}, u32[]{:S(2)}, u32[]{:S(2)}) collective-permute-start(bf16[4,192,128]{2,1,0:T(8,128)(2,1)S(1)} %collective-permute-done), channel_id=1, source_target_pairs={{0,1},{1,2},{2,3},{3,4},{4,5},{5,6},{6,7},{7,0},{8,9},{9,10},{10,1... | collective-permute-start | bytes 589832 | tf_op jit(solution)/shard_map/ppermute | solution.py:121
  45.0 6.9 %collective-permute-start.3 = (bf16[4,192,128]{2,1,0:T(8,128)(2,1)S(1)}, bf16[4,192,128]{2,1,0:T(8,128)(2,1)S(1)}, u32[]{:S(2)}, u32[]{:S(2)}) collective-permute-start(bf16[4,192,128]{2,1,0:T(8,128)(2,1)S(1)} %collective-permute-done.1), channel_id=1, source_target_pairs={{0,7},{1,0},{2,1},{3,2},{4,3},{5,4},{6,5},{7,6},{8,15},{9,8},{10,9... | collective-permute-start | bytes 589832 | tf_op jit(solution)/shard_map/ppermute | solution.py:124
  51.9 6.1 %collective-permute-start.4 = (bf16[4,192,128]{2,1,0:T(8,128)(2,1)S(1)}, bf16[4,192,128]{2,1,0:T(8,128)(2,1)S(1)}, u32[]{:S(2)}, u32[]{:S(2)}) collective-permute-start(bf16[4,192,128]{2,1,0:T(8,128)(2,1)S(1)} %collective-permute-done.2), channel_id=1, source_target_pairs={{0,1},{1,2},{2,3},{3,4},{4,5},{5,6},{6,7},{7,0},{8,9},{9,10},{10,1... | collective-permute-start | bytes 589832 | tf_op jit(solution)/shard_map/ppermute | solution.py:121
  51.9 6.1 %collective-permute-start.5 = (bf16[4,192,128]{2,1,0:T(8,128)(2,1)S(1)}, bf16[4,192,128]{2,1,0:T(8,128)(2,1)S(1)}, u32[]{:S(2)}, u32[]{:S(2)}) collective-permute-start(bf16[4,192,128]{2,1,0:T(8,128)(2,1)S(1)} %collective-permute-done.3), channel_id=1, source_target_pairs={{0,7},{1,0},{2,1},{3,2},{4,3},{5,4},{6,5},{7,6},{8,15},{9,8},{10,9... | collective-permute-start | bytes 589832 | tf_op jit(solution)/shard_map/ppermute | solution.py:124
  54.6 13.5 %copy-start.6 = (f32[2,16,32,1,1]{2,1,0,4,3:T(8,128)S(1)}, f32[2,16,32,1,1]{2,1,0,4,3:T(8,128)}, u32[]{:S(2)}) copy-start(f32[2,16,32,1,1]{2,1,0,4,3:T(8,128)} %constant.107) | copy-start | bytes 12292
  58.0 5.7 %collective-permute-start.6 = (bf16[4,192,128]{2,1,0:T(8,128)(2,1)S(1)}, bf16[4,192,128]{2,1,0:T(8,128)(2,1)S(1)}, u32[]{:S(2)}, u32[]{:S(2)}) collective-permute-start(bf16[4,192,128]{2,1,0:T(8,128)(2,1)S(1)} %collective-permute-done.4), channel_id=1, source_target_pairs={{0,1},{1,2},{2,3},{3,4},{4,5},{5,6},{6,7},{7,0},{8,9},{9,10},{10,1... | collective-permute-start | bytes 589832 | tf_op jit(solution)/shard_map/ppermute | solution.py:121
  63.8 33.1 %collective-permute-start.7 = (bf16[32,192,128]{2,1,0:T(8,128)(2,1)S(1)}, bf16[32,192,128]{2,1,0:T(8,128)(2,1)}, u32[]{:S(2)}, u32[]{:S(2)}) collective-permute-start(bf16[32,192,128]{2,1,0:T(8,128)(2,1)S(1)} %constant_dynamic-update-slice_fusion.mine_ref), channel_id=1, source_target_pairs={{0,8},{8,0},{16,24},{24,16},{32,40},{40,32},{48,56},{56,48},{64,72... | collective-permute-start | bytes 4718600 | tf_op jit(solution)/shard_map/ppermute | solution.py:136
  70.5 23.5 %all-to-all-start.3 = ((bf16[32,128,128]{2,1,0:T(8,128)(2,1)}), bf16[32,128,128]{2,1,0:T(8,128)(2,1)S(1)}, u32[]{:S(2)}, u32[]{:S(2)}) async-start(bf16[32,128,128]{2,1,0:T(8,128)(2,1)} %bitcast.20), calls=%async_computation.3 | async-start | bytes 2097152 | tf_op jit(solution)/shard_map/all_to_all | solution.py:97
  104.8 14.2 %all-to-all-start.4 = ((f32[32,24,128]{2,1,0:T(8,128)}), f32[32,24,128]{2,1,0:T(8,128)S(1)}, u32[]{:S(2)}, u32[]{:S(2)}) async-start(f32[32,24,128]{2,1,0:T(8,128)} %reshape.108), calls=%async_computation.4 | async-start | bytes 786432 | tf_op jit(solution)/shard_map/all_to_all | solution.py:145
  133.5 7.6 %collective-permute-start.8 = (bf16[4,192,128]{2,1,0:T(8,128)(2,1)S(1)}, bf16[4,192,128]{2,1,0:T(8,128)(2,1)S(1)}, u32[]{:S(2)}, u32[]{:S(2)}) collective-permute-start(bf16[4,192,128]{2,1,0:T(8,128)(2,1)S(1)} %get-tuple-element.13), channel_id=1, source_target_pairs={{0,1},{1,2},{2,3},{3,4},{4,5},{5,6},{6,7},{7,0},{8,9},{9,10},{10,1... | collective-permute-start | bytes 589832 | tf_op jit(solution)/shard_map/ppermute | solution.py:121
  133.6 7.5 %collective-permute-start.9 = (bf16[4,192,128]{2,1,0:T(8,128)(2,1)S(1)}, bf16[4,192,128]{2,1,0:T(8,128)(2,1)S(1)}, u32[]{:S(2)}, u32[]{:S(2)}) collective-permute-start(bf16[4,192,128]{2,1,0:T(8,128)(2,1)S(1)} %get-tuple-element.13), channel_id=1, source_target_pairs={{0,7},{1,0},{2,1},{3,2},{4,3},{5,4},{6,5},{7,6},{8,15},{9,8},{10,9... | collective-permute-start | bytes 589832 | tf_op jit(solution)/shard_map/ppermute | solution.py:124
  141.1 6.7 %collective-permute-start.10 = (bf16[4,192,128]{2,1,0:T(8,128)(2,1)S(1)}, bf16[4,192,128]{2,1,0:T(8,128)(2,1)S(1)}, u32[]{:S(2)}, u32[]{:S(2)}) collective-permute-start(bf16[4,192,128]{2,1,0:T(8,128)(2,1)S(1)} %collective-permute-done.8), channel_id=1, source_target_pairs={{0,1},{1,2},{2,3},{3,4},{4,5},{5,6},{6,7},{7,0},{8,9},{9,10},{10,1... | collective-permute-start | bytes 589832 | tf_op jit(solution)/shard_map/ppermute | solution.py:121
  141.1 6.7 %collective-permute-start.11 = (bf16[4,192,128]{2,1,0:T(8,128)(2,1)S(1)}, bf16[4,192,128]{2,1,0:T(8,128)(2,1)S(1)}, u32[]{:S(2)}, u32[]{:S(2)}) collective-permute-start(bf16[4,192,128]{2,1,0:T(8,128)(2,1)S(1)} %collective-permute-done.9), channel_id=1, source_target_pairs={{0,7},{1,0},{2,1},{3,2},{4,3},{5,4},{6,5},{7,6},{8,15},{9,8},{10,9... | collective-permute-start | bytes 589832 | tf_op jit(solution)/shard_map/ppermute | solution.py:124
  147.7 5.7 %collective-permute-start.12 = (bf16[4,192,128]{2,1,0:T(8,128)(2,1)S(1)}, bf16[4,192,128]{2,1,0:T(8,128)(2,1)S(1)}, u32[]{:S(2)}, u32[]{:S(2)}) collective-permute-start(bf16[4,192,128]{2,1,0:T(8,128)(2,1)S(1)} %collective-permute-done.10), channel_id=1, source_target_pairs={{0,1},{1,2},{2,3},{3,4},{4,5},{5,6},{6,7},{7,0},{8,9},{9,10},{10,1... | collective-permute-start | bytes 589832 | tf_op jit(solution)/shard_map/ppermute | solution.py:121
  147.8 5.8 %collective-permute-start.13 = (bf16[4,192,128]{2,1,0:T(8,128)(2,1)S(1)}, bf16[4,192,128]{2,1,0:T(8,128)(2,1)S(1)}, u32[]{:S(2)}, u32[]{:S(2)}) collective-permute-start(bf16[4,192,128]{2,1,0:T(8,128)(2,1)S(1)} %collective-permute-done.11), channel_id=1, source_target_pairs={{0,7},{1,0},{2,1},{3,2},{4,3},{5,4},{6,5},{7,6},{8,15},{9,8},{10,9... | collective-permute-start | bytes 589832 | tf_op jit(solution)/shard_map/ppermute | solution.py:124
  153.5 5.7 %collective-permute-start.14 = (bf16[4,192,128]{2,1,0:T(8,128)(2,1)S(1)}, bf16[4,192,128]{2,1,0:T(8,128)(2,1)S(1)}, u32[]{:S(2)}, u32[]{:S(2)}) collective-permute-start(bf16[4,192,128]{2,1,0:T(8,128)(2,1)S(1)} %collective-permute-done.12), channel_id=1, source_target_pairs={{0,1},{1,2},{2,3},{3,4},{4,5},{5,6},{6,7},{7,0},{8,9},{9,10},{10,1... | collective-permute-start | bytes 589832 | tf_op jit(solution)/shard_map/ppermute | solution.py:121
  159.3 7.3 %collective-permute-start.15 = (bf16[32,192,128]{2,1,0:T(8,128)(2,1)S(1)}, bf16[32,192,128]{2,1,0:T(8,128)(2,1)S(1)}, u32[]{:S(2)}, u32[]{:S(2)}) collective-permute-start(bf16[32,192,128]{2,1,0:T(8,128)(2,1)S(1)} %constant_dynamic-update-slice_fusion.8.mine_ref), channel_id=1, source_target_pairs={{0,8},{8,0},{16,24},{24,16},{32,40},{40,32},{48,56},{56,48},{64,72... | collective-permute-start | bytes 4718600 | tf_op jit(solution)/shard_map/ppermute | solution.py:136
  (6 other events, 22.1 us)

commit v9 on v6

--- a/solution.py
+++ b/solution.py
@@ -43,7 +43,7 @@
         out_ref[r] = out_ref[r] + prod
         return carry
 
-    lax.fori_loop(0, kk_ref.shape[0], step, 0, unroll=16)
+    lax.fori_loop(0, kk_ref.shape[0], step, 0, unroll=True)
 
 
 def block_products(pick, src, row, mine, other, kk, rows_local):

time: 206 us -> 206 us (level)
  no operation moved by 1% of the time
where the time goes in v9:
time: 206 us; the launch traced here: 205 us
  waiting for transfers between devices  65.9 us (32%)
  blocking collectives  50.8 us (25%)
  starting transfers between devices  50.2 us (24%)
  local copies, waits for them, and re-layouts  18.1 us (9%)
  Pallas kernels  9.17 us (4%)
  other arithmetic  6.97 us (3%)
  matrix products  3.06 us (1%)
    ppermute x8, waiting for transfers between devices, ring_gather(): a = lax.ppermute(a, 'state', fwd)  31.8 us
    all_to_all x2, blocking collectives, respond(): xs = lax.all_to_all(xs, 'tm', 0, 0, tiled=True)  23.5 us
    ppermute x6, starting transfers between devices, ring_gather(): b = lax.ppermute(b, 'state', bwd)  17.3 us
    all_to_all x1, waiting for transfers between devices, shards(): kspec = lax.all_to_all(kspec, 'tm', 0, 0, tiled=True)  15.3 us
    all_to_all x1, blocking collectives, shards(): field = lax.all_to_all(field, 'tm', 0, 0, tiled=True)  13.7 us
    all_to_all x1, blocking collectives, respond(): ys = lax.all_to_all(ys, 'tm', 0, 0, tiled=True)  13.6 us
    pallas_call x2, Pallas kernels, block_products(): pl.pallas_call(_products_body, grid_spec=pltpu.PrefetchScalarGridSpec(num...  9.17 us
    all_to_all x1, waiting for transfers between devices, respond(): ys = lax.all_to_all(ys, 'tm', 0, 0, tiled=True)  9.1 us
  transfers between devices with their start and end apart: 20, of which 12 were waited for; matrix products, arithmetic and copies ran while one was open for 6% of the time, Pallas kernels for 0%

profile of v9, /device:TPU:1, one launch (start us, length us, event | category | flops | bytes accessed | tf_op | source)
XLA Modules:
  0.0 204.7 jit_solution(16132979632076005622)
XLA Ops:
  1.9 8.7 %all-to-all-start = ((f32[32,24,128]{2,1,0:T(8,128)}), f32[32,24,128]{2,1,0:T(8,128)S(1)}, u32[]{:S(2)}, u32[]{:S(2)}) async-start(f32[32,24,128]{2,1,0:T(8,128)} %reshape_squeeze.6), calls=%async_computation | async-start | bytes 786432 | tf_op jit(solution)/shard_map/all_to_all | solution.py:89
  14.1 6.7 %all-to-all-done = f32[32,24,128]{2,1,0:T(8,128)S(1)} async-done(((f32[32,24,128]{2,1,0:T(8,128)}), f32[32,24,128]{2,1,0:T(8,128)S(1)}, u32[]{:S(2)}, u32[]{:S(2)}) %all-to-all-start) | async-done | bytes 393248 | tf_op jit(solution)/shard_map/all_to_all | solution.py:89
  21.4 11.7 %all_to_all.40 = bf16[32,24,128]{2,1,0:T(8,128)(2,1)S(1)} all-to-all(bf16[32,24,128]{2,1,0:T(8,128)(2,1)S(1)} %bitcast.108), channel_id=1, replica_groups=mesh['tm'=32,'state'=8] {'tm'}, dimensions={0} | all-to-all | bytes 393216 | tf_op jit(solution)/shard_map/all_to_all | solution.py:132
  35.7 3.9 %collective-permute-start.1 = (bf16[4,192,128]{2,1,0:T(8,128)(2,1)}, bf16[4,192,128]{2,1,0:T(8,128)(2,1)S(1)}, u32[]{:S(2)}, u32[]{:S(2)}) collective-permute-start(bf16[4,192,128]{2,1,0:T(8,128)(2,1)} %get-tuple-element.15), channel_id=1, source_target_pairs={{0,7},{1,0},{2,1},{3,2},{4,3},{5,4},{6,5},{7,6},{8,15},{9,8},{10,9... | collective-permute-start | bytes 589832 | tf_op jit(solution)/shard_map/ppermute | solution.py:124
  39.7 4.1 %all-to-all-start.2 = ((bf16[32,128,128]{2,1,0:T(8,128)(2,1)}), bf16[32,128,128]{2,1,0:T(8,128)(2,1)S(1)}, u32[]{:S(2)}, u32[]{:S(2)}) async-start(bf16[32,128,128]{2,1,0:T(8,128)(2,1)} %bitcast.2), calls=%async_computation.2 | async-start | bytes 2097152 | tf_op jit(solution)/shard_map/all_to_all | solution.py:91
  47.7 4.2 %collective-permute-done.2 = bf16[4,192,128]{2,1,0:T(8,128)(2,1)S(1)} collective-permute-done((bf16[4,192,128]{2,1,0:T(8,128)(2,1)S(1)}, bf16[4,192,128]{2,1,0:T(8,128)(2,1)S(1)}, u32[]{:S(2)}, u32[]{:S(2)}) %collective-permute-start.2) | collective-permute-done | bytes 196640 | tf_op jit(solution)/shard_map/ppermute | solution.py:121
  54.7 3.3 %collective-permute-done.4 = bf16[4,192,128]{2,1,0:T(8,128)(2,1)S(1)} collective-permute-done((bf16[4,192,128]{2,1,0:T(8,128)(2,1)S(1)}, bf16[4,192,128]{2,1,0:T(8,128)(2,1)S(1)}, u32[]{:S(2)}, u32[]{:S(2)}) %collective-permute-start.4) | collective-permute-done | bytes 196640 | tf_op jit(solution)/shard_map/ppermute | solution.py:121
  58.1 5.7 %collective-permute-done.6 = bf16[4,192,128]{2,1,0:T(8,128)(2,1)S(1)} collective-permute-done((bf16[4,192,128]{2,1,0:T(8,128)(2,1)S(1)}, bf16[4,192,128]{2,1,0:T(8,128)(2,1)S(1)}, u32[]{:S(2)}, u32[]{:S(2)}) %collective-permute-start.6) | collective-permute-done | bytes 196640 | tf_op jit(solution)/shard_map/ppermute | solution.py:121
  63.8 3.7 %collective-permute-start.7 = (bf16[32,192,128]{2,1,0:T(8,128)(2,1)S(1)}, bf16[32,192,128]{2,1,0:T(8,128)(2,1)}, u32[]{:S(2)}, u32[]{:S(2)}) collective-permute-start(bf16[32,192,128]{2,1,0:T(8,128)(2,1)S(1)} %constant_dynamic-update-slice_fusion.mine_ref), channel_id=1, source_target_pairs={{0,8},{8,0},{16,24},{24,16},{32,40},{40,32},{48,56},{56,48},{64,72... | collective-permute-start | bytes 4718600 | tf_op jit(solution)/shard_map/ppermute | solution.py:136
  70.5 6.5 %all-to-all-start.3 = ((bf16[32,128,128]{2,1,0:T(8,128)(2,1)}), bf16[32,128,128]{2,1,0:T(8,128)(2,1)S(1)}, u32[]{:S(2)}, u32[]{:S(2)}) async-start(bf16[32,128,128]{2,1,0:T(8,128)(2,1)} %bitcast.20), calls=%async_computation.3 | async-start | bytes 2097152 | tf_op jit(solution)/shard_map/all_to_all | solution.py:97
  78.7 15.3 %all-to-all-done.3 = bf16[32,128,128]{2,1,0:T(8,128)(2,1)S(1)} async-done(((bf16[32,128,128]{2,1,0:T(8,128)(2,1)}), bf16[32,128,128]{2,1,0:T(8,128)(2,1)S(1)}, u32[]{:S(2)}, u32[]{:S(2)}) %all-to-all-start.3) | async-done | bytes 1048608 | tf_op jit(solution)/shard_map/all_to_all | solution.py:97
  96.9 4.6 %shard_map.64 = f32[8,192,128]{2,1,0:T(8,128)} custom-call(s32[32]{0:T(128)} %fusion.16.pick_ref, s32[32]{0:T(128)} %compare_convert_fusion.src_ref, s32[32]{0:T(128)} %clamp_bitcast_fusion.row_ref, bf16[32,192,128]{2,1,0:T(8,128)(2,1)} %copy-done, bf16[32,192,128]{2,1,0:T(8,128)(2,1)} %collective-permute-done.7.other_ref, bf16[32,128,128]{2,1,0:T(8,128)(2,1)} %bitcast.97), custom_call_target="tpu_custom_call" | custom-call | tf_op jit(solution)/shard_map/pallas_call | solution.py:53
  104.7 3.9 %all-to-all-start.4 = ((f32[32,24,128]{2,1,0:T(8,128)}), f32[32,24,128]{2,1,0:T(8,128)S(1)}, u32[]{:S(2)}, u32[]{:S(2)}) async-start(f32[32,24,128]{2,1,0:T(8,128)} %reshape.108), calls=%async_computation.4 | async-start | bytes 786432 | tf_op jit(solution)/shard_map/all_to_all | solution.py:145
  109.7 9.1 %all-to-all-done.4 = f32[32,24,128]{2,1,0:T(8,128)S(1)} async-done(((f32[32,24,128]{2,1,0:T(8,128)}), f32[32,24,128]{2,1,0:T(8,128)S(1)}, u32[]{:S(2)}, u32[]{:S(2)}) %all-to-all-start.4) | async-done | bytes 393248 | tf_op jit(solution)/shard_map/all_to_all | solution.py:145
  121.4 11.7 %all_to_all.41 = bf16[32,24,128]{2,1,0:T(8,128)(2,1)S(1)} all-to-all(bf16[32,24,128]{2,1,0:T(8,128)(2,1)S(1)} %bitcast.110), channel_id=1, replica_groups=mesh['tm'=32,'state'=8] {'tm'}, dimensions={0} | all-to-all | bytes 393216 | tf_op jit(solution)/shard_map/all_to_all | solution.py:132
  136.1 4.8 %collective-permute-done.8 = bf16[4,192,128]{2,1,0:T(8,128)(2,1)S(1)} collective-permute-done((bf16[4,192,128]{2,1,0:T(8,128)(2,1)S(1)}, bf16[4,192,128]{2,1,0:T(8,128)(2,1)S(1)}, u32[]{:S(2)}, u32[]{:S(2)}) %collective-permute-start.8) | collective-permute-done | bytes 196640 | tf_op jit(solution)/shard_map/ppermute | solution.py:121
  143.7 3.9 %collective-permute-done.10 = bf16[4,192,128]{2,1,0:T(8,128)(2,1)S(1)} collective-permute-done((bf16[4,192,128]{2,1,0:T(8,128)(2,1)S(1)}, bf16[4,192,128]{2,1,0:T(8,128)(2,1)S(1)}, u32[]{:S(2)}, u32[]{:S(2)}) %collective-permute-start.10) | collective-permute-done | bytes 196640 | tf_op jit(solution)/shard_map/ppermute | solution.py:121
  150.3 3.0 %collective-permute-done.12 = bf16[4,192,128]{2,1,0:T(8,128)(2,1)S(1)} collective-permute-done((bf16[4,192,128]{2,1,0:T(8,128)(2,1)S(1)}, bf16[4,192,128]{2,1,0:T(8,128)(2,1)S(1)}, u32[]{:S(2)}, u32[]{:S(2)}) %collective-permute-start.12) | collective-permute-done | bytes 196640 | tf_op jit(solution)/shard_map/ppermute | solution.py:121
  153.4 5.7 %collective-permute-done.14 = bf16[4,192,128]{2,1,0:T(8,128)(2,1)S(1)} collective-permute-done((bf16[4,192,128]{2,1,0:T(8,128)(2,1)S(1)}, bf16[4,192,128]{2,1,0:T(8,128)(2,1)S(1)}, u32[]{:S(2)}, u32[]{:S(2)}) %collective-permute-start.14) | collective-permute-done | bytes 196640 | tf_op jit(solution)/shard_map/ppermute | solution.py:121
  159.1 4.3 %collective-permute-start.15 = (bf16[32,192,128]{2,1,0:T(8,128)(2,1)S(1)}, bf16[32,192,128]{2,1,0:T(8,128)(2,1)S(1)}, u32[]{:S(2)}, u32[]{:S(2)}) collective-permute-start(bf16[32,192,128]{2,1,0:T(8,128)(2,1)S(1)} %constant_dynamic-update-slice_fusion.8.mine_ref), channel_id=1, source_target_pairs={{0,8},{8,0},{16,24},{24,16},{32,40},{40,32},{48,56},{56,48},{64,72... | collective-permute-start | bytes 4718600 | tf_op jit(solution)/shard_map/ppermute | solution.py:136
  163.3 3.0 %collective-permute-done.15.other_ref = bf16[32,192,128]{2,1,0:T(8,128)(2,1)S(1)} collective-permute-done((bf16[32,192,128]{2,1,0:T(8,128)(2,1)S(1)}, bf16[32,192,128]{2,1,0:T(8,128)(2,1)S(1)}, u32[]{:S(2)}, u32[]{:S(2)}) %collective-permute-start.15) | collective-permute-done | bytes 1572896 | tf_op jit(solution)/shard_map/ppermute | solution.py:136
  167.5 4.6 %shard_map.65 = f32[8,192,128]{2,1,0:T(8,128)} custom-call(s32[32]{0:T(128)} %fusion.16.pick_ref, s32[32]{0:T(128)} %compare_convert_fusion.src_ref, s32[32]{0:T(128)} %clamp_bitcast_fusion.row_ref, bf16[32,192,128]{2,1,0:T(8,128)(2,1)} %copy-done.1, bf16[32,192,128]{2,1,0:T(8,128)(2,1)} %copy-done.2, bf16[32,128,128]{2,1,0:T(8,128)(2,1)} %bitcast.98), custom_call_target="tpu_custom_call" | custom-call | tf_op jit(solution)/shard_map/pallas_call | solution.py:53
  174.6 13.6 %all_to_all.42 = f32[32,24,128]{2,1,0:T(8,128)S(1)} all-to-all(f32[32,24,128]{2,1,0:T(8,128)S(1)} %reshape.115), channel_id=1, replica_groups=mesh['tm'=32,'state'=8] {'tm'}, dimensions={0} | all-to-all | bytes 786432 | tf_op jit(solution)/shard_map/all_to_all | solution.py:145
  190.3 13.7 %all_to_all.43 = f32[32,24,128]{2,1,0:T(8,128)S(1)} all-to-all(f32[32,24,128]{2,1,0:T(8,128)S(1)} %copy.61), channel_id=1, replica_groups=mesh['tm'=32,'state'=8] {'tm'}, dimensions={0} | all-to-all | bytes 786432 | tf_op jit(solution)/shard_map/all_to_all | solution.py:156
  (101 shorter events, 44.5 us)
Async XLA Ops:
  0.0 10.6 %copy-start.3 = (bf16[32,1,128,128]{3,2,1,0:T(8,128)(2,1)S(1)}, bf16[32,1,128,128]{3,2,1,0:T(8,128)(2,1)}, u32[]{:S(2)}) copy-start(bf16[32,1,128,128]{3,2,1,0:T(8,128)(2,1)} %param.7) | copy-start | bytes 3145732
  1.9 10.9 %copy-start.7 = (s32[2]{0:T(128)S(1)}, s32[2]{0:T(128)}, u32[]{:S(2)}) copy-start(s32[2]{0:T(128)} %param.9) | copy-start | bytes 28
  1.9 18.9 %copy-start.5 = (f32[32,32,1]{1,0,2:T(8,128)S(1)}, f32[32,32,1]{1,0,2:T(8,128)}, u32[]{:S(2)}) copy-start(f32[32,32,1]{1,0,2:T(8,128)} %constant.106) | copy-start | bytes 12292
  1.9 18.9 %all-to-all-start = ((f32[32,24,128]{2,1,0:T(8,128)}), f32[32,24,128]{2,1,0:T(8,128)S(1)}, u32[]{:S(2)}, u32[]{:S(2)}) async-start(f32[32,24,128]{2,1,0:T(8,128)} %reshape_squeeze.6), calls=%async_computation | async-start | bytes 786432 | tf_op jit(solution)/shard_map/all_to_all | solution.py:89
  34.1 10.9 %collective-permute-start = (bf16[4,192,128]{2,1,0:T(8,128)(2,1)}, bf16[4,192,128]{2,1,0:T(8,128)(2,1)S(1)}, u32[]{:S(2)}, u32[]{:S(2)}) collective-permute-start(bf16[4,192,128]{2,1,0:T(8,128)(2,1)} %get-tuple-element.15), channel_id=1, source_target_pairs={{0,1},{1,2},{2,3},{3,4},{4,5},{5,6},{6,7},{7,0},{8,9},{9,10},{10,1... | collective-permute-start | bytes 589832 | tf_op jit(solution)/shard_map/ppermute | solution.py:121
  35.7 9.3 %collective-permute-start.1 = (bf16[4,192,128]{2,1,0:T(8,128)(2,1)}, bf16[4,192,128]{2,1,0:T(8,128)(2,1)S(1)}, u32[]{:S(2)}, u32[]{:S(2)}) collective-permute-start(bf16[4,192,128]{2,1,0:T(8,128)(2,1)} %get-tuple-element.15), channel_id=1, source_target_pairs={{0,7},{1,0},{2,1},{3,2},{4,3},{5,4},{6,5},{7,6},{8,15},{9,8},{10,9... | collective-permute-start | bytes 589832 | tf_op jit(solution)/shard_map/ppermute | solution.py:124
  39.7 27.8 %all-to-all-start.2 = ((bf16[32,128,128]{2,1,0:T(8,128)(2,1)}), bf16[32,128,128]{2,1,0:T(8,128)(2,1)S(1)}, u32[]{:S(2)}, u32[]{:S(2)}) async-start(bf16[32,128,128]{2,1,0:T(8,128)(2,1)} %bitcast.2), calls=%async_computation.2 | async-start | bytes 2097152 | tf_op jit(solution)/shard_map/all_to_all | solution.py:91
  45.0 6.9 %collective-permute-start.2 = (bf16[4,192,128]{2,1,0:T(8,128)(2,1)S(1)}, bf16[4,192,128]{2,1,0:T(8,128)(2,1)S(1)}, u32[]{:S(2)}, u32[]{:S(2)}) collective-permute-start(bf16[4,192,128]{2,1,0:T(8,128)(2,1)S(1)} %collective-permute-done), channel_id=1, source_target_pairs={{0,1},{1,2},{2,3},{3,4},{4,5},{5,6},{6,7},{7,0},{8,9},{9,10},{10,1... | collective-permute-start | bytes 589832 | tf_op jit(solution)/shard_map/ppermute | solution.py:121
  45.0 6.9 %collective-permute-start.3 = (bf16[4,192,128]{2,1,0:T(8,128)(2,1)S(1)}, bf16[4,192,128]{2,1,0:T(8,128)(2,1)S(1)}, u32[]{:S(2)}, u32[]{:S(2)}) collective-permute-start(bf16[4,192,128]{2,1,0:T(8,128)(2,1)S(1)} %collective-permute-done.1), channel_id=1, source_target_pairs={{0,7},{1,0},{2,1},{3,2},{4,3},{5,4},{6,5},{7,6},{8,15},{9,8},{10,9... | collective-permute-start | bytes 589832 | tf_op jit(solution)/shard_map/ppermute | solution.py:124
  51.9 6.1 %collective-permute-start.4 = (bf16[4,192,128]{2,1,0:T(8,128)(2,1)S(1)}, bf16[4,192,128]{2,1,0:T(8,128)(2,1)S(1)}, u32[]{:S(2)}, u32[]{:S(2)}) collective-permute-start(bf16[4,192,128]{2,1,0:T(8,128)(2,1)S(1)} %collective-permute-done.2), channel_id=1, source_target_pairs={{0,1},{1,2},{2,3},{3,4},{4,5},{5,6},{6,7},{7,0},{8,9},{9,10},{10,1... | collective-permute-start | bytes 589832 | tf_op jit(solution)/shard_map/ppermute | solution.py:121
  51.9 6.1 %collective-permute-start.5 = (bf16[4,192,128]{2,1,0:T(8,128)(2,1)S(1)}, bf16[4,192,128]{2,1,0:T(8,128)(2,1)S(1)}, u32[]{:S(2)}, u32[]{:S(2)}) collective-permute-start(bf16[4,192,128]{2,1,0:T(8,128)(2,1)S(1)} %collective-permute-done.3), channel_id=1, source_target_pairs={{0,7},{1,0},{2,1},{3,2},{4,3},{5,4},{6,5},{7,6},{8,15},{9,8},{10,9... | collective-permute-start | bytes 589832 | tf_op jit(solution)/shard_map/ppermute | solution.py:124
  54.6 13.5 %copy-start.6 = (f32[2,16,32,1,1]{2,1,0,4,3:T(8,128)S(1)}, f32[2,16,32,1,1]{2,1,0,4,3:T(8,128)}, u32[]{:S(2)}) copy-start(f32[2,16,32,1,1]{2,1,0,4,3:T(8,128)} %constant.107) | copy-start | bytes 12292
  58.0 5.7 %collective-permute-start.6 = (bf16[4,192,128]{2,1,0:T(8,128)(2,1)S(1)}, bf16[4,192,128]{2,1,0:T(8,128)(2,1)S(1)}, u32[]{:S(2)}, u32[]{:S(2)}) collective-permute-start(bf16[4,192,128]{2,1,0:T(8,128)(2,1)S(1)} %collective-permute-done.4), channel_id=1, source_target_pairs={{0,1},{1,2},{2,3},{3,4},{4,5},{5,6},{6,7},{7,0},{8,9},{9,10},{10,1... | collective-permute-start | bytes 589832 | tf_op jit(solution)/shard_map/ppermute | solution.py:121
  63.8 33.1 %collective-permute-start.7 = (bf16[32,192,128]{2,1,0:T(8,128)(2,1)S(1)}, bf16[32,192,128]{2,1,0:T(8,128)(2,1)}, u32[]{:S(2)}, u32[]{:S(2)}) collective-permute-start(bf16[32,192,128]{2,1,0:T(8,128)(2,1)S(1)} %constant_dynamic-update-slice_fusion.mine_ref), channel_id=1, source_target_pairs={{0,8},{8,0},{16,24},{24,16},{32,40},{40,32},{48,56},{56,48},{64,72... | collective-permute-start | bytes 4718600 | tf_op jit(solution)/shard_map/ppermute | solution.py:136
  70.5 23.5 %all-to-all-start.3 = ((bf16[32,128,128]{2,1,0:T(8,128)(2,1)}), bf16[32,128,128]{2,1,0:T(8,128)(2,1)S(1)}, u32[]{:S(2)}, u32[]{:S(2)}) async-start(bf16[32,128,128]{2,1,0:T(8,128)(2,1)} %bitcast.20), calls=%async_computation.3 | async-start | bytes 2097152 | tf_op jit(solution)/shard_map/all_to_all | solution.py:97
  104.7 14.2 %all-to-all-start.4 = ((f32[32,24,128]{2,1,0:T(8,128)}), f32[32,24,128]{2,1,0:T(8,128)S(1)}, u32[]{:S(2)}, u32[]{:S(2)}) async-start(f32[32,24,128]{2,1,0:T(8,128)} %reshape.108), calls=%async_computation.4 | async-start | bytes 786432 | tf_op jit(solution)/shard_map/all_to_all | solution.py:145
  133.3 7.6 %collective-permute-start.8 = (bf16[4,192,128]{2,1,0:T(8,128)(2,1)S(1)}, bf16[4,192,128]{2,1,0:T(8,128)(2,1)S(1)}, u32[]{:S(2)}, u32[]{:S(2)}) collective-permute-start(bf16[4,192,128]{2,1,0:T(8,128)(2,1)S(1)} %get-tuple-element.13), channel_id=1, source_target_pairs={{0,1},{1,2},{2,3},{3,4},{4,5},{5,6},{6,7},{7,0},{8,9},{9,10},{10,1... | collective-permute-start | bytes 589832 | tf_op jit(solution)/shard_map/ppermute | solution.py:121
  133.4 7.5 %collective-permute-start.9 = (bf16[4,192,128]{2,1,0:T(8,128)(2,1)S(1)}, bf16[4,192,128]{2,1,0:T(8,128)(2,1)S(1)}, u32[]{:S(2)}, u32[]{:S(2)}) collective-permute-start(bf16[4,192,128]{2,1,0:T(8,128)(2,1)S(1)} %get-tuple-element.13), channel_id=1, source_target_pairs={{0,7},{1,0},{2,1},{3,2},{4,3},{5,4},{6,5},{7,6},{8,15},{9,8},{10,9... | collective-permute-start | bytes 589832 | tf_op jit(solution)/shard_map/ppermute | solution.py:124
  140.9 6.7 %collective-permute-start.10 = (bf16[4,192,128]{2,1,0:T(8,128)(2,1)S(1)}, bf16[4,192,128]{2,1,0:T(8,128)(2,1)S(1)}, u32[]{:S(2)}, u32[]{:S(2)}) collective-permute-start(bf16[4,192,128]{2,1,0:T(8,128)(2,1)S(1)} %collective-permute-done.8), channel_id=1, source_target_pairs={{0,1},{1,2},{2,3},{3,4},{4,5},{5,6},{6,7},{7,0},{8,9},{9,10},{10,1... | collective-permute-start | bytes 589832 | tf_op jit(solution)/shard_map/ppermute | solution.py:121
  140.9 6.7 %collective-permute-start.11 = (bf16[4,192,128]{2,1,0:T(8,128)(2,1)S(1)}, bf16[4,192,128]{2,1,0:T(8,128)(2,1)S(1)}, u32[]{:S(2)}, u32[]{:S(2)}) collective-permute-start(bf16[4,192,128]{2,1,0:T(8,128)(2,1)S(1)} %collective-permute-done.9), channel_id=1, source_target_pairs={{0,7},{1,0},{2,1},{3,2},{4,3},{5,4},{6,5},{7,6},{8,15},{9,8},{10,9... | collective-permute-start | bytes 589832 | tf_op jit(solution)/shard_map/ppermute | solution.py:124
  147.6 5.7 %collective-permute-start.12 = (bf16[4,192,128]{2,1,0:T(8,128)(2,1)S(1)}, bf16[4,192,128]{2,1,0:T(8,128)(2,1)S(1)}, u32[]{:S(2)}, u32[]{:S(2)}) collective-permute-start(bf16[4,192,128]{2,1,0:T(8,128)(2,1)S(1)} %collective-permute-done.10), channel_id=1, source_target_pairs={{0,1},{1,2},{2,3},{3,4},{4,5},{5,6},{6,7},{7,0},{8,9},{9,10},{10,1... | collective-permute-start | bytes 589832 | tf_op jit(solution)/shard_map/ppermute | solution.py:121
  147.6 5.8 %collective-permute-start.13 = (bf16[4,192,128]{2,1,0:T(8,128)(2,1)S(1)}, bf16[4,192,128]{2,1,0:T(8,128)(2,1)S(1)}, u32[]{:S(2)}, u32[]{:S(2)}) collective-permute-start(bf16[4,192,128]{2,1,0:T(8,128)(2,1)S(1)} %collective-permute-done.11), channel_id=1, source_target_pairs={{0,7},{1,0},{2,1},{3,2},{4,3},{5,4},{6,5},{7,6},{8,15},{9,8},{10,9... | collective-permute-start | bytes 589832 | tf_op jit(solution)/shard_map/ppermute | solution.py:124
  153.3 5.7 %collective-permute-start.14 = (bf16[4,192,128]{2,1,0:T(8,128)(2,1)S(1)}, bf16[4,192,128]{2,1,0:T(8,128)(2,1)S(1)}, u32[]{:S(2)}, u32[]{:S(2)}) collective-permute-start(bf16[4,192,128]{2,1,0:T(8,128)(2,1)S(1)} %collective-permute-done.12), channel_id=1, source_target_pairs={{0,1},{1,2},{2,3},{3,4},{4,5},{5,6},{6,7},{7,0},{8,9},{9,10},{10,1... | collective-permute-start | bytes 589832 | tf_op jit(solution)/shard_map/ppermute | solution.py:121
  159.1 7.3 %collective-permute-start.15 = (bf16[32,192,128]{2,1,0:T(8,128)(2,1)S(1)}, bf16[32,192,128]{2,1,0:T(8,128)(2,1)S(1)}, u32[]{:S(2)}, u32[]{:S(2)}) collective-permute-start(bf16[32,192,128]{2,1,0:T(8,128)(2,1)S(1)} %constant_dynamic-update-slice_fusion.8.mine_ref), channel_id=1, source_target_pairs={{0,8},{8,0},{16,24},{24,16},{32,40},{40,32},{48,56},{56,48},{64,72... | collective-permute-start | bytes 4718600 | tf_op jit(solution)/shard_map/ppermute | solution.py:136
  (6 other events, 22.1 us)

commit v10 on v9

--- a/solution.py
+++ b/solution.py
@@ -93,10 +93,10 @@
     kspec = jnp.einsum(
         "xqt,thrj->qhxrj", fwd_table.reshape(2, half, length), klags, precision=HIGH
     ).astype(jnp.bfloat16)
-    kspec = kspec.reshape(ntm, -1, block)
-    kspec = lax.all_to_all(kspec, "tm", 0, 0, tiled=True)
-    kspec = kspec.reshape(ntm, 2, nnz, rows_dev, block)
-    kk = jnp.transpose(kspec, (2, 1, 0, 3, 4)).reshape(nnz, block, block)
+    kspec = kspec.reshape(ntm, 2, nnz, 1, rows_dev, block)
+    kspec = jnp.transpose(kspec, (0, 2, 1, 3, 4, 5))
+    kspec = lax.all_to_all(kspec, "tm", 0, 3, tiled=True)
+    kk = kspec.reshape(nnz, block, block)
     local_rows = pattern[:, 0] - my_state * rows_local
     row_of = jnp.clip(local_rows, 0, rows_local - 1)
     real_slot = (my_slot != 0).astype(jnp.float32)

time: 206 us -> 205 us (level)
    transpose x1 -> x0, local copies, waits for them, and re-layouts: 2.1 us -> none  [shards(): kk = jnp.transpose(kspec, (2, 1, 0, 3, 4)).reshape(nnz, block, block)]
where the time goes in v10:
time: 205 us; the launch traced here: 204 us
  waiting for transfers between devices  65.9 us (32%)
  blocking collectives  50.8 us (25%)
  starting transfers between devices  50.4 us (25%)
  local copies, waits for them, and re-layouts  17.5 us (9%)
  Pallas kernels  9.17 us (4%)
  other arithmetic  6.97 us (3%)
  matrix products  3.06 us (1%)
    ppermute x8, waiting for transfers between devices, ring_gather(): a = lax.ppermute(a, 'state', fwd)  31.8 us
    all_to_all x2, blocking collectives, respond(): xs = lax.all_to_all(xs, 'tm', 0, 0, tiled=True)  23.5 us
    ppermute x6, starting transfers between devices, ring_gather(): b = lax.ppermute(b, 'state', bwd)  17.3 us
    all_to_all x1, waiting for transfers between devices, shards(): kspec = lax.all_to_all(kspec, 'tm', 0, 3, tiled=True)  15.3 us
    all_to_all x1, blocking collectives, shards(): field = lax.all_to_all(field, 'tm', 0, 0, tiled=True)  13.7 us
    all_to_all x1, blocking collectives, respond(): ys = lax.all_to_all(ys, 'tm', 0, 0, tiled=True)  13.6 us
    pallas_call x2, Pallas kernels, block_products(): pl.pallas_call(_products_body, grid_spec=pltpu.PrefetchScalarGridSpec(num...  9.17 us
    all_to_all x1, waiting for transfers between devices, respond(): ys = lax.all_to_all(ys, 'tm', 0, 0, tiled=True)  9.1 us
  transfers between devices with their start and end apart: 20, of which 12 were waited for; matrix products, arithmetic and copies ran while one was open for 6% of the time, Pallas kernels for 0%

profile of v10, /device:TPU:1, one launch (start us, length us, event | category | flops | bytes accessed | tf_op | source)
XLA Modules:
  0.0 204.4 jit_solution(8844254520698263063)
XLA Ops:
  1.9 8.7 %all-to-all-start = ((f32[32,24,128]{2,1,0:T(8,128)}), f32[32,24,128]{2,1,0:T(8,128)S(1)}, u32[]{:S(2)}, u32[]{:S(2)}) async-start(f32[32,24,128]{2,1,0:T(8,128)} %reshape_squeeze.6), calls=%async_computation | async-start | bytes 786432 | tf_op jit(solution)/shard_map/all_to_all | solution.py:89
  14.1 6.7 %all-to-all-done = f32[32,24,128]{2,1,0:T(8,128)S(1)} async-done(((f32[32,24,128]{2,1,0:T(8,128)}), f32[32,24,128]{2,1,0:T(8,128)S(1)}, u32[]{:S(2)}, u32[]{:S(2)}) %all-to-all-start) | async-done | bytes 393248 | tf_op jit(solution)/shard_map/all_to_all | solution.py:89
  21.4 11.7 %all_to_all.50 = bf16[32,24,128]{2,1,0:T(8,128)(2,1)S(1)} all-to-all(bf16[32,24,128]{2,1,0:T(8,128)(2,1)S(1)} %bitcast.112), channel_id=1, replica_groups=mesh['tm'=32,'state'=8] {'tm'}, dimensions={0} | all-to-all | bytes 393216 | tf_op jit(solution)/shard_map/all_to_all | solution.py:132
  35.7 3.9 %collective-permute-start.1 = (bf16[4,192,128]{2,1,0:T(8,128)(2,1)}, bf16[4,192,128]{2,1,0:T(8,128)(2,1)S(1)}, u32[]{:S(2)}, u32[]{:S(2)}) collective-permute-start(bf16[4,192,128]{2,1,0:T(8,128)(2,1)} %get-tuple-element.15), channel_id=1, source_target_pairs={{0,7},{1,0},{2,1},{3,2},{4,3},{5,4},{6,5},{7,6},{8,15},{9,8},{10,9... | collective-permute-start | bytes 589832 | tf_op jit(solution)/shard_map/ppermute | solution.py:124
  39.7 4.1 %all-to-all-start.2 = ((bf16[32,128,128]{2,1,0:T(8,128)(2,1)}), bf16[32,128,128]{2,1,0:T(8,128)(2,1)S(1)}, u32[]{:S(2)}, u32[]{:S(2)}) async-start(bf16[32,128,128]{2,1,0:T(8,128)(2,1)} %bitcast.2), calls=%async_computation.2 | async-start | bytes 2097152 | tf_op jit(solution)/shard_map/all_to_all | solution.py:91
  47.7 4.2 %collective-permute-done.2 = bf16[4,192,128]{2,1,0:T(8,128)(2,1)S(1)} collective-permute-done((bf16[4,192,128]{2,1,0:T(8,128)(2,1)S(1)}, bf16[4,192,128]{2,1,0:T(8,128)(2,1)S(1)}, u32[]{:S(2)}, u32[]{:S(2)}) %collective-permute-start.2) | collective-permute-done | bytes 196640 | tf_op jit(solution)/shard_map/ppermute | solution.py:121
  54.7 3.3 %collective-permute-done.4 = bf16[4,192,128]{2,1,0:T(8,128)(2,1)S(1)} collective-permute-done((bf16[4,192,128]{2,1,0:T(8,128)(2,1)S(1)}, bf16[4,192,128]{2,1,0:T(8,128)(2,1)S(1)}, u32[]{:S(2)}, u32[]{:S(2)}) %collective-permute-start.4) | collective-permute-done | bytes 196640 | tf_op jit(solution)/shard_map/ppermute | solution.py:121
  58.1 5.7 %collective-permute-done.6 = bf16[4,192,128]{2,1,0:T(8,128)(2,1)S(1)} collective-permute-done((bf16[4,192,128]{2,1,0:T(8,128)(2,1)S(1)}, bf16[4,192,128]{2,1,0:T(8,128)(2,1)S(1)}, u32[]{:S(2)}, u32[]{:S(2)}) %collective-permute-start.6) | collective-permute-done | bytes 196640 | tf_op jit(solution)/shard_map/ppermute | solution.py:121
  63.8 3.7 %collective-permute-start.7 = (bf16[32,192,128]{2,1,0:T(8,128)(2,1)S(1)}, bf16[32,192,128]{2,1,0:T(8,128)(2,1)}, u32[]{:S(2)}, u32[]{:S(2)}) collective-permute-start(bf16[32,192,128]{2,1,0:T(8,128)(2,1)S(1)} %constant_dynamic-update-slice_fusion.mine_ref), channel_id=1, source_target_pairs={{0,8},{8,0},{16,24},{24,16},{32,40},{40,32},{48,56},{56,48},{64,72... | collective-permute-start | bytes 4718600 | tf_op jit(solution)/shard_map/ppermute | solution.py:136
  70.5 6.5 %all-to-all-start.3 = ((bf16[32,32,2,1,2,128]{5,4,1,2,3,0:T(2,128)(2,1)}), bf16[32,32,2,1,2,128]{5,4,1,2,3,0:T(2,128)(2,1)S(1)}, u32[]{:S(2)}, u32[]{:S(2)}) async-start(bf16[32,32,2,1,2,128]{5,4,1,2,3,0:T(2,128)(2,1)} %bitcast.22), calls=%async_computation.3 | async-start | bytes 2097152 | tf_op jit(solution)/shard_map/all_to_all | solution.py:98
  78.7 15.3 %all-to-all-done.3 = bf16[32,32,2,1,2,128]{5,4,1,2,3,0:T(2,128)(2,1)S(1)} async-done(((bf16[32,32,2,1,2,128]{5,4,1,2,3,0:T(2,128)(2,1)}), bf16[32,32,2,1,2,128]{5,4,1,2,3,0:T(2,128)(2,1)S(1)}, u32[]{:S(2)}, u32[]{:S(2)}) %all-to-all-start.3) | async-done | bytes 1048608 | tf_op jit(solution)/shard_map/all_to_all | solution.py:98
  96.3 4.6 %shard_map.64 = f32[8,192,128]{2,1,0:T(8,128)} custom-call(s32[32]{0:T(128)} %fusion.16.pick_ref, s32[32]{0:T(128)} %compare_convert_fusion.src_ref, s32[32]{0:T(128)} %clamp_bitcast_fusion.row_ref, bf16[32,192,128]{2,1,0:T(8,128)(2,1)} %copy-done, bf16[32,192,128]{2,1,0:T(8,128)(2,1)} %collective-permute-done.7.other_ref, bf16[32,128,128]{2,1,0:T(8,128)(2,1)} %bitcast.101), custom_call_target="tpu_custom_call" | custom-call | tf_op jit(solution)/shard_map/pallas_call | solution.py:53
  104.0 3.9 %all-to-all-start.4 = ((f32[32,24,128]{2,1,0:T(8,128)}), f32[32,24,128]{2,1,0:T(8,128)S(1)}, u32[]{:S(2)}, u32[]{:S(2)}) async-start(f32[32,24,128]{2,1,0:T(8,128)} %reshape.105), calls=%async_computation.4 | async-start | bytes 786432 | tf_op jit(solution)/shard_map/all_to_all | solution.py:145
  109.1 9.1 %all-to-all-done.4 = f32[32,24,128]{2,1,0:T(8,128)S(1)} async-done(((f32[32,24,128]{2,1,0:T(8,128)}), f32[32,24,128]{2,1,0:T(8,128)S(1)}, u32[]{:S(2)}, u32[]{:S(2)}) %all-to-all-start.4) | async-done | bytes 393248 | tf_op jit(solution)/shard_map/all_to_all | solution.py:145
  120.8 11.7 %all_to_all.51 = bf16[32,24,128]{2,1,0:T(8,128)(2,1)S(1)} all-to-all(bf16[32,24,128]{2,1,0:T(8,128)(2,1)S(1)} %bitcast.114), channel_id=1, replica_groups=mesh['tm'=32,'state'=8] {'tm'}, dimensions={0} | all-to-all | bytes 393216 | tf_op jit(solution)/shard_map/all_to_all | solution.py:132
  135.5 4.8 %collective-permute-done.8 = bf16[4,192,128]{2,1,0:T(8,128)(2,1)S(1)} collective-permute-done((bf16[4,192,128]{2,1,0:T(8,128)(2,1)S(1)}, bf16[4,192,128]{2,1,0:T(8,128)(2,1)S(1)}, u32[]{:S(2)}, u32[]{:S(2)}) %collective-permute-start.8) | collective-permute-done | bytes 196640 | tf_op jit(solution)/shard_map/ppermute | solution.py:121
  143.1 3.9 %collective-permute-done.10 = bf16[4,192,128]{2,1,0:T(8,128)(2,1)S(1)} collective-permute-done((bf16[4,192,128]{2,1,0:T(8,128)(2,1)S(1)}, bf16[4,192,128]{2,1,0:T(8,128)(2,1)S(1)}, u32[]{:S(2)}, u32[]{:S(2)}) %collective-permute-start.10) | collective-permute-done | bytes 196640 | tf_op jit(solution)/shard_map/ppermute | solution.py:121
  149.7 3.0 %collective-permute-done.12 = bf16[4,192,128]{2,1,0:T(8,128)(2,1)S(1)} collective-permute-done((bf16[4,192,128]{2,1,0:T(8,128)(2,1)S(1)}, bf16[4,192,128]{2,1,0:T(8,128)(2,1)S(1)}, u32[]{:S(2)}, u32[]{:S(2)}) %collective-permute-start.12) | collective-permute-done | bytes 196640 | tf_op jit(solution)/shard_map/ppermute | solution.py:121
  152.8 5.7 %collective-permute-done.14 = bf16[4,192,128]{2,1,0:T(8,128)(2,1)S(1)} collective-permute-done((bf16[4,192,128]{2,1,0:T(8,128)(2,1)S(1)}, bf16[4,192,128]{2,1,0:T(8,128)(2,1)S(1)}, u32[]{:S(2)}, u32[]{:S(2)}) %collective-permute-start.14) | collective-permute-done | bytes 196640 | tf_op jit(solution)/shard_map/ppermute | solution.py:121
  158.5 4.5 %collective-permute-start.15 = (bf16[32,192,128]{2,1,0:T(8,128)(2,1)S(1)}, bf16[32,192,128]{2,1,0:T(8,128)(2,1)S(1)}, u32[]{:S(2)}, u32[]{:S(2)}) collective-permute-start(bf16[32,192,128]{2,1,0:T(8,128)(2,1)S(1)} %constant_dynamic-update-slice_fusion.8.mine_ref), channel_id=1, source_target_pairs={{0,8},{8,0},{16,24},{24,16},{32,40},{40,32},{48,56},{56,48},{64,72... | collective-permute-start | bytes 4718600 | tf_op jit(solution)/shard_map/ppermute | solution.py:136
  163.0 3.0 %collective-permute-done.15.other_ref = bf16[32,192,128]{2,1,0:T(8,128)(2,1)S(1)} collective-permute-done((bf16[32,192,128]{2,1,0:T(8,128)(2,1)S(1)}, bf16[32,192,128]{2,1,0:T(8,128)(2,1)S(1)}, u32[]{:S(2)}, u32[]{:S(2)}) %collective-permute-start.15) | collective-permute-done | bytes 1572896 | tf_op jit(solution)/shard_map/ppermute | solution.py:136
  167.1 4.6 %shard_map.65 = f32[8,192,128]{2,1,0:T(8,128)} custom-call(s32[32]{0:T(128)} %fusion.16.pick_ref, s32[32]{0:T(128)} %compare_convert_fusion.src_ref, s32[32]{0:T(128)} %clamp_bitcast_fusion.row_ref, bf16[32,192,128]{2,1,0:T(8,128)(2,1)} %copy-done.1, bf16[32,192,128]{2,1,0:T(8,128)(2,1)} %copy-done.2, bf16[32,128,128]{2,1,0:T(8,128)(2,1)} %bitcast.102), custom_call_target="tpu_custom_call" | custom-call | tf_op jit(solution)/shard_map/pallas_call | solution.py:53
  174.2 13.6 %all_to_all.52 = f32[32,24,128]{2,1,0:T(8,128)S(1)} all-to-all(f32[32,24,128]{2,1,0:T(8,128)S(1)} %reshape.112), channel_id=1, replica_groups=mesh['tm'=32,'state'=8] {'tm'}, dimensions={0} | all-to-all | bytes 786432 | tf_op jit(solution)/shard_map/all_to_all | solution.py:145
  189.9 13.7 %all_to_all.53 = f32[32,24,128]{2,1,0:T(8,128)S(1)} all-to-all(f32[32,24,128]{2,1,0:T(8,128)S(1)} %copy.60), channel_id=1, replica_groups=mesh['tm'=32,'state'=8] {'tm'}, dimensions={0} | all-to-all | bytes 786432 | tf_op jit(solution)/shard_map/all_to_all | solution.py:156
  (100 shorter events, 43.9 us)
Async XLA Ops:
  0.0 10.6 %copy-start.3 = (bf16[32,1,128,128]{3,2,1,0:T(8,128)(2,1)S(1)}, bf16[32,1,128,128]{3,2,1,0:T(8,128)(2,1)}, u32[]{:S(2)}) copy-start(bf16[32,1,128,128]{3,2,1,0:T(8,128)(2,1)} %param.7) | copy-start | bytes 3145732
  1.9 10.9 %copy-start.7 = (s32[2]{0:T(128)S(1)}, s32[2]{0:T(128)}, u32[]{:S(2)}) copy-start(s32[2]{0:T(128)} %param.9) | copy-start | bytes 28
  1.9 18.9 %copy-start.5 = (f32[32,32,1]{1,0,2:T(8,128)S(1)}, f32[32,32,1]{1,0,2:T(8,128)}, u32[]{:S(2)}) copy-start(f32[32,32,1]{1,0,2:T(8,128)} %constant.106) | copy-start | bytes 12292
  1.9 18.9 %all-to-all-start = ((f32[32,24,128]{2,1,0:T(8,128)}), f32[32,24,128]{2,1,0:T(8,128)S(1)}, u32[]{:S(2)}, u32[]{:S(2)}) async-start(f32[32,24,128]{2,1,0:T(8,128)} %reshape_squeeze.6), calls=%async_computation | async-start | bytes 786432 | tf_op jit(solution)/shard_map/all_to_all | solution.py:89
  34.1 10.9 %collective-permute-start = (bf16[4,192,128]{2,1,0:T(8,128)(2,1)}, bf16[4,192,128]{2,1,0:T(8,128)(2,1)S(1)}, u32[]{:S(2)}, u32[]{:S(2)}) collective-permute-start(bf16[4,192,128]{2,1,0:T(8,128)(2,1)} %get-tuple-element.15), channel_id=1, source_target_pairs={{0,1},{1,2},{2,3},{3,4},{4,5},{5,6},{6,7},{7,0},{8,9},{9,10},{10,1... | collective-permute-start | bytes 589832 | tf_op jit(solution)/shard_map/ppermute | solution.py:121
  35.7 9.3 %collective-permute-start.1 = (bf16[4,192,128]{2,1,0:T(8,128)(2,1)}, bf16[4,192,128]{2,1,0:T(8,128)(2,1)S(1)}, u32[]{:S(2)}, u32[]{:S(2)}) collective-permute-start(bf16[4,192,128]{2,1,0:T(8,128)(2,1)} %get-tuple-element.15), channel_id=1, source_target_pairs={{0,7},{1,0},{2,1},{3,2},{4,3},{5,4},{6,5},{7,6},{8,15},{9,8},{10,9... | collective-permute-start | bytes 589832 | tf_op jit(solution)/shard_map/ppermute | solution.py:124
  39.7 27.8 %all-to-all-start.2 = ((bf16[32,128,128]{2,1,0:T(8,128)(2,1)}), bf16[32,128,128]{2,1,0:T(8,128)(2,1)S(1)}, u32[]{:S(2)}, u32[]{:S(2)}) async-start(bf16[32,128,128]{2,1,0:T(8,128)(2,1)} %bitcast.2), calls=%async_computation.2 | async-start | bytes 2097152 | tf_op jit(solution)/shard_map/all_to_all | solution.py:91
  45.0 6.9 %collective-permute-start.2 = (bf16[4,192,128]{2,1,0:T(8,128)(2,1)S(1)}, bf16[4,192,128]{2,1,0:T(8,128)(2,1)S(1)}, u32[]{:S(2)}, u32[]{:S(2)}) collective-permute-start(bf16[4,192,128]{2,1,0:T(8,128)(2,1)S(1)} %collective-permute-done), channel_id=1, source_target_pairs={{0,1},{1,2},{2,3},{3,4},{4,5},{5,6},{6,7},{7,0},{8,9},{9,10},{10,1... | collective-permute-start | bytes 589832 | tf_op jit(solution)/shard_map/ppermute | solution.py:121
  45.0 6.9 %collective-permute-start.3 = (bf16[4,192,128]{2,1,0:T(8,128)(2,1)S(1)}, bf16[4,192,128]{2,1,0:T(8,128)(2,1)S(1)}, u32[]{:S(2)}, u32[]{:S(2)}) collective-permute-start(bf16[4,192,128]{2,1,0:T(8,128)(2,1)S(1)} %collective-permute-done.1), channel_id=1, source_target_pairs={{0,7},{1,0},{2,1},{3,2},{4,3},{5,4},{6,5},{7,6},{8,15},{9,8},{10,9... | collective-permute-start | bytes 589832 | tf_op jit(solution)/shard_map/ppermute | solution.py:124
  51.9 6.1 %collective-permute-start.4 = (bf16[4,192,128]{2,1,0:T(8,128)(2,1)S(1)}, bf16[4,192,128]{2,1,0:T(8,128)(2,1)S(1)}, u32[]{:S(2)}, u32[]{:S(2)}) collective-permute-start(bf16[4,192,128]{2,1,0:T(8,128)(2,1)S(1)} %collective-permute-done.2), channel_id=1, source_target_pairs={{0,1},{1,2},{2,3},{3,4},{4,5},{5,6},{6,7},{7,0},{8,9},{9,10},{10,1... | collective-permute-start | bytes 589832 | tf_op jit(solution)/shard_map/ppermute | solution.py:121
  51.9 6.1 %collective-permute-start.5 = (bf16[4,192,128]{2,1,0:T(8,128)(2,1)S(1)}, bf16[4,192,128]{2,1,0:T(8,128)(2,1)S(1)}, u32[]{:S(2)}, u32[]{:S(2)}) collective-permute-start(bf16[4,192,128]{2,1,0:T(8,128)(2,1)S(1)} %collective-permute-done.3), channel_id=1, source_target_pairs={{0,7},{1,0},{2,1},{3,2},{4,3},{5,4},{6,5},{7,6},{8,15},{9,8},{10,9... | collective-permute-start | bytes 589832 | tf_op jit(solution)/shard_map/ppermute | solution.py:124
  54.6 13.5 %copy-start.6 = (f32[2,16,32,1,1]{2,1,0,4,3:T(8,128)S(1)}, f32[2,16,32,1,1]{2,1,0,4,3:T(8,128)}, u32[]{:S(2)}) copy-start(f32[2,16,32,1,1]{2,1,0,4,3:T(8,128)} %constant.107) | copy-start | bytes 12292
  58.0 5.7 %collective-permute-start.6 = (bf16[4,192,128]{2,1,0:T(8,128)(2,1)S(1)}, bf16[4,192,128]{2,1,0:T(8,128)(2,1)S(1)}, u32[]{:S(2)}, u32[]{:S(2)}) collective-permute-start(bf16[4,192,128]{2,1,0:T(8,128)(2,1)S(1)} %collective-permute-done.4), channel_id=1, source_target_pairs={{0,1},{1,2},{2,3},{3,4},{4,5},{5,6},{6,7},{7,0},{8,9},{9,10},{10,1... | collective-permute-start | bytes 589832 | tf_op jit(solution)/shard_map/ppermute | solution.py:121
  63.8 32.5 %collective-permute-start.7 = (bf16[32,192,128]{2,1,0:T(8,128)(2,1)S(1)}, bf16[32,192,128]{2,1,0:T(8,128)(2,1)}, u32[]{:S(2)}, u32[]{:S(2)}) collective-permute-start(bf16[32,192,128]{2,1,0:T(8,128)(2,1)S(1)} %constant_dynamic-update-slice_fusion.mine_ref), channel_id=1, source_target_pairs={{0,8},{8,0},{16,24},{24,16},{32,40},{40,32},{48,56},{56,48},{64,72... | collective-permute-start | bytes 4718600 | tf_op jit(solution)/shard_map/ppermute | solution.py:136
  70.5 23.5 %all-to-all-start.3 = ((bf16[32,32,2,1,2,128]{5,4,1,2,3,0:T(2,128)(2,1)}), bf16[32,32,2,1,2,128]{5,4,1,2,3,0:T(2,128)(2,1)S(1)}, u32[]{:S(2)}, u32[]{:S(2)}) async-start(bf16[32,32,2,1,2,128]{5,4,1,2,3,0:T(2,128)(2,1)} %bitcast.22), calls=%async_computation.3 | async-start | bytes 2097152 | tf_op jit(solution)/shard_map/all_to_all | solution.py:98
  104.0 14.2 %all-to-all-start.4 = ((f32[32,24,128]{2,1,0:T(8,128)}), f32[32,24,128]{2,1,0:T(8,128)S(1)}, u32[]{:S(2)}, u32[]{:S(2)}) async-start(f32[32,24,128]{2,1,0:T(8,128)} %reshape.105), calls=%async_computation.4 | async-start | bytes 786432 | tf_op jit(solution)/shard_map/all_to_all | solution.py:145
  132.7 7.6 %collective-permute-start.8 = (bf16[4,192,128]{2,1,0:T(8,128)(2,1)S(1)}, bf16[4,192,128]{2,1,0:T(8,128)(2,1)S(1)}, u32[]{:S(2)}, u32[]{:S(2)}) collective-permute-start(bf16[4,192,128]{2,1,0:T(8,128)(2,1)S(1)} %get-tuple-element.13), channel_id=1, source_target_pairs={{0,1},{1,2},{2,3},{3,4},{4,5},{5,6},{6,7},{7,0},{8,9},{9,10},{10,1... | collective-permute-start | bytes 589832 | tf_op jit(solution)/shard_map/ppermute | solution.py:121
  132.8 7.5 %collective-permute-start.9 = (bf16[4,192,128]{2,1,0:T(8,128)(2,1)S(1)}, bf16[4,192,128]{2,1,0:T(8,128)(2,1)S(1)}, u32[]{:S(2)}, u32[]{:S(2)}) collective-permute-start(bf16[4,192,128]{2,1,0:T(8,128)(2,1)S(1)} %get-tuple-element.13), channel_id=1, source_target_pairs={{0,7},{1,0},{2,1},{3,2},{4,3},{5,4},{6,5},{7,6},{8,15},{9,8},{10,9... | collective-permute-start | bytes 589832 | tf_op jit(solution)/shard_map/ppermute | solution.py:124
  140.3 6.7 %collective-permute-start.10 = (bf16[4,192,128]{2,1,0:T(8,128)(2,1)S(1)}, bf16[4,192,128]{2,1,0:T(8,128)(2,1)S(1)}, u32[]{:S(2)}, u32[]{:S(2)}) collective-permute-start(bf16[4,192,128]{2,1,0:T(8,128)(2,1)S(1)} %collective-permute-done.8), channel_id=1, source_target_pairs={{0,1},{1,2},{2,3},{3,4},{4,5},{5,6},{6,7},{7,0},{8,9},{9,10},{10,1... | collective-permute-start | bytes 589832 | tf_op jit(solution)/shard_map/ppermute | solution.py:121
  140.3 6.7 %collective-permute-start.11 = (bf16[4,192,128]{2,1,0:T(8,128)(2,1)S(1)}, bf16[4,192,128]{2,1,0:T(8,128)(2,1)S(1)}, u32[]{:S(2)}, u32[]{:S(2)}) collective-permute-start(bf16[4,192,128]{2,1,0:T(8,128)(2,1)S(1)} %collective-permute-done.9), channel_id=1, source_target_pairs={{0,7},{1,0},{2,1},{3,2},{4,3},{5,4},{6,5},{7,6},{8,15},{9,8},{10,9... | collective-permute-start | bytes 589832 | tf_op jit(solution)/shard_map/ppermute | solution.py:124
  147.0 5.7 %collective-permute-start.12 = (bf16[4,192,128]{2,1,0:T(8,128)(2,1)S(1)}, bf16[4,192,128]{2,1,0:T(8,128)(2,1)S(1)}, u32[]{:S(2)}, u32[]{:S(2)}) collective-permute-start(bf16[4,192,128]{2,1,0:T(8,128)(2,1)S(1)} %collective-permute-done.10), channel_id=1, source_target_pairs={{0,1},{1,2},{2,3},{3,4},{4,5},{5,6},{6,7},{7,0},{8,9},{9,10},{10,1... | collective-permute-start | bytes 589832 | tf_op jit(solution)/shard_map/ppermute | solution.py:121
  147.0 5.8 %collective-permute-start.13 = (bf16[4,192,128]{2,1,0:T(8,128)(2,1)S(1)}, bf16[4,192,128]{2,1,0:T(8,128)(2,1)S(1)}, u32[]{:S(2)}, u32[]{:S(2)}) collective-permute-start(bf16[4,192,128]{2,1,0:T(8,128)(2,1)S(1)} %collective-permute-done.11), channel_id=1, source_target_pairs={{0,7},{1,0},{2,1},{3,2},{4,3},{5,4},{6,5},{7,6},{8,15},{9,8},{10,9... | collective-permute-start | bytes 589832 | tf_op jit(solution)/shard_map/ppermute | solution.py:124
  152.7 5.7 %collective-permute-start.14 = (bf16[4,192,128]{2,1,0:T(8,128)(2,1)S(1)}, bf16[4,192,128]{2,1,0:T(8,128)(2,1)S(1)}, u32[]{:S(2)}, u32[]{:S(2)}) collective-permute-start(bf16[4,192,128]{2,1,0:T(8,128)(2,1)S(1)} %collective-permute-done.12), channel_id=1, source_target_pairs={{0,1},{1,2},{2,3},{3,4},{4,5},{5,6},{6,7},{7,0},{8,9},{9,10},{10,1... | collective-permute-start | bytes 589832 | tf_op jit(solution)/shard_map/ppermute | solution.py:121
  158.5 7.5 %collective-permute-start.15 = (bf16[32,192,128]{2,1,0:T(8,128)(2,1)S(1)}, bf16[32,192,128]{2,1,0:T(8,128)(2,1)S(1)}, u32[]{:S(2)}, u32[]{:S(2)}) collective-permute-start(bf16[32,192,128]{2,1,0:T(8,128)(2,1)S(1)} %constant_dynamic-update-slice_fusion.8.mine_ref), channel_id=1, source_target_pairs={{0,8},{8,0},{16,24},{24,16},{32,40},{40,32},{48,56},{56,48},{64,72... | collective-permute-start | bytes 4718600 | tf_op jit(solution)/shard_map/ppermute | solution.py:136
  (6 other events, 22.3 us)
